TPU v7x, 32 devices: a whole 2x2x4 slice. The times are simulated.
32 devices in a mesh: shot: 4 (over y, core), tile: 8 (over z, x).
Axes of the slice: x: 2, y: 2, z: 4, core: 2. Of those that a mesh axis runs over, the one named last changes fastest.
Arguments:
- coefs: float32 [3, 16, 1024, 128], P(None, 'shot', 'tile')
- fwd_state: float32 [4, 4, 16, 1024, 128], P('shot', None, None, 'tile'), may hold values from -3 to 3
- adj_state: float32 [4, 4, 16, 1024, 128], P('shot', None, None, 'tile'), may hold values from -3 to 3
- src_cell: int32 [4, 8], P('shot', 'tile'), may hold values from 0 to 262143
- src_wave: float32 [4, 6], P('shot'), may hold values from -8 to 8
- rec_cells: int32 [4, 1024], P('shot', 'tile'), may hold values from 0 to 262143
- observed: float32 [4, 6, 1024], P('shot', None, 'tile'), may hold values from -6 to 6
Outputs:
- gradient: float32 [3, 16, 1024, 128], P(None, 'shot', 'tile')
- fwd_final: float32 [4, 2, 16, 1024, 128], P('shot', None, None, 'tile')
- adj_final: float32 [4, 2, 16, 1024, 128], P('shot', None, None, 'tile')
Inputs may be any that keep to these rules, and one draw needn't show every extreme that they name: `src_cell`: local cell index depth * 128 * 128 + first * 128 + second inside the aperture tile. `rec_cells`: local cell index inside the tile of the receiver's block; cells may repeat.
All inputs are finite; a program needn't handle non-finite values.
Results may differ from a plain program's by a relative error of at most 0.0003.
Values sent between devices are 32-bit elements; how exact they have to be, the bound alone decides.
No kernel may reach another device: no remote copies, remote signals or barrier semaphores. Data moves between devices by JAX's collectives and lax.ppermute only.
A program may use at most 192 MiB of HBM per device.

v0:
```python
import jax
import jax.numpy as jnp
from jax import lax
from jax.experimental import pallas as pl
from jax.experimental.pallas import tpu as pltpu
from jax.sharding import PartitionSpec as P

HALO = 12
OFF = 16
PADX = 8
INTERPRET = False


def d2(m2, m1, c0, p1, p2):
    return ((((-m2) + 16.0 * m1) - 30.0 * c0) + 16.0 * p1 - p2) * (1.0 / 12.0)


def forward_kernel(wave_ref, st_ref, cf_ref, mask_ref, h_ref, z_ref, pl_ref, q_ref, pb, qb):
    steps = h_ref.shape[0]
    az, xd, ay = st_ref.shape[1:]
    ax = h_ref.shape[2]
    pb[...] = jnp.zeros(pb.shape, jnp.float32)
    qb[...] = jnp.zeros(qb.shape, jnp.float32)
    inner = pl.ds(PADX, xd)
    pb[0, 2:2 + az, inner, :] = st_ref[0]
    qb[0, 2:2 + az, inner, :] = st_ref[1]
    pb[1, 2:2 + az, inner, :] = st_ref[2]
    qb[1, 2:2 + az, inner, :] = st_ref[3]
    lane = lax.broadcasted_iota(jnp.int32, (xd, ay), 1)
    for n in range(steps):
        cur = n % 2
        old = 1 - cur
        wv = wave_ref[n]

        def plane(d, carry):
            pc = pb[cur, d + 2, inner, :]
            d2x = d2(pb[cur, d + 2, pl.ds(PADX - 2, xd), :], pb[cur, d + 2, pl.ds(PADX - 1, xd), :], pc,
                     pb[cur, d + 2, pl.ds(PADX + 1, xd), :], pb[cur, d + 2, pl.ds(PADX + 2, xd), :])
            ym2 = jnp.where(lane >= 2, pltpu.roll(pc, 2, 1), 0.0)
            ym1 = jnp.where(lane >= 1, pltpu.roll(pc, 1, 1), 0.0)
            yp1 = jnp.where(lane < ay - 1, pltpu.roll(pc, ay - 1, 1), 0.0)
            yp2 = jnp.where(lane < ay - 2, pltpu.roll(pc, ay - 2, 1), 0.0)
            h = d2x + d2(ym2, ym1, pc, yp1, yp2)
            qc = qb[cur, d + 2, inner, :]
            z = d2(qb[cur, d, inner, :], qb[cur, d + 1, inner, :], qc, qb[cur, d + 3, inner, :], qb[cur, d + 4, inner, :])
            c = cf_ref[0, d]
            a = cf_ref[1, d]
            b = cf_ref[2, d]
            pulse = wv * mask_ref[d]
            pn = 2.0 * pc - pb[old, d + 2, inner, :] + c * (a * h + b * z) + pulse
            qn = 2.0 * qc - qb[old, d + 2, inner, :] + c * (b * h + z) + pulse
            pb[old, d + 2, inner, :] = pn
            qb[old, d + 2, inner, :] = qn
            h_ref[n, d] = h[OFF:OFF + ax]
            z_ref[n, d] = z[OFF:OFF + ax]
            pl_ref[n, d] = pn[OFF:OFF + ax]
            if n == steps - 1:
                q_ref[d] = qn[OFF:OFF + ax]
            return carry

        lax.fori_loop(0, az, plane, 0)


def adjoint_kernel(adj_ref, cf_ref, h_ref, z_ref, e_ref, acc_ref, fin_ref, lb, mb, ob, fb):
    steps = h_ref.shape[0]
    az, xd, ay = adj_ref.shape[1:]
    ax = h_ref.shape[2]
    lb[0] = adj_ref[0]
    mb[0] = adj_ref[1]
    lb[1] = adj_ref[2]
    mb[1] = adj_ref[3]
    ob[...] = jnp.zeros(ob.shape, jnp.float32)
    fb[...] = jnp.zeros(fb.shape, jnp.float32)
    acc_ref[...] = jnp.zeros(acc_ref.shape, jnp.float32)
    lane = lax.broadcasted_iota(jnp.int32, (xd, ay), 1)
    inner = pl.ds(PADX, xd)
    for s in reversed(range(steps)):
        cur = (steps - 1 - s) % 2
        old = 1 - cur

        def other_plane(d, carry):
            ob[d + 2] = cf_ref[0, d] * (cf_ref[2, d] * lb[cur, d] + mb[cur, d])
            return carry

        lax.fori_loop(0, az, other_plane, 0)

        def plane(d, carry):
            lc = lb[cur, d]
            mc = mb[cur, d]
            c = cf_ref[0, d]
            a = cf_ref[1, d]
            b = cf_ref[2, d]
            f = c * (a * lc + b * mc)
            fb[inner, :] = f
            d2x = d2(fb[pl.ds(PADX - 2, xd), :], fb[pl.ds(PADX - 1, xd), :], f, fb[pl.ds(PADX + 1, xd), :], fb[pl.ds(PADX + 2, xd), :])
            ym2 = jnp.where(lane >= 2, pltpu.roll(f, 2, 1), 0.0)
            ym1 = jnp.where(lane >= 1, pltpu.roll(f, 1, 1), 0.0)
            yp1 = jnp.where(lane < ay - 1, pltpu.roll(f, ay - 1, 1), 0.0)
            yp2 = jnp.where(lane < ay - 2, pltpu.roll(f, ay - 2, 1), 0.0)
            hf = d2x + d2(ym2, ym1, f, yp1, yp2)
            ln = e_ref[s, d] + 2.0 * lc + hf - lb[old, d]
            mn = 2.0 * mc + d2(ob[d], ob[d + 1], ob[d + 2], ob[d + 3], ob[d + 4]) - mb[old, d]
            lb[old, d] = ln
            mb[old, d] = mn
            lo = ln[OFF:OFF + ax]
            mo = mn[OFF:OFF + ax]
            h = h_ref[s, d]
            z = z_ref[s, d]
            acc_ref[0, d] = acc_ref[0, d] + lo * h
            acc_ref[1, d] = acc_ref[1, d] + lo * z + mo * h
            acc_ref[2, d] = acc_ref[2, d] + mo * z
            if s == 0:
                fin_ref[0, d] = lo
                fin_ref[1, d] = mo
            return carry

        lax.fori_loop(0, az, plane, 0)


def run_adjoint(adj, cf, h_all, z_all, e_all):
    _, az, xd, ay = adj.shape
    ax = h_all.shape[2]
    vm = pl.BlockSpec(memory_space=pltpu.VMEM)
    return pl.pallas_call(
        adjoint_kernel,
        out_shape=(jax.ShapeDtypeStruct((3, az, ax, ay), jnp.float32), jax.ShapeDtypeStruct((2, az, ax, ay), jnp.float32)),
        in_specs=[vm] * 5,
        out_specs=(vm, vm),
        scratch_shapes=[
            pltpu.VMEM((2, az, xd, ay), jnp.float32),
            pltpu.VMEM((2, az, xd, ay), jnp.float32),
            pltpu.VMEM((az + 4, xd, ay), jnp.float32),
            pltpu.VMEM((xd + 2 * PADX, ay), jnp.float32),
        ],
        compiler_params=pltpu.CompilerParams(vmem_limit_bytes=62 * 1024 * 1024),
        interpret=INTERPRET,
    )(adj, cf, h_all, z_all, e_all)


def exact_parts(x):
    hi = x.astype(jnp.bfloat16)
    rest = x - hi.astype(jnp.float32)
    mid = rest.astype(jnp.bfloat16)
    lo = (rest - mid.astype(jnp.float32)).astype(jnp.bfloat16)
    return hi, mid, lo


def run_forward(wave, st, cf, mask, ax):
    steps = wave.shape[0]
    _, az, xd, ay = st.shape
    vm = pl.BlockSpec(memory_space=pltpu.VMEM)
    loc = jax.ShapeDtypeStruct((steps, az, ax, ay), jnp.float32)
    return pl.pallas_call(
        forward_kernel,
        out_shape=(loc, loc, loc, jax.ShapeDtypeStruct((az, ax, ay), jnp.float32)),
        in_specs=[pl.BlockSpec(memory_space=pltpu.SMEM), vm, vm, vm],
        out_specs=(vm, vm, vm, vm),
        scratch_shapes=[pltpu.VMEM((2, az + 4, xd + 2 * PADX, ay), jnp.float32)] * 2,
        compiler_params=pltpu.CompilerParams(vmem_limit_bytes=60 * 1024 * 1024),
        interpret=INTERPRET,
    )(wave, st, cf, mask)


def taps(padded, size, axis):

    def part(k):
        return lax.slice_in_dim(padded, k, k + size, axis=axis)

    return (-part(0) + 16.0 * part(1) - 30.0 * part(2) + 16.0 * part(3) - part(4)) / 12.0


def along_local(field, axis):
    pads = [(0, 0)] * field.ndim
    pads[axis] = (2, 2)
    return taps(jnp.pad(field, pads), field.shape[axis], axis)


def horiz(field):
    return along_local(field, field.ndim - 2) + along_local(field, field.ndim - 1)


def to_left_right(head, tail, axis):
    count = lax.axis_size(axis)
    from_left = lax.ppermute(tail, axis, [(i, i + 1) for i in range(count - 1)])
    from_right = lax.ppermute(head, axis, [(i + 1, i) for i in range(count - 1)])
    return from_left, from_right


def rows(x):
    return x.reshape(-1, x.shape[-1])


def per_device(coefs, fwd_state, adj_state, src_cell, src_wave, rec_cells, observed):
    w = HALO
    _, zl, ax, ay = coefs.shape
    n_tile = lax.axis_size("tile")
    tile = lax.axis_index("tile")
    steps = src_wave.shape[1]
    full = lax.all_gather(coefs, "shot", axis=1, tiled=True)
    az = full.shape[1]
    xe = ax + 2 * OFF
    ext_shape = (az, xe, ay)
    cells_ext = az * xe * ay

    def widen(lo, mid, hi):
        pad = jnp.zeros(mid.shape[:-2] + (OFF - w, ay), jnp.float32)
        lo, hi = lax.optimization_barrier((jnp.concatenate([pad, lo], axis=-2), jnp.concatenate([hi, pad], axis=-2)))
        return jnp.concatenate([lo, mid, hi], axis=-2)

    fs = fwd_state[0]
    src_row = jnp.broadcast_to(src_cell[0, 0].astype(jnp.float32), (1, ay))
    head1 = jnp.concatenate([rows(fs[:, :, :w]), rows(coefs[:, :, :w]), src_row], axis=0)
    tail1 = jnp.concatenate([rows(fs[:, :, ax - w:]), rows(coefs[:, :, ax - w:]), src_row], axis=0)
    left1, right1 = to_left_right(head1, tail1, "tile")
    n_fs = 4 * az * w
    n_cf = 3 * zl * w

    def unpack1(m):
        st = m[:n_fs].reshape(4, az, w, ay)
        cf = m[n_fs:n_fs + n_cf].reshape(3, zl, w, ay)
        sc = m[n_fs + n_cf, 0]
        return st, cf, sc

    st_l, cf_l, sc_l = unpack1(left1)
    st_r, cf_r, sc_r = unpack1(right1)
    cf_halo = lax.all_gather(jnp.concatenate([cf_l, cf_r], axis=2), "shot", axis=1, tiled=True)
    full_ext = widen(cf_halo[:, :, :w], full, cf_halo[:, :, w:])
    speed, stretch, couple = full_ext[0], full_ext[1], full_ext[2]
    state = widen(st_l, fs, st_r)

    def ext_index(cell, shift):
        depth = cell // (ax * ay)
        first = (cell // ay) % ax + shift + OFF
        second = cell % ay
        ok = (first >= OFF - w) & (first < xe - OFF + w)
        return jnp.where(ok, (depth * xe + first) * ay + second, cells_ext), ok

    src_own, _ = ext_index(src_cell[0, 0], 0)
    src_lft, ok_l = ext_index(sc_l.astype(jnp.int32), -ax)
    src_rgt, ok_r = ext_index(sc_r.astype(jnp.int32), ax)
    ok_l = ok_l & (tile > 0)
    ok_r = ok_r & (tile < n_tile - 1)
    src_idx = jnp.stack([src_own, src_lft, src_rgt])
    src_on = jnp.stack([jnp.float32(1.0), ok_l.astype(jnp.float32), ok_r.astype(jnp.float32)])
    source_mask = jnp.zeros((cells_ext,), jnp.float32).at[src_idx].add(src_on, mode="drop").reshape(ext_shape)

    ad = adj_state[0]
    ad_head, ad_tail, state = lax.optimization_barrier((rows(ad[:, :, :w]), rows(ad[:, :, ax - w:]), state))
    left2, right2 = to_left_right(ad_head, ad_tail, "tile")
    adj_ext = widen(left2.reshape(4, az, w, ay), ad, right2.reshape(4, az, w, ay))

    h_all, z_all, p_all, q_last = run_forward(src_wave[0], state, full_ext, source_mask, ax)
    receivers = rec_cells[0]
    records = jnp.stack([p_all[n].reshape(-1)[receivers] for n in range(steps)]) - observed[0]

    msg = jnp.concatenate([records, receivers.astype(jnp.float32)[None]], axis=0)
    left3, right3 = to_left_right(msg, msg, "tile")
    rec_own, _ = ext_index(receivers, 0)
    rec_l, okr_l = ext_index(left3[steps].astype(jnp.int32), -ax)
    rec_r, okr_r = ext_index(right3[steps].astype(jnp.int32), ax)
    okr_l = okr_l & (tile > 0)
    okr_r = okr_r & (tile < n_tile - 1)
    rec_l = jnp.where(okr_l, rec_l, cells_ext)
    rec_r = jnp.where(okr_r, rec_r, cells_ext)
    rec_all = jnp.concatenate([rec_own, rec_l, rec_r])

    n_rows = az * xe
    pick_row = (lax.broadcasted_iota(jnp.int32, (n_rows, rec_all.shape[0]), 0) == (rec_all // ay)[None, :]).astype(jnp.bfloat16)
    pick_lane = lax.broadcasted_iota(jnp.int32, (rec_all.shape[0], ay), 1) == (rec_all % ay)[:, None]
    dense = []
    for step in range(steps):
        vals = jnp.concatenate([records[step], left3[step], right3[step]])
        spread = jnp.where(pick_lane, vals[:, None], 0.0)
        total = None
        for part in exact_parts(spread):
            term = jnp.dot(pick_row, part, preferred_element_type=jnp.float32)
            total = term if total is None else total + term
        dense.append(total.reshape(ext_shape))
    acc, fin = run_adjoint(adj_ext, full_ext, h_all, z_all, jnp.stack(dense))
    acc_h, acc_x, acc_z = acc[0], acc[1], acc[2]

    n_shot = lax.axis_size("shot")
    acc = jnp.stack([acc_h, acc_x, acc_z])
    acc = acc.reshape(3, n_shot, az // n_shot, ax, ay).transpose(1, 0, 2, 3, 4)
    summed = lax.psum_scatter(acc, "shot", scatter_dimension=0, tiled=True)[0]
    q_h, q_x, q_z = summed[0], summed[1], summed[2]
    c, a, b = coefs[0], coefs[1], coefs[2]
    gradient = jnp.stack([a * q_h + b * q_x + q_z, c * q_h, c * q_x])
    fwd_final = jnp.stack([p_all[steps - 1], q_last])[None]
    adj_final = fin[None]
    return (gradient, fwd_final, adj_final)


def solution(mesh):
    placed = (
        P(None, "shot", "tile", None),
        P("shot", None, None, "tile", None),
        P("shot", None, None, "tile", None),
        P("shot", "tile"),
        P("shot", None),
        P("shot", "tile"),
        P("shot", None, "tile"),
    )
    return jax.shard_map(
        per_device,
        mesh=mesh,
        in_specs=placed,
        out_specs=(
            P(None, "shot", "tile", None),
            P("shot", None, None, "tile", None),
            P("shot", None, None, "tile", None),
        ),
        check_vma=False,
    )
```

profile of v0, /device:TPU:0, one launch (start us, length us, event | category | flops | bytes accessed | tf_op | source)
XLA Modules:
  0.0 240.9 jit_solution(13571401213552649922)
XLA Ops:
  8.0 1.0 fusion.158
  8.9 1.3 fusion.156
  11.3 4.9 %collective-permute-start = (f32[913,128]{1,0:T(8,128)S(1)}, f32[913,128]{1,0:T(8,128)S(1)}, u32[]{:S(2)}, u32[]{:S(2)}) collective-permute-start(f32[913,128]{1,0:T(8,128)S(1)} %get-tuple-element.69), channel_id=1, source_target_pairs={{0,1},{1,2},{2,3},{3,4},{4,5},{5,6},{6,7},{8,9},{9,10},{10,11},{11... | collective-permute-start | bytes 1402376 | tf_op jit(solution)/shard_map/ppermute | solution.py:184
  16.2 1.3 collective-permute-start.1
  17.5 1.4 fusion.157
  20.6 15.7 %collective-permute-done = f32[913,128]{1,0:T(8,128)S(1)} collective-permute-done((f32[913,128]{1,0:T(8,128)S(1)}, f32[913,128]{1,0:T(8,128)S(1)}, u32[]{:S(2)}, u32[]{:S(2)}) %collective-permute-start) | collective-permute-done | bytes 467488 | tf_op jit(solution)/shard_map/ppermute | solution.py:184
  36.6 5.4 %pad_maximum_fusion.st_ref = f32[4,16,160,128]{3,2,1,0:T(8,128)} fusion(f32[4,16,16,128]{3,2,1,0:T(8,128)S(1)} %concatenate.113, f32[4,16,128,128]{3,2,1,0:T(8,128)} %bitcast.160, f32[4,16,16,128]{3,2,1,0:T(8,128)S(1)} %concatenate.111), kind=kLoop, calls=%fused_computation.7 | loop fusion | flops 2621440 | bytes 10485760 | tf_op jit(solution)/shard_map/concatenate | solution.py:208
  42.0 5.2 %collective-permute-start.2 = (f32[768,128]{1,0:T(8,128)S(1)}, f32[768,128]{1,0:T(8,128)}, u32[]{:S(2)}, u32[]{:S(2)}) collective-permute-start(f32[768,128]{1,0:T(8,128)S(1)} %copy-done.2), channel_id=1, source_target_pairs={{0,1},{1,2},{2,3},{3,4},{4,5},{5,6},{6,7},{8,9},{9,10},{10,11},{11... | collective-permute-start | bytes 1179656 | tf_op jit(solution)/shard_map/ppermute | solution.py:184
  47.1 1.3 collective-permute-start.3
  48.5 7.6 %all_gather.6 = f32[3,16,24,128]{3,2,1,0:T(8,128)S(1)} all-gather(f32[3,4,24,128]{3,2,1,0:T(8,128)S(1)} %pad_maximum_fusion.3), channel_id=1, replica_groups=mesh['shot'=4,'tile'=8] {'shot'}, dimensions={1}, use_global_device_ids=true | all-gather | bytes 737280 | tf_op jit(solution)/shard_map/all_gather | solution.py:226
  58.9 1.7 scatter_custom_fusion
  60.6 0.9 constant_dynamic-update-slice_fusion.2
  61.5 0.9 collective-permute-done.2
  62.4 1.0 reshape.368
  63.5 1.0 reshape.369
  64.6 5.3 %pad_maximum_fusion.1.adj_ref = f32[4,16,160,128]{3,2,1,0:T(8,128)} fusion(f32[4,16,16,128]{3,2,1,0:T(8,128)S(1)} %concatenate.116, f32[4,16,128,128]{3,2,1,0:T(8,128)} %bitcast.162, f32[4,16,16,128]{3,2,1,0:T(8,128)S(1)} %concatenate.115), kind=kLoop, calls=%fused_computation.8 | loop fusion | flops 2621440 | bytes 10485760 | tf_op jit(solution)/shard_map/concatenate | solution.py:208
  69.9 3.9 %constant_dynamic-update-slice_fusion.1 = f32[3,16,160,128]{3,2,1,0:T(8,128)} fusion(f32[3,16,160,128]{3,2,1,0:T(8,128)} %constant_dynamic-update-slice_fusion.2, f32[3,16,128,128]{3,2,1,0:T(8,128)} %all-gather.2.cloned.1.call-done), kind=kLoop, calls=%fused_computation.134 | loop fusion | bytes 6291456
  74.6 29.9 %shard_map.94 = (f32[6,16,128,128]{3,2,1,0:T(8,128)}, f32[6,16,128,128]{3,2,1,0:T(8,128)}, f32[6,16,128,128]{3,2,1,0:T(8,128)}, f32[16,128,128]{2,1,0:T(8,128)}) custom-call(f32[6]{0:T(128)} %bitcast.184, f32[4,16,160,128]{3,2,1,0:T(8,128)} %pad_maximum_fusion.st_ref, f32[3,16,160,128]{3,2,1,0:T(8,128)} %constant_dynamic-update-slice_fusion.cf_ref, ...), custom_call_target="tpu_custom_call" | custom-call | tf_op jit(solution)/shard_map/pallas_call | solution.py:153
  104.5 5.2 %fusion.155 = (f32[1,16,128,128]{3,2,1,0:T(8,128)S(1)}, f32[1,16,128,128]{3,2,1,0:T(8,128)S(1)}, f32[1,16,128,128]{3,2,1,0:T(8,128)}, f32[1,16,128,128]{3,2,1,0:...) fusion(f32[6,16,128,128]{3,2,1,0:T(8,128)} %get-tuple-element.29), kind=kLoop, calls=%fused_computation.311 | loop fusion | bytes 12582912 | tf_op jit(solution)/shard_map/slice | solution.py:254
  109.7 2.0 gather_fusion
  111.7 2.0 gather_fusion.1
  113.7 2.1 gather_fusion.2
  115.8 2.1 gather_fusion.3
  117.9 1.1 gather_fusion.4
  119.1 1.1 gather_fusion.5
  120.3 1.3 collective-permute-start.5
  121.6 5.3 %collective-permute-start.4 = (f32[7,128]{1,0:T(8,128)S(1)}, f32[7,128]{1,0:T(8,128)S(1)}, u32[]{:S(2)}, u32[]{:S(2)}) collective-permute-start(f32[7,128]{1,0:T(8,128)S(1)} %pad_maximum_fusion.4), channel_id=1, source_target_pairs={{0,1},{1,2},{2,3},{3,4},{4,5},{5,6},{6,7},{8,9},{9,10},{10,11},{11... | collective-permute-start | bytes 10760 | tf_op jit(solution)/shard_map/ppermute | solution.py:184
  127.0 1.0 collective-permute-done.4
  133.3 0.9 fusion.6
  134.1 0.8 fusion.7
  138.4 0.9 fusion.19
  139.3 1.1 constant_dynamic-update-slice_fusion.8
  140.5 1.1 fusion.21
  141.6 1.3 constant_dynamic-update-slice_fusion.7
  142.9 0.9 fusion.23
  143.8 1.2 constant_dynamic-update-slice_fusion.6
  144.9 0.9 fusion.25
  145.8 1.2 constant_dynamic-update-slice_fusion.5
  147.0 0.9 fusion.27
  147.9 1.2 constant_dynamic-update-slice_fusion.4
  149.1 0.9 fusion.29
  150.0 1.2 constant_dynamic-update-slice_fusion.3.e_ref
  151.2 34.6 %shard_map.95 = (f32[3,16,128,128]{3,2,1,0:T(8,128)}, f32[2,16,128,128]{3,2,1,0:T(8,128)}) custom-call(f32[4,16,160,128]{3,2,1,0:T(8,128)} %pad_maximum_fusion.1.adj_ref, f32[3,16,160,128]{3,2,1,0:T(8,128)} %constant_dynamic-update-slice_fusion.cf_ref, f32[6,16,128,128]{3,2,1,0:T(8,128)} %get-tuple-element.27.h_ref, ...), custom_call_target="tpu_custom_call" | custom-call | tf_op jit(solution)/shard_map/pallas_call | solution.py:124
  185.8 3.9 %copy.15 = f32[3,4,4,128,128]{4,3,2,0,1:T(8,128)} copy(f32[3,4,4,128,128]{4,3,2,1,0:T(8,128)} %bitcast.171) | data formatting | bytes 6291456 | tf_op jit(solution)/shard_map/reshape | solution.py:284
  189.7 2.8 %maximum_bitcast_fusion = f32[1,2,16,128,128]{4,3,2,1,0:T(8,128)} fusion(f32[1,16,128,128]{3,2,1,0:T(8,128)} %bitcast.177, f32[1,16,128,128]{3,2,1,0:T(8,128)S(1)} %get-tuple-element.33), kind=kLoop, calls=%fused_computation.41 | loop fusion | flops 524288 | bytes 4194304 | tf_op jit(solution)/shard_map/broadcast_in_dim | solution.py:289
  192.6 39.4 %reduce-scatter.2.cloned.1.call-done = f32[1,3,4,128,128]{4,3,2,1,0:T(8,128)} async-done(((f32[4,3,4,128,128]{4,3,2,1,0:T(8,128)}), f32[1,3,4,128,128]{4,3,2,1,0:T(8,128)}) %reduce-scatter.2.cloned.1.call-update) | async-done | bytes 786448 | tf_op jit(solution)/shard_map/reduce_scatter | solution.py:285
  231.9 1.2 fusion.50
  233.1 0.9 pad_maximum_fusion.2
  (75 shorter events, 13.9 us)
Async XLA Ops:
  7.2 10.3 %copy-start.4 = (s32[1,128]{1,0:T(1,128)S(1)}, s32[1,128]{1,0:T(1,128)}, u32[]{:S(2)}) copy-start(s32[1,128]{1,0:T(1,128)} %param.12) | copy-start | bytes 1540
  7.2 62.7 %all-gather.2.cloned.1.call-start = ((), (), s32[]{:S(2)}) async-start(), calls=%async_computation.1 | async-start | bytes 3932160 | tf_op jit(solution)/shard_map/all_gather | solution.py:199
  7.9 224.0 %reduce-scatter.2.cloned.1.call-start = ((), (), s32[]{:S(2)}) async-start(), calls=%async_computation.2 | async-start | bytes 3932160 | tf_op jit(solution)/shard_map/reduce_scatter | solution.py:285
  11.3 25.0 %collective-permute-start = (f32[913,128]{1,0:T(8,128)S(1)}, f32[913,128]{1,0:T(8,128)S(1)}, u32[]{:S(2)}, u32[]{:S(2)}) collective-permute-start(f32[913,128]{1,0:T(8,128)S(1)} %get-tuple-element.69), channel_id=1, source_target_pairs={{0,1},{1,2},{2,3},{3,4},{4,5},{5,6},{6,7},{8,9},{9,10},{10,11},{11... | collective-permute-start | bytes 1402376 | tf_op jit(solution)/shard_map/ppermute | solution.py:184
  16.2 20.2 %collective-permute-start.1 = (f32[913,128]{1,0:T(8,128)S(1)}, f32[913,128]{1,0:T(8,128)S(1)}, u32[]{:S(2)}, u32[]{:S(2)}) collective-permute-start(f32[913,128]{1,0:T(8,128)S(1)} %get-tuple-element.68), channel_id=1, source_target_pairs={{1,0},{2,1},{3,2},{4,3},{5,4},{6,5},{7,6},{9,8},{10,9},{11,10},{12... | collective-permute-start | bytes 1402376 | tf_op jit(solution)/shard_map/ppermute | solution.py:185
  36.5 5.4 %copy-start.2 = (f32[768,128]{1,0:T(8,128)S(1)}, f32[768,128]{1,0:T(8,128)}, u32[]{:S(2)}) copy-start(f32[768,128]{1,0:T(8,128)} %reshape.361) | copy-start | bytes 1179652
  36.5 10.6 %copy-start.1 = (f32[768,128]{1,0:T(8,128)S(1)}, f32[768,128]{1,0:T(8,128)}, u32[]{:S(2)}) copy-start(f32[768,128]{1,0:T(8,128)} %reshape.360) | copy-start | bytes 1179652
  42.0 20.4 %collective-permute-start.2 = (f32[768,128]{1,0:T(8,128)S(1)}, f32[768,128]{1,0:T(8,128)}, u32[]{:S(2)}, u32[]{:S(2)}) collective-permute-start(f32[768,128]{1,0:T(8,128)S(1)} %copy-done.2), channel_id=1, source_target_pairs={{0,1},{1,2},{2,3},{3,4},{4,5},{5,6},{6,7},{8,9},{9,10},{10,11},{11... | collective-permute-start | bytes 1179656 | tf_op jit(solution)/shard_map/ppermute | solution.py:184
  47.1 16.3 %collective-permute-start.3 = (f32[768,128]{1,0:T(8,128)S(1)}, f32[768,128]{1,0:T(8,128)}, u32[]{:S(2)}, u32[]{:S(2)}) collective-permute-start(f32[768,128]{1,0:T(8,128)S(1)} %copy-done.1), channel_id=1, source_target_pairs={{1,0},{2,1},{3,2},{4,3},{5,4},{6,5},{7,6},{9,8},{10,9},{11,10},{12... | collective-permute-start | bytes 1179656 | tf_op jit(solution)/shard_map/ppermute | solution.py:185
  104.5 15.7 %copy-start.3 = (f32[1,6,128]{2,0,1:T(1,128)S(1)}, f32[1,6,128]{2,0,1:T(1,128)}, u32[]{:S(2)}) copy-start(f32[1,6,128]{2,0,1:T(1,128)} %param.13) | copy-start | bytes 9220
  120.3 6.6 %collective-permute-start.5 = (f32[7,128]{1,0:T(8,128)S(1)}, f32[7,128]{1,0:T(8,128)S(1)}, u32[]{:S(2)}, u32[]{:S(2)}) collective-permute-start(f32[7,128]{1,0:T(8,128)S(1)} %pad_maximum_fusion.4), channel_id=1, source_target_pairs={{1,0},{2,1},{3,2},{4,3},{5,4},{6,5},{7,6},{9,8},{10,9},{11,10},{12... | collective-permute-start | bytes 10760 | tf_op jit(solution)/shard_map/ppermute | solution.py:185
  121.6 6.4 %collective-permute-start.4 = (f32[7,128]{1,0:T(8,128)S(1)}, f32[7,128]{1,0:T(8,128)S(1)}, u32[]{:S(2)}, u32[]{:S(2)}) collective-permute-start(f32[7,128]{1,0:T(8,128)S(1)} %pad_maximum_fusion.4), channel_id=1, source_target_pairs={{0,1},{1,2},{2,3},{3,4},{4,5},{5,6},{6,7},{8,9},{9,10},{10,11},{11... | collective-permute-start | bytes 10760 | tf_op jit(solution)/shard_map/ppermute | solution.py:184
  189.7 42.2 %copy-start = (f32[3,4,128,128]{3,2,1,0:T(8,128)S(1)}, f32[3,4,128,128]{3,2,1,0:T(8,128)}, u32[]{:S(2)}) copy-start(f32[3,4,128,128]{3,2,1,0:T(8,128)} %param.7) | copy-start | bytes 2359300
Sparse Core Ops, SparseCore 0:
  9.5 31.2 all-gather.1
  189.8 42.0 reduce-scatter.1
where the time goes:
time: 242 us; the launch traced here: 241 us
  Pallas kernels  64.5 us (27%)
  waiting for transfers between devices  57.7 us (24%)
  local copies, waits for them, and re-layouts  41.2 us (17%)
  starting transfers between devices  19.3 us (8%)
  other arithmetic  18 us (7%)
  between operations  16.8 us (7%)
  matrix products  15.8 us (7%)
  blocking collectives  7.56 us (3%)
    reduce_scatter x1, waiting for transfers between devices, per_device(): summed = lax.psum_scatter(acc, 'shot', scatter_dimension=0, tiled=True)[0]  39.4 us
    pallas_call x1, Pallas kernels, run_adjoint(): pl.pallas_call(adjoint_kernel, out_shape=(jax.ShapeDtypeStruct((3, az, ax...  34.6 us
    pallas_call x1, Pallas kernels, run_forward(): pl.pallas_call(forward_kernel, out_shape=(loc, loc, loc, jax.ShapeDtypeSt...  29.9 us
    ppermute x3, waiting for transfers between devices, to_left_right(): from_left = lax.ppermute(tail, axis, [(i, i + 1) for i in range(count - 1)])  17.7 us
    dot_general x18, matrix products, per_device(): term = jnp.dot(pick_row, part, preferred_element_type=jnp.float32)  15.8 us
    ppermute x3, starting transfers between devices, to_left_right(): from_left = lax.ppermute(tail, axis, [(i, i + 1) for i in range(count - 1)])  15.4 us
    unnamed x17, local copies, waits for them, and re-layouts  10.7 us
    concatenate x2, other arithmetic, widen(): return jnp.concatenate([lo, mid, hi], axis=-2)  10.7 us
  transfers between devices with their start and end apart: 8, of which 4 were waited for; matrix products, arithmetic and copies ran while one was open for 11% of the time, Pallas kernels for 0%

commit v1 on v0

--- a/solution.py
+++ b/solution.py
@@ -61,7 +61,7 @@
         lax.fori_loop(0, az, plane, 0)
 
 
-def adjoint_kernel(adj_ref, cf_ref, h_ref, z_ref, e_ref, acc_ref, fin_ref, lb, mb, ob, fb):
+def adjoint_kernel(adj_ref, cf_ref, h_ref, z_ref, row_ref, m_ref, acc_ref, fin_ref, lb, mb, ob, fb):
     steps = h_ref.shape[0]
     az, xd, ay = adj_ref.shape[1:]
     ax = h_ref.shape[2]
@@ -98,7 +98,12 @@
             yp1 = jnp.where(lane < ay - 1, pltpu.roll(f, ay - 1, 1), 0.0)
             yp2 = jnp.where(lane < ay - 2, pltpu.roll(f, ay - 2, 1), 0.0)
             hf = d2x + d2(ym2, ym1, f, yp1, yp2)
-            ln = e_ref[s, d] + 2.0 * lc + hf - lb[old, d]
+            hit = lax.broadcasted_iota(jnp.int32, (xd, row_ref.shape[1]), 0) + d * xd == row_ref[...]
+            pick = jnp.where(hit, 1.0, 0.0).astype(jnp.bfloat16)
+            e = jnp.dot(pick, m_ref[s, 0], preferred_element_type=jnp.float32)
+            e = e + jnp.dot(pick, m_ref[s, 1], preferred_element_type=jnp.float32)
+            e = e + jnp.dot(pick, m_ref[s, 2], preferred_element_type=jnp.float32)
+            ln = e + 2.0 * lc + hf - lb[old, d]
             mn = 2.0 * mc + d2(ob[d], ob[d + 1], ob[d + 2], ob[d + 3], ob[d + 4]) - mb[old, d]
             lb[old, d] = ln
             mb[old, d] = mn
@@ -117,14 +122,14 @@
         lax.fori_loop(0, az, plane, 0)
 
 
-def run_adjoint(adj, cf, h_all, z_all, e_all):
+def run_adjoint(adj, cf, h_all, z_all, row, parts):
     _, az, xd, ay = adj.shape
     ax = h_all.shape[2]
     vm = pl.BlockSpec(memory_space=pltpu.VMEM)
     return pl.pallas_call(
         adjoint_kernel,
         out_shape=(jax.ShapeDtypeStruct((3, az, ax, ay), jnp.float32), jax.ShapeDtypeStruct((2, az, ax, ay), jnp.float32)),
-        in_specs=[vm] * 5,
+        in_specs=[vm] * 6,
         out_specs=(vm, vm),
         scratch_shapes=[
             pltpu.VMEM((2, az, xd, ay), jnp.float32),
@@ -134,15 +139,15 @@
         ],
         compiler_params=pltpu.CompilerParams(vmem_limit_bytes=62 * 1024 * 1024),
         interpret=INTERPRET,
-    )(adj, cf, h_all, z_all, e_all)
+    )(adj, cf, h_all, z_all, row, parts)
 
 
 def exact_parts(x):
-    hi = x.astype(jnp.bfloat16)
-    rest = x - hi.astype(jnp.float32)
-    mid = rest.astype(jnp.bfloat16)
-    lo = (rest - mid.astype(jnp.float32)).astype(jnp.bfloat16)
-    return hi, mid, lo
+    hi = lax.reduce_precision(x, exponent_bits=8, mantissa_bits=7)
+    rest = x - hi
+    mid = lax.reduce_precision(rest, exponent_bits=8, mantissa_bits=7)
+    lo = lax.reduce_precision(rest - mid, exponent_bits=8, mantissa_bits=7)
+    return hi.astype(jnp.bfloat16), mid.astype(jnp.bfloat16), lo.astype(jnp.bfloat16)
 
 
 def run_forward(wave, st, cf, mask, ax):
@@ -264,25 +269,30 @@
     rec_r = jnp.where(okr_r, rec_r, cells_ext)
     rec_all = jnp.concatenate([rec_own, rec_l, rec_r])
 
-    n_rows = az * xe
-    pick_row = (lax.broadcasted_iota(jnp.int32, (n_rows, rec_all.shape[0]), 0) == (rec_all // ay)[None, :]).astype(jnp.bfloat16)
     pick_lane = lax.broadcasted_iota(jnp.int32, (rec_all.shape[0], ay), 1) == (rec_all % ay)[:, None]
-    dense = []
+    parts = []
     for step in range(steps):
         vals = jnp.concatenate([records[step], left3[step], right3[step]])
-        spread = jnp.where(pick_lane, vals[:, None], 0.0)
-        total = None
-        for part in exact_parts(spread):
-            term = jnp.dot(pick_row, part, preferred_element_type=jnp.float32)
-            total = term if total is None else total + term
-        dense.append(total.reshape(ext_shape))
-    acc, fin = run_adjoint(adj_ext, full_ext, h_all, z_all, jnp.stack(dense))
-    acc_h, acc_x, acc_z = acc[0], acc[1], acc[2]
+        parts.append(jnp.stack(exact_parts(jnp.where(pick_lane, vals[:, None], 0.0))))
+    rec_rows = (rec_all // ay)[None, :]
+    acc, fin = run_adjoint(adj_ext, full_ext, h_all, z_all, rec_rows, jnp.stack(parts))
 
     n_shot = lax.axis_size("shot")
-    acc = jnp.stack([acc_h, acc_x, acc_z])
-    acc = acc.reshape(3, n_shot, az // n_shot, ax, ay).transpose(1, 0, 2, 3, 4)
-    summed = lax.psum_scatter(acc, "shot", scatter_dimension=0, tiled=True)[0]
+    n_y = n_shot // 2
+    zc = az // n_shot
+    me = lax.axis_index("shot")
+    core = me % 2
+    yy = me // 2
+    chunks = acc.reshape(3, n_y, 2, zc, ax, ay)
+    send = lax.dynamic_index_in_dim(chunks, 1 - core, axis=2, keepdims=False)
+    got = lax.ppermute(send, "shot", [(i, i ^ 1) for i in range(n_shot)])
+    mine = lax.dynamic_index_in_dim(chunks, core, axis=2, keepdims=False) + got
+    ring = [(y * 2 + c, ((y + 1) % n_y) * 2 + c) for y in range(n_y) for c in range(2)]
+    partial = lax.dynamic_index_in_dim(mine, (yy + n_y - 1) % n_y, axis=1, keepdims=False)
+    for t in range(n_y - 1):
+        partial = lax.ppermute(partial, "shot", ring)
+        partial = partial + lax.dynamic_index_in_dim(mine, (yy + 2 * n_y - t - 2) % n_y, axis=1, keepdims=False)
+    summed = partial
     q_h, q_x, q_z = summed[0], summed[1], summed[2]
     c, a, b = coefs[0], coefs[1], coefs[2]
     gradient = jnp.stack([a * q_h + b * q_x + q_z, c * q_h, c * q_x])

time: 242 us -> 223 us (0.921)
  waiting for transfers between devices: 57.7 us -> 40.5 us
  matrix products: 15.8 us -> 0 us
  Pallas kernels: 64.5 us -> 73 us
  other arithmetic: 18 us -> 24.2 us
    reduce_scatter x1 -> x0, waiting for transfers between devices: 39.4 us -> none  [per_device(): summed = lax.psum_scatter(acc, 'shot', scatter_dimension=0, tiled=True)[0]]
    ppermute x0 -> x2, waiting for transfers between devices: none -> 20.8 us  [the longest x1 17.1 us: per_device(): partial = lax.ppermute(partial, 'shot', ring)]
    dot_general x18 -> x0, matrix products: 15.8 us -> none  [per_device(): term = jnp.dot(pick_row, part, preferred_element_type=jnp.float32)]
    pallas_call x1, Pallas kernels: 34.6 us -> 43.2 us  [run_adjoint(): pl.pallas_call(adjoint_kernel, out_shape=(jax.ShapeDtypeStruct((3, az, ax...]
    unnamed x17 -> x20, local copies, waits for them, and re-layouts: 10.7 us -> 5.91 us
    ppermute x3, waiting for transfers between devices: 0.01 us -> 4.01 us  [to_left_right(): lax.ppermute(head, axis, [(i + 1, i) for i in range(count - 1)])]
    reshape x1 -> x0, local copies, waits for them, and re-layouts: 3.88 us -> none  [per_device(): acc = acc.reshape(3, n_shot, az // n_shot, ax, ay).transpose(1, 0, 2, 3, 4)]
    unnamed x0 -> x5, other arithmetic: none -> 3.67 us
  transfers between devices with their start and end apart: 8 -> 9, of which waited for: 4 -> 4; matrix products, arithmetic and copies ran while one was open for 11% -> 13% of each run, Pallas kernels for 0% -> 0%
where the time goes in v1:
time: 223 us; the launch traced here: 222 us
  Pallas kernels  73 us (33%)
  waiting for transfers between devices  40.5 us (18%)
  local copies, waits for them, and re-layouts  38.8 us (17%)
  other arithmetic  24.2 us (11%)
  starting transfers between devices  20.8 us (9%)
  between operations  16.8 us (8%)
  blocking collectives  7.56 us (3%)
    pallas_call x1, Pallas kernels, run_adjoint(): pl.pallas_call(adjoint_kernel, out_shape=(jax.ShapeDtypeStruct((3, az, ax...  43.2 us
    pallas_call x1, Pallas kernels, run_forward(): pl.pallas_call(forward_kernel, out_shape=(loc, loc, loc, jax.ShapeDtypeSt...  29.7 us
    ppermute x1, waiting for transfers between devices, per_device(): partial = lax.ppermute(partial, 'shot', ring)  17.1 us
    ppermute x3, starting transfers between devices, to_left_right(): from_left = lax.ppermute(tail, axis, [(i, i + 1) for i in range(count - 1)])  15.4 us
    ppermute x3, waiting for transfers between devices, to_left_right(): from_left = lax.ppermute(tail, axis, [(i, i + 1) for i in range(count - 1)])  15 us
    concatenate x2, other arithmetic, widen(): return jnp.concatenate([lo, mid, hi], axis=-2)  10.6 us
    gather x6, local copies, waits for them, and re-layouts, per_device(): p_all[n].reshape(-1)[receivers]  10.5 us
    all_gather x1, blocking collectives, per_device(): lax.all_gather(jnp.concatenate([cf_l, cf_r], axis=2), 'shot', axis=1, til...  7.56 us
  transfers between devices with their start and end apart: 9, of which 4 were waited for; matrix products, arithmetic and copies ran while one was open for 13% of the time, Pallas kernels for 0%

profile of v1, /device:TPU:0, one launch (start us, length us, event | category | flops | bytes accessed | tf_op | source)
XLA Modules:
  0.0 221.6 jit_solution(11344147394724952383)
XLA Ops:
  8.6 1.3 fusion.46
  10.4 5.6 %collective-permute-start = (f32[913,128]{1,0:T(8,128)S(1)}, f32[913,128]{1,0:T(8,128)}, u32[]{:S(2)}, u32[]{:S(2)}) collective-permute-start(f32[913,128]{1,0:T(8,128)S(1)} %get-tuple-element.87), channel_id=1, source_target_pairs={{0,1},{1,2},{2,3},{3,4},{4,5},{5,6},{6,7},{8,9},{9,10},{10,11},{11... | collective-permute-start | bytes 1402376 | tf_op jit(solution)/shard_map/ppermute | solution.py:189
  16.0 1.3 collective-permute-start.1
  17.3 1.4 fusion.47
  18.8 0.8 reshape.1249
  19.6 0.8 reshape.1250
  20.4 15.0 %collective-permute-done = f32[913,128]{1,0:T(8,128)} collective-permute-done((f32[913,128]{1,0:T(8,128)S(1)}, f32[913,128]{1,0:T(8,128)}, u32[]{:S(2)}, u32[]{:S(2)}) %collective-permute-start) | collective-permute-done | bytes 467488 | tf_op jit(solution)/shard_map/ppermute | solution.py:189
  35.4 0.9 slice.203
  36.3 0.9 slice.204
  37.8 1.1 slice.200
  38.9 1.0 slice.202
  40.1 5.3 %pad_maximum_fusion.st_ref = f32[4,16,160,128]{3,2,1,0:T(8,128)} fusion(f32[4,16,16,128]{3,2,1,0:T(8,128)S(1)} %concatenate.119, f32[4,16,128,128]{3,2,1,0:T(8,128)} %bitcast.164, f32[4,16,16,128]{3,2,1,0:T(8,128)S(1)} %concatenate.117), kind=kLoop, calls=%fused_computation.7 | loop fusion | flops 2621440 | bytes 10485760 | tf_op jit(solution)/shard_map/concatenate | solution.py:213
  45.4 5.2 %collective-permute-start.2 = (f32[768,128]{1,0:T(8,128)S(1)}, f32[768,128]{1,0:T(8,128)}, u32[]{:S(2)}, u32[]{:S(2)}) collective-permute-start(f32[768,128]{1,0:T(8,128)S(1)} %copy-done.5), channel_id=1, source_target_pairs={{0,1},{1,2},{2,3},{3,4},{4,5},{5,6},{6,7},{8,9},{9,10},{10,11},{11... | collective-permute-start | bytes 1179656 | tf_op jit(solution)/shard_map/ppermute | solution.py:189
  50.7 1.3 collective-permute-start.3
  52.0 7.6 %all_gather.6 = f32[3,16,24,128]{3,2,1,0:T(8,128)S(1)} all-gather(f32[3,4,24,128]{3,2,1,0:T(8,128)S(1)} %pad_maximum_fusion.3), channel_id=1, replica_groups=mesh['shot'=4,'tile'=8] {'shot'}, dimensions={1}, use_global_device_ids=true | all-gather | bytes 737280 | tf_op jit(solution)/shard_map/all_gather | solution.py:231
  59.6 1.2 slice.207
  61.5 1.2 slice.208
  63.7 1.7 scatter_custom_fusion
  65.4 0.8 constant_dynamic-update-slice_fusion.2
  66.3 1.0 reshape.1257
  67.4 5.3 %pad_maximum_fusion.1.adj_ref = f32[4,16,160,128]{3,2,1,0:T(8,128)} fusion(f32[4,16,16,128]{3,2,1,0:T(8,128)S(1)} %concatenate.122, f32[4,16,128,128]{3,2,1,0:T(8,128)} %bitcast.166, f32[4,16,16,128]{3,2,1,0:T(8,128)S(1)} %concatenate.121), kind=kLoop, calls=%fused_computation.8 | loop fusion | flops 2621440 | bytes 10485760 | tf_op jit(solution)/shard_map/concatenate | solution.py:213
  72.7 3.9 %constant_dynamic-update-slice_fusion.1 = f32[3,16,160,128]{3,2,1,0:T(8,128)} fusion(f32[3,16,160,128]{3,2,1,0:T(8,128)} %constant_dynamic-update-slice_fusion.2, f32[3,16,128,128]{3,2,1,0:T(8,128)} %all-gather.2.cloned.1.call-done), kind=kLoop, calls=%fused_computation.73 | loop fusion | bytes 6291456
  76.6 0.8 constant_dynamic-update-slice_fusion.cf_ref
  77.4 29.7 %shard_map.94 = (f32[6,16,128,128]{3,2,1,0:T(8,128)}, f32[6,16,128,128]{3,2,1,0:T(8,128)}, f32[6,16,128,128]{3,2,1,0:T(8,128)}, f32[16,128,128]{2,1,0:T(8,128)}) custom-call(f32[6]{0:T(128)} %bitcast.183, f32[4,16,160,128]{3,2,1,0:T(8,128)} %pad_maximum_fusion.st_ref, f32[3,16,160,128]{3,2,1,0:T(8,128)} %constant_dynamic-update-slice_fusion.cf_ref, ...), custom_call_target="tpu_custom_call" | custom-call | tf_op jit(solution)/shard_map/pallas_call | solution.py:158
  107.1 5.2 %fusion.45 = (f32[1,16,128,128]{3,2,1,0:T(8,128)S(1)}, f32[1,16,128,128]{3,2,1,0:T(8,128)S(1)}, f32[1,16,128,128]{3,2,1,0:T(8,128)}, f32[1,16,128,128]{3,2,1,0:T...) fusion(f32[6,16,128,128]{3,2,1,0:T(8,128)} %get-tuple-element.29), kind=kLoop, calls=%fused_computation.220 | loop fusion | bytes 12582912 | tf_op jit(solution)/shard_map/slice | solution.py:259
  112.3 2.0 gather_fusion
  114.3 2.0 gather_fusion.1
  116.3 2.1 gather_fusion.2
  118.4 2.1 gather_fusion.3
  120.5 1.1 gather_fusion.4
  121.6 1.1 gather_fusion.5
  122.9 4.6 %collective-permute-start.4 = (f32[7,128]{1,0:T(8,128)S(1)}, f32[7,128]{1,0:T(8,128)S(1)}, u32[]{:S(2)}, u32[]{:S(2)}) collective-permute-start(f32[7,128]{1,0:T(8,128)S(1)} %pad_maximum_fusion.4), channel_id=1, source_target_pairs={{0,1},{1,2},{2,3},{3,4},{4,5},{5,6},{6,7},{8,9},{9,10},{10,11},{11... | collective-permute-start | bytes 10760 | tf_op jit(solution)/shard_map/ppermute | solution.py:189
  127.4 1.5 collective-permute-start.5
  128.9 4.0 %collective-permute-done.5 = f32[7,128]{1,0:T(8,128)S(1)} collective-permute-done((f32[7,128]{1,0:T(8,128)S(1)}, f32[7,128]{1,0:T(8,128)S(1)}, u32[]{:S(2)}, u32[]{:S(2)}) %collective-permute-start.5) | collective-permute-done | bytes 3616 | tf_op jit(solution)/shard_map/ppermute | solution.py:190
  133.6 0.7 fusion.2
  135.7 0.7 fusion.4
  136.4 0.7 fusion.5
  138.6 43.2 %shard_map.95 = (f32[3,16,128,128]{3,2,1,0:T(8,128)}, f32[2,16,128,128]{3,2,1,0:T(8,128)}) custom-call(f32[4,16,160,128]{3,2,1,0:T(8,128)} %pad_maximum_fusion.1.adj_ref, f32[3,16,160,128]{3,2,1,0:T(8,128)} %constant_dynamic-update-slice_fusion.cf_ref, f32[6,16,128,128]{3,2,1,0:T(8,128)} %get-tuple-element.27.h_ref, ...), custom_call_target="tpu_custom_call" | custom-call | tf_op jit(solution)/shard_map/pallas_call | solution.py:129
  181.9 2.7 %dynamic-slice_bitcast_fusion = f32[3,2,4,128,128]{4,3,2,1,0:T(8,128)} fusion(f32[3,2,2,4,128,128]{5,4,3,2,1,0:T(8,128)} %bitcast.169, s32[]{:T(128)S(6)} %select_n.483), kind=kLoop, calls=%fused_computation.11 | loop fusion | bytes 3145732 | tf_op jit(solution)/shard_map/jit(dynamic_index_in_dim)/squeeze | solution.py:287
  184.6 3.7 %collective-permute-done.6 = f32[3,2,4,128,128]{4,3,2,1,0:T(8,128)} collective-permute-done((f32[3,2,4,128,128]{4,3,2,1,0:T(8,128)}, f32[3,2,4,128,128]{4,3,2,1,0:T(8,128)}, u32[]{:S(2)}, u32[]{:S(2)}) %collective-permute-start.6) | collective-permute-done | bytes 1572896 | tf_op jit(solution)/shard_map/ppermute | solution.py:288
  188.3 2.1 bitcast_add_fusion
  190.4 1.2 copy-done
  191.6 0.9 dynamic-slice_bitcast_fusion.1
  192.5 1.3 collective-permute-start.7
  193.8 1.5 maximum_bitcast_fusion
  195.3 17.1 %collective-permute-done.7 = f32[3,4,128,128]{3,2,1,0:T(8,128)} collective-permute-done((f32[3,4,128,128]{3,2,1,0:T(8,128)}, f32[3,4,128,128]{3,2,1,0:T(8,128)}, u32[]{:S(2)}, u32[]{:S(2)}) %collective-permute-start.7) | collective-permute-done | bytes 786464 | tf_op jit(solution)/shard_map/ppermute | solution.py:293
  212.4 1.3 bitcast_add_fusion.1
  213.8 0.9 pad_maximum_fusion.2
  (71 shorter events, 6.0 us)
Async XLA Ops:
  7.2 65.5 %all-gather.2.cloned.1.call-start = ((), (), s32[]{:S(2)}) async-start(), calls=%async_computation | async-start | bytes 3932160 | tf_op jit(solution)/shard_map/all_gather | solution.py:204
  7.9 2.1 copy-start.2
  9.9 7.4 %copy-start.8 = (s32[1,128]{1,0:T(1,128)S(1)}, s32[1,128]{1,0:T(1,128)}, u32[]{:S(2)}) copy-start(s32[1,128]{1,0:T(1,128)} %param.12) | copy-start | bytes 1540
  10.4 25.0 %collective-permute-start = (f32[913,128]{1,0:T(8,128)S(1)}, f32[913,128]{1,0:T(8,128)}, u32[]{:S(2)}, u32[]{:S(2)}) collective-permute-start(f32[913,128]{1,0:T(8,128)S(1)} %get-tuple-element.87), channel_id=1, source_target_pairs={{0,1},{1,2},{2,3},{3,4},{4,5},{5,6},{6,7},{8,9},{9,10},{10,11},{11... | collective-permute-start | bytes 1402376 | tf_op jit(solution)/shard_map/ppermute | solution.py:189
  16.0 20.3 %collective-permute-start.1 = (f32[913,128]{1,0:T(8,128)S(1)}, f32[913,128]{1,0:T(8,128)}, u32[]{:S(2)}, u32[]{:S(2)}) collective-permute-start(f32[913,128]{1,0:T(8,128)S(1)} %get-tuple-element.86), channel_id=1, source_target_pairs={{1,0},{2,1},{3,2},{4,3},{5,4},{6,5},{7,6},{9,8},{10,9},{11,10},{12... | collective-permute-start | bytes 1402376 | tf_op jit(solution)/shard_map/ppermute | solution.py:190
  40.1 5.4 %copy-start.5 = (f32[768,128]{1,0:T(8,128)S(1)}, f32[768,128]{1,0:T(8,128)}, u32[]{:S(2)}) copy-start(f32[768,128]{1,0:T(8,128)} %reshape.1250) | copy-start | bytes 1179652
  40.1 10.6 %copy-start.4 = (f32[768,128]{1,0:T(8,128)S(1)}, f32[768,128]{1,0:T(8,128)}, u32[]{:S(2)}) copy-start(f32[768,128]{1,0:T(8,128)} %reshape.1249) | copy-start | bytes 1179652
  40.1 11.8 %copy-start.6 = (f32[3,4,12,128]{3,2,1,0:T(8,128)S(1)}, f32[3,4,12,128]{3,2,1,0:T(8,128)}, u32[]{:S(2)}) copy-start(f32[3,4,12,128]{3,2,1,0:T(8,128)} %reshape.1260) | copy-start | bytes 221188
  45.4 20.8 %collective-permute-start.2 = (f32[768,128]{1,0:T(8,128)S(1)}, f32[768,128]{1,0:T(8,128)}, u32[]{:S(2)}, u32[]{:S(2)}) collective-permute-start(f32[768,128]{1,0:T(8,128)S(1)} %copy-done.5), channel_id=1, source_target_pairs={{0,1},{1,2},{2,3},{3,4},{4,5},{5,6},{6,7},{8,9},{9,10},{10,11},{11... | collective-permute-start | bytes 1179656 | tf_op jit(solution)/shard_map/ppermute | solution.py:189
  50.7 16.7 %collective-permute-start.3 = (f32[768,128]{1,0:T(8,128)S(1)}, f32[768,128]{1,0:T(8,128)S(1)}, u32[]{:S(2)}, u32[]{:S(2)}) collective-permute-start(f32[768,128]{1,0:T(8,128)S(1)} %copy-done.4), channel_id=1, source_target_pairs={{1,0},{2,1},{3,2},{4,3},{5,4},{6,5},{7,6},{9,8},{10,9},{11,10},{12... | collective-permute-start | bytes 1179656 | tf_op jit(solution)/shard_map/ppermute | solution.py:190
  112.3 10.5 %copy-start.7 = (f32[1,6,128]{2,0,1:T(1,128)S(1)}, f32[1,6,128]{2,0,1:T(1,128)}, u32[]{:S(2)}) copy-start(f32[1,6,128]{2,0,1:T(1,128)} %param.13) | copy-start | bytes 9220
  122.9 10.1 %collective-permute-start.4 = (f32[7,128]{1,0:T(8,128)S(1)}, f32[7,128]{1,0:T(8,128)S(1)}, u32[]{:S(2)}, u32[]{:S(2)}) collective-permute-start(f32[7,128]{1,0:T(8,128)S(1)} %pad_maximum_fusion.4), channel_id=1, source_target_pairs={{0,1},{1,2},{2,3},{3,4},{4,5},{5,6},{6,7},{8,9},{9,10},{10,11},{11... | collective-permute-start | bytes 10760 | tf_op jit(solution)/shard_map/ppermute | solution.py:189
  127.4 5.5 %collective-permute-start.5 = (f32[7,128]{1,0:T(8,128)S(1)}, f32[7,128]{1,0:T(8,128)S(1)}, u32[]{:S(2)}, u32[]{:S(2)}) collective-permute-start(f32[7,128]{1,0:T(8,128)S(1)} %pad_maximum_fusion.4), channel_id=1, source_target_pairs={{1,0},{2,1},{3,2},{4,3},{5,4},{6,5},{7,6},{9,8},{10,9},{11,10},{12... | collective-permute-start | bytes 10760 | tf_op jit(solution)/shard_map/ppermute | solution.py:190
  184.6 3.8 %collective-permute-start.6 = (f32[3,2,4,128,128]{4,3,2,1,0:T(8,128)}, f32[3,2,4,128,128]{4,3,2,1,0:T(8,128)}, u32[]{:S(2)}, u32[]{:S(2)}) collective-permute-start(f32[3,2,4,128,128]{4,3,2,1,0:T(8,128)} %dynamic-slice_bitcast_fusion), channel_id=1, source_target_pairs={{0,8},{8,0},{16,24},{24,16},{1,9},{9,1},{17,25},{25,17},{2,10},{10... | collective-permute-start | bytes 4718600 | tf_op jit(solution)/shard_map/ppermute | solution.py:288
  184.6 9.2 %copy-start.3 = (f32[16,128,128]{2,1,0:T(8,128)S(1)}, f32[16,128,128]{2,1,0:T(8,128)}, u32[]{:S(2)}) copy-start(f32[16,128,128]{2,1,0:T(8,128)} %get-tuple-element.31) | copy-start | bytes 3145732
  190.4 1.2 copy-start
  192.5 19.9 %collective-permute-start.7 = (f32[3,4,128,128]{3,2,1,0:T(8,128)}, f32[3,4,128,128]{3,2,1,0:T(8,128)}, u32[]{:S(2)}, u32[]{:S(2)}) collective-permute-start(f32[3,4,128,128]{3,2,1,0:T(8,128)} %dynamic-slice_bitcast_fusion.1), channel_id=1, source_target_pairs={{0,16},{8,24},{16,0},{24,8},{1,17},{9,25},{17,1},{25,9},{2,18},{10... | collective-permute-start | bytes 2359304 | tf_op jit(solution)/shard_map/ppermute | solution.py:293
  193.8 18.6 %copy-start.1 = (f32[3,2,4,128,128]{4,3,2,1,0:T(8,128)S(1)}, f32[3,2,4,128,128]{4,3,2,1,0:T(8,128)}, u32[]{:S(2)}) copy-start(f32[3,2,4,128,128]{4,3,2,1,0:T(8,128)} %copy-done) | copy-start | bytes 4718596
Sparse Core Ops, SparseCore 0:
  9.5 31.2 all-gather.1

commit v2 on v1

--- a/solution.py
+++ b/solution.py
@@ -15,17 +15,26 @@
     return ((((-m2) + 16.0 * m1) - 30.0 * c0) + 16.0 * p1 - p2) * (1.0 / 12.0)
 
 
-def forward_kernel(wave_ref, st_ref, cf_ref, mask_ref, h_ref, z_ref, pl_ref, q_ref, pb, qb):
+def place(dst, mid, lo, hi, at):
+    w = lo.shape[-2]
+    ax = mid.shape[-2]
+    dst[..., pl.ds(at + OFF - w, w), :] = lo
+    dst[..., pl.ds(at + OFF, ax), :] = mid
+    dst[..., pl.ds(at + OFF + ax, w), :] = hi
+
+
+def forward_kernel(wave_ref, fs_ref, sl_ref, sr_ref, co_ref, ch_ref, mask_ref, h_ref, z_ref, pl_ref, q_ref, pb, qb, cf_ref):
     steps = h_ref.shape[0]
-    az, xd, ay = st_ref.shape[1:]
+    az, xd, ay = mask_ref.shape
     ax = h_ref.shape[2]
+    w = sl_ref.shape[2]
     pb[...] = jnp.zeros(pb.shape, jnp.float32)
     qb[...] = jnp.zeros(qb.shape, jnp.float32)
+    cf_ref[...] = jnp.zeros(cf_ref.shape, jnp.float32)
     inner = pl.ds(PADX, xd)
-    pb[0, 2:2 + az, inner, :] = st_ref[0]
-    qb[0, 2:2 + az, inner, :] = st_ref[1]
-    pb[1, 2:2 + az, inner, :] = st_ref[2]
-    qb[1, 2:2 + az, inner, :] = st_ref[3]
+    for k, (buf, slot) in enumerate(((pb, 0), (qb, 0), (pb, 1), (qb, 1))):
+        place(buf.at[slot, 2:2 + az], fs_ref[k], sl_ref[k], sr_ref[k], PADX)
+    place(cf_ref, co_ref[...], ch_ref[:, :, :w], ch_ref[:, :, w:], 0)
     lane = lax.broadcasted_iota(jnp.int32, (xd, ay), 1)
     for n in range(steps):
         cur = n % 2
@@ -61,14 +70,17 @@
         lax.fori_loop(0, az, plane, 0)
 
 
-def adjoint_kernel(adj_ref, cf_ref, h_ref, z_ref, row_ref, m_ref, acc_ref, fin_ref, lb, mb, ob, fb):
+def adjoint_kernel(ad_ref, al_ref, ar_ref, co_ref, ch_ref, h_ref, z_ref, row_ref, m_ref, acc_ref, fin_ref, lb, mb, ob, fb, cf_ref):
     steps = h_ref.shape[0]
-    az, xd, ay = adj_ref.shape[1:]
+    az, xd, ay = ob.shape[0] - 4, ob.shape[1], ob.shape[2]
     ax = h_ref.shape[2]
-    lb[0] = adj_ref[0]
-    mb[0] = adj_ref[1]
-    lb[1] = adj_ref[2]
-    mb[1] = adj_ref[3]
+    w = al_ref.shape[2]
+    lb[...] = jnp.zeros(lb.shape, jnp.float32)
+    mb[...] = jnp.zeros(mb.shape, jnp.float32)
+    cf_ref[...] = jnp.zeros(cf_ref.shape, jnp.float32)
+    for k, (buf, slot) in enumerate(((lb, 0), (mb, 0), (lb, 1), (mb, 1))):
+        place(buf.at[slot], ad_ref[k], al_ref[k], ar_ref[k], 0)
+    place(cf_ref, co_ref[...], ch_ref[:, :, :w], ch_ref[:, :, w:], 0)
     ob[...] = jnp.zeros(ob.shape, jnp.float32)
     fb[...] = jnp.zeros(fb.shape, jnp.float32)
     acc_ref[...] = jnp.zeros(acc_ref.shape, jnp.float32)
@@ -122,24 +134,25 @@
         lax.fori_loop(0, az, plane, 0)
 
 
-def run_adjoint(adj, cf, h_all, z_all, row, parts):
-    _, az, xd, ay = adj.shape
-    ax = h_all.shape[2]
+def run_adjoint(ad, al, ar, co, ch, h_all, z_all, row, parts):
+    _, az, ax, ay = ad.shape
+    xd = ax + 2 * OFF
     vm = pl.BlockSpec(memory_space=pltpu.VMEM)
     return pl.pallas_call(
         adjoint_kernel,
         out_shape=(jax.ShapeDtypeStruct((3, az, ax, ay), jnp.float32), jax.ShapeDtypeStruct((2, az, ax, ay), jnp.float32)),
-        in_specs=[vm] * 6,
+        in_specs=[vm] * 9,
         out_specs=(vm, vm),
         scratch_shapes=[
             pltpu.VMEM((2, az, xd, ay), jnp.float32),
             pltpu.VMEM((2, az, xd, ay), jnp.float32),
             pltpu.VMEM((az + 4, xd, ay), jnp.float32),
             pltpu.VMEM((xd + 2 * PADX, ay), jnp.float32),
+            pltpu.VMEM((3, az, xd, ay), jnp.float32),
         ],
         compiler_params=pltpu.CompilerParams(vmem_limit_bytes=62 * 1024 * 1024),
         interpret=INTERPRET,
-    )(adj, cf, h_all, z_all, row, parts)
+    )(ad, al, ar, co, ch, h_all, z_all, row, parts)
 
 
 def exact_parts(x):
@@ -150,20 +163,21 @@
     return hi.astype(jnp.bfloat16), mid.astype(jnp.bfloat16), lo.astype(jnp.bfloat16)
 
 
-def run_forward(wave, st, cf, mask, ax):
+def run_forward(wave, fs, sl, sr, co, ch, mask):
     steps = wave.shape[0]
-    _, az, xd, ay = st.shape
+    az, xd, ay = mask.shape
+    ax = fs.shape[2]
     vm = pl.BlockSpec(memory_space=pltpu.VMEM)
     loc = jax.ShapeDtypeStruct((steps, az, ax, ay), jnp.float32)
     return pl.pallas_call(
         forward_kernel,
         out_shape=(loc, loc, loc, jax.ShapeDtypeStruct((az, ax, ay), jnp.float32)),
-        in_specs=[pl.BlockSpec(memory_space=pltpu.SMEM), vm, vm, vm],
+        in_specs=[pl.BlockSpec(memory_space=pltpu.SMEM)] + [vm] * 6,
         out_specs=(vm, vm, vm, vm),
-        scratch_shapes=[pltpu.VMEM((2, az + 4, xd + 2 * PADX, ay), jnp.float32)] * 2,
-        compiler_params=pltpu.CompilerParams(vmem_limit_bytes=60 * 1024 * 1024),
+        scratch_shapes=[pltpu.VMEM((2, az + 4, xd + 2 * PADX, ay), jnp.float32)] * 2 + [pltpu.VMEM((3, az, xd, ay), jnp.float32)],
+        compiler_params=pltpu.CompilerParams(vmem_limit_bytes=62 * 1024 * 1024),
         interpret=INTERPRET,
-    )(wave, st, cf, mask)
+    )(wave, fs, sl, sr, co, ch, mask)
 
 
 def taps(padded, size, axis):
@@ -229,9 +243,6 @@
     st_l, cf_l, sc_l = unpack1(left1)
     st_r, cf_r, sc_r = unpack1(right1)
     cf_halo = lax.all_gather(jnp.concatenate([cf_l, cf_r], axis=2), "shot", axis=1, tiled=True)
-    full_ext = widen(cf_halo[:, :, :w], full, cf_halo[:, :, w:])
-    speed, stretch, couple = full_ext[0], full_ext[1], full_ext[2]
-    state = widen(st_l, fs, st_r)
 
     def ext_index(cell, shift):
         depth = cell // (ax * ay)
@@ -250,11 +261,10 @@
     source_mask = jnp.zeros((cells_ext,), jnp.float32).at[src_idx].add(src_on, mode="drop").reshape(ext_shape)
 
     ad = adj_state[0]
-    ad_head, ad_tail, state = lax.optimization_barrier((rows(ad[:, :, :w]), rows(ad[:, :, ax - w:]), state))
+    ad_head, ad_tail, st_l, st_r = lax.optimization_barrier((rows(ad[:, :, :w]), rows(ad[:, :, ax - w:]), st_l, st_r))
     left2, right2 = to_left_right(ad_head, ad_tail, "tile")
-    adj_ext = widen(left2.reshape(4, az, w, ay), ad, right2.reshape(4, az, w, ay))
-
-    h_all, z_all, p_all, q_last = run_forward(src_wave[0], state, full_ext, source_mask, ax)
+
+    h_all, z_all, p_all, q_last = run_forward(src_wave[0], fs, st_l, st_r, full, cf_halo, source_mask)
     receivers = rec_cells[0]
     records = jnp.stack([p_all[n].reshape(-1)[receivers] for n in range(steps)]) - observed[0]
 
@@ -275,7 +285,7 @@
         vals = jnp.concatenate([records[step], left3[step], right3[step]])
         parts.append(jnp.stack(exact_parts(jnp.where(pick_lane, vals[:, None], 0.0))))
     rec_rows = (rec_all // ay)[None, :]
-    acc, fin = run_adjoint(adj_ext, full_ext, h_all, z_all, rec_rows, jnp.stack(parts))
+    acc, fin = run_adjoint(ad, left2.reshape(4, az, w, ay), right2.reshape(4, az, w, ay), full, cf_halo, h_all, z_all, rec_rows, jnp.stack(parts))
 
     n_shot = lax.axis_size("shot")
     n_y = n_shot // 2

time: 223 us -> 211 us (0.946)
  other arithmetic: 24.2 us -> 13.6 us
  local copies, waits for them, and re-layouts: 38.8 us -> 33.2 us
  waiting for transfers between devices: 40.5 us -> 45 us
    concatenate x2 -> x0, other arithmetic: 10.6 us -> none  [widen(): return jnp.concatenate([lo, mid, hi], axis=-2)]
    unnamed x20 -> x12, local copies, waits for them, and re-layouts: 5.91 us -> 1.21 us
    ppermute x3, waiting for transfers between devices: 15 us -> 19.3 us  [to_left_right(): from_left = lax.ppermute(tail, axis, [(i, i + 1) for i in range(count - 1)])]
  transfers between devices with their start and end apart: 9 -> 9, of which waited for: 4 -> 5; matrix products, arithmetic and copies ran while one was open for 13% -> 8% of each run, Pallas kernels for 0% -> 0%
where the time goes in v2:
time: 211 us; the launch traced here: 210 us
  Pallas kernels  73.8 us (35%)
  waiting for transfers between devices  45 us (21%)
  local copies, waits for them, and re-layouts  33.2 us (16%)
  starting transfers between devices  19.8 us (9%)
  between operations  16.6 us (8%)
  other arithmetic  13.6 us (6%)
  blocking collectives  8 us (4%)
    pallas_call x1, Pallas kernels, run_adjoint(): pl.pallas_call(adjoint_kernel, out_shape=(jax.ShapeDtypeStruct((3, az, ax...  43.7 us
    pallas_call x1, Pallas kernels, run_forward(): pl.pallas_call(forward_kernel, out_shape=(loc, loc, loc, jax.ShapeDtypeSt...  30 us
    ppermute x3, waiting for transfers between devices, to_left_right(): from_left = lax.ppermute(tail, axis, [(i, i + 1) for i in range(count - 1)])  19.3 us
    ppermute x1, waiting for transfers between devices, per_device(): partial = lax.ppermute(partial, 'shot', ring)  17.1 us
    ppermute x3, starting transfers between devices, to_left_right(): from_left = lax.ppermute(tail, axis, [(i, i + 1) for i in range(count - 1)])  14.6 us
    gather x6, local copies, waits for them, and re-layouts, per_device(): p_all[n].reshape(-1)[receivers]  10.5 us
    all_gather x1, blocking collectives, per_device(): lax.all_gather(jnp.concatenate([cf_l, cf_r], axis=2), 'shot', axis=1, til...  8 us
    slice x1, local copies, waits for them, and re-layouts, per_device(): p_all[n].reshape(-1)[receivers]  5.27 us
  transfers between devices with their start and end apart: 9, of which 5 were waited for; matrix products, arithmetic and copies ran while one was open for 8% of the time, Pallas kernels for 0%

profile of v2, /device:TPU:0, one launch (start us, length us, event | category | flops | bytes accessed | tf_op | source)
XLA Modules:
  0.0 210.0 jit_solution(12735699871309858935)
XLA Ops:
  8.6 1.4 fusion.46
  10.4 5.7 %collective-permute-start = (f32[913,128]{1,0:T(8,128)S(1)}, f32[913,128]{1,0:T(8,128)}, u32[]{:S(2)}, u32[]{:S(2)}) collective-permute-start(f32[913,128]{1,0:T(8,128)S(1)} %get-tuple-element.75), channel_id=1, source_target_pairs={{0,1},{1,2},{2,3},{3,4},{4,5},{5,6},{6,7},{8,9},{9,10},{10,11},{11... | collective-permute-start | bytes 1402376 | tf_op jit(solution)/shard_map/ppermute | solution.py:203
  16.1 1.3 collective-permute-start.1
  17.4 1.4 fusion.47
  19.0 16.4 %collective-permute-done = f32[913,128]{1,0:T(8,128)} collective-permute-done((f32[913,128]{1,0:T(8,128)S(1)}, f32[913,128]{1,0:T(8,128)}, u32[]{:S(2)}, u32[]{:S(2)}) %collective-permute-start) | collective-permute-done | bytes 467488 | tf_op jit(solution)/shard_map/ppermute | solution.py:203
  35.4 1.2 slice.197
  37.3 1.2 slice.198
  39.2 1.0 slice.192
  40.3 0.8 reshape.1253.sl_ref
  41.1 1.0 slice.194
  42.1 0.8 reshape.1256.sr_ref
  43.0 4.5 %collective-permute-start.2 = (f32[768,128]{1,0:T(8,128)S(1)}, f32[768,128]{1,0:T(8,128)S(1)}, u32[]{:S(2)}, u32[]{:S(2)}) collective-permute-start(f32[768,128]{1,0:T(8,128)S(1)} %reshape.1250), channel_id=1, source_target_pairs={{0,1},{1,2},{2,3},{3,4},{4,5},{5,6},{6,7},{8,9},{9,10},{10,11},{11... | collective-permute-start | bytes 1179656 | tf_op jit(solution)/shard_map/ppermute | solution.py:203
  47.5 1.3 collective-permute-start.3
  48.9 0.9 slice.195
  49.8 0.9 slice.196
  50.7 1.7 scatter_custom_fusion
  52.5 8.0 %all_gather.7.ch_ref = f32[3,16,24,128]{3,2,1,0:T(8,128)} all-gather(f32[3,4,24,128]{3,2,1,0:T(8,128)S(1)} %pad_maximum_fusion.1), channel_id=1, replica_groups=mesh['shot'=4,'tile'=8] {'shot'}, dimensions={1}, use_global_device_ids=true | all-gather | bytes 737280 | tf_op jit(solution)/shard_map/all_gather | solution.py:245
  60.5 2.9 %collective-permute-done.2 = f32[768,128]{1,0:T(8,128)S(1)} collective-permute-done((f32[768,128]{1,0:T(8,128)S(1)}, f32[768,128]{1,0:T(8,128)S(1)}, u32[]{:S(2)}, u32[]{:S(2)}) %collective-permute-start.2) | collective-permute-done | bytes 393248 | tf_op jit(solution)/shard_map/ppermute | solution.py:203
  63.4 0.8 reshape.1257.al_ref
  64.2 0.8 reshape.1258.ar_ref
  65.1 30.0 %shard_map.94 = (f32[6,16,128,128]{3,2,1,0:T(8,128)}, f32[6,16,128,128]{3,2,1,0:T(8,128)}, f32[6,16,128,128]{3,2,1,0:T(8,128)}, f32[16,128,128]{2,1,0:T(8,128)}) custom-call(f32[6]{0:T(128)} %bitcast.183, f32[4,16,128,128]{3,2,1,0:T(8,128)} %bitcast.164, f32[4,16,12,128]{3,2,1,0:T(8,128)} %reshape.1253.sl_ref, f32[4,16,12,128]{3,2,1,0:T(8,128)} %reshape.1256.sr_ref, ...), custom_call_target="tpu_custom_call" | custom-call | tf_op jit(solution)/shard_map/pallas_call | solution.py:172
  95.1 5.3 %fusion.45 = (f32[1,16,128,128]{3,2,1,0:T(8,128)S(1)}, f32[1,16,128,128]{3,2,1,0:T(8,128)S(1)}, f32[1,16,128,128]{3,2,1,0:T(8,128)}, f32[1,16,128,128]{3,2,1,0:T...) fusion(f32[6,16,128,128]{3,2,1,0:T(8,128)} %get-tuple-element.19), kind=kLoop, calls=%fused_computation.215 | loop fusion | bytes 12582912 | tf_op jit(solution)/shard_map/slice | solution.py:269
  100.4 2.0 gather_fusion
  102.4 2.0 gather_fusion.1
  104.4 2.1 gather_fusion.2
  106.5 2.1 gather_fusion.3
  108.6 1.1 gather_fusion.4
  109.7 1.1 gather_fusion.5
  110.9 4.4 %collective-permute-start.4 = (f32[7,128]{1,0:T(8,128)S(1)}, f32[7,128]{1,0:T(8,128)S(1)}, u32[]{:S(2)}, u32[]{:S(2)}) collective-permute-start(f32[7,128]{1,0:T(8,128)S(1)} %pad_maximum_fusion.2), channel_id=1, source_target_pairs={{0,1},{1,2},{2,3},{3,4},{4,5},{5,6},{6,7},{8,9},{9,10},{10,11},{11... | collective-permute-start | bytes 10760 | tf_op jit(solution)/shard_map/ppermute | solution.py:203
  115.3 1.3 collective-permute-start.5
  116.6 4.2 %collective-permute-done.5 = f32[7,128]{1,0:T(8,128)S(1)} collective-permute-done((f32[7,128]{1,0:T(8,128)S(1)}, f32[7,128]{1,0:T(8,128)S(1)}, u32[]{:S(2)}, u32[]{:S(2)}) %collective-permute-start.5) | collective-permute-done | bytes 3616 | tf_op jit(solution)/shard_map/ppermute | solution.py:204
  121.5 0.7 fusion.2
  122.9 0.7 fusion.3
  123.6 0.7 fusion.4
  124.4 0.7 fusion.5
  125.1 0.7 fusion.6
  125.8 0.7 fusion.7.m_ref
  126.6 43.7 %shard_map.95 = (f32[3,16,128,128]{3,2,1,0:T(8,128)}, f32[2,16,128,128]{3,2,1,0:T(8,128)}) custom-call(f32[4,16,128,128]{3,2,1,0:T(8,128)} %bitcast.166, f32[4,16,12,128]{3,2,1,0:T(8,128)} %reshape.1257.al_ref, f32[4,16,12,128]{3,2,1,0:T(8,128)} %reshape.1258.ar_ref, f32[3,16,128,128]{3,2,1,0:T(8,128)} %all-gather.2.cloned.1.call-done.co_ref, ...), custom_call_target="tpu_custom_call" | custom-call | tf_op jit(solution)/shard_map/pallas_call | solution.py:141
  170.3 2.7 %dynamic-slice_bitcast_fusion = f32[3,2,4,128,128]{4,3,2,1,0:T(8,128)} fusion(f32[3,2,2,4,128,128]{5,4,3,2,1,0:T(8,128)} %bitcast.169, s32[]{:T(128)S(6)} %select_n.483), kind=kLoop, calls=%fused_computation.9 | loop fusion | bytes 3145732 | tf_op jit(solution)/shard_map/jit(dynamic_index_in_dim)/squeeze | solution.py:297
  173.0 3.7 %collective-permute-done.6 = f32[3,2,4,128,128]{4,3,2,1,0:T(8,128)} collective-permute-done((f32[3,2,4,128,128]{4,3,2,1,0:T(8,128)}, f32[3,2,4,128,128]{4,3,2,1,0:T(8,128)}, u32[]{:S(2)}, u32[]{:S(2)}) %collective-permute-start.6) | collective-permute-done | bytes 1572896 | tf_op jit(solution)/shard_map/ppermute | solution.py:298
  176.8 2.1 bitcast_add_fusion
  178.8 1.2 copy-done
  180.0 0.9 dynamic-slice_bitcast_fusion.1
  180.9 1.3 collective-permute-start.7
  182.3 1.5 maximum_bitcast_fusion
  183.8 17.1 %collective-permute-done.7 = f32[3,4,128,128]{3,2,1,0:T(8,128)} collective-permute-done((f32[3,4,128,128]{3,2,1,0:T(8,128)}, f32[3,4,128,128]{3,2,1,0:T(8,128)}, u32[]{:S(2)}, u32[]{:S(2)}) %collective-permute-start.7) | collective-permute-done | bytes 786464 | tf_op jit(solution)/shard_map/ppermute | solution.py:303
  200.9 1.3 bitcast_add_fusion.1
  202.2 0.9 pad_maximum_fusion
  (53 shorter events, 2.8 us)
Async XLA Ops:
  7.2 57.9 %all-gather.2.cloned.1.call-start = ((), (), s32[]{:S(2)}) async-start(), calls=%async_computation | async-start | bytes 3932160 | tf_op jit(solution)/shard_map/all_gather | solution.py:218
  8.5 1.5 copy-start.2
  10.0 7.4 %copy-start.5 = (s32[1,128]{1,0:T(1,128)S(1)}, s32[1,128]{1,0:T(1,128)}, u32[]{:S(2)}) copy-start(s32[1,128]{1,0:T(1,128)} %param.12) | copy-start | bytes 1540
  10.4 25.0 %collective-permute-start = (f32[913,128]{1,0:T(8,128)S(1)}, f32[913,128]{1,0:T(8,128)}, u32[]{:S(2)}, u32[]{:S(2)}) collective-permute-start(f32[913,128]{1,0:T(8,128)S(1)} %get-tuple-element.75), channel_id=1, source_target_pairs={{0,1},{1,2},{2,3},{3,4},{4,5},{5,6},{6,7},{8,9},{9,10},{10,11},{11... | collective-permute-start | bytes 1402376 | tf_op jit(solution)/shard_map/ppermute | solution.py:203
  16.1 21.2 %collective-permute-start.1 = (f32[913,128]{1,0:T(8,128)S(1)}, f32[913,128]{1,0:T(8,128)}, u32[]{:S(2)}, u32[]{:S(2)}) collective-permute-start(f32[913,128]{1,0:T(8,128)S(1)} %get-tuple-element.74), channel_id=1, source_target_pairs={{1,0},{2,1},{3,2},{4,3},{5,4},{6,5},{7,6},{9,8},{10,9},{11,10},{12... | collective-permute-start | bytes 1402376 | tf_op jit(solution)/shard_map/ppermute | solution.py:204
  43.0 20.4 %collective-permute-start.2 = (f32[768,128]{1,0:T(8,128)S(1)}, f32[768,128]{1,0:T(8,128)S(1)}, u32[]{:S(2)}, u32[]{:S(2)}) collective-permute-start(f32[768,128]{1,0:T(8,128)S(1)} %reshape.1250), channel_id=1, source_target_pairs={{0,1},{1,2},{2,3},{3,4},{4,5},{5,6},{6,7},{8,9},{9,10},{10,11},{11... | collective-permute-start | bytes 1179656 | tf_op jit(solution)/shard_map/ppermute | solution.py:203
  47.5 16.8 %collective-permute-start.3 = (f32[768,128]{1,0:T(8,128)S(1)}, f32[768,128]{1,0:T(8,128)S(1)}, u32[]{:S(2)}, u32[]{:S(2)}) collective-permute-start(f32[768,128]{1,0:T(8,128)S(1)} %reshape.1249), channel_id=1, source_target_pairs={{1,0},{2,1},{3,2},{4,3},{5,4},{6,5},{7,6},{9,8},{10,9},{11,10},{12... | collective-permute-start | bytes 1179656 | tf_op jit(solution)/shard_map/ppermute | solution.py:204
  100.4 10.5 %copy-start.4 = (f32[1,6,128]{2,0,1:T(1,128)S(1)}, f32[1,6,128]{2,0,1:T(1,128)}, u32[]{:S(2)}) copy-start(f32[1,6,128]{2,0,1:T(1,128)} %param.13) | copy-start | bytes 9220
  110.9 9.9 %collective-permute-start.4 = (f32[7,128]{1,0:T(8,128)S(1)}, f32[7,128]{1,0:T(8,128)S(1)}, u32[]{:S(2)}, u32[]{:S(2)}) collective-permute-start(f32[7,128]{1,0:T(8,128)S(1)} %pad_maximum_fusion.2), channel_id=1, source_target_pairs={{0,1},{1,2},{2,3},{3,4},{4,5},{5,6},{6,7},{8,9},{9,10},{10,11},{11... | collective-permute-start | bytes 10760 | tf_op jit(solution)/shard_map/ppermute | solution.py:203
  115.3 5.5 %collective-permute-start.5 = (f32[7,128]{1,0:T(8,128)S(1)}, f32[7,128]{1,0:T(8,128)S(1)}, u32[]{:S(2)}, u32[]{:S(2)}) collective-permute-start(f32[7,128]{1,0:T(8,128)S(1)} %pad_maximum_fusion.2), channel_id=1, source_target_pairs={{1,0},{2,1},{3,2},{4,3},{5,4},{6,5},{7,6},{9,8},{10,9},{11,10},{12... | collective-permute-start | bytes 10760 | tf_op jit(solution)/shard_map/ppermute | solution.py:204
  173.0 3.8 %collective-permute-start.6 = (f32[3,2,4,128,128]{4,3,2,1,0:T(8,128)}, f32[3,2,4,128,128]{4,3,2,1,0:T(8,128)}, u32[]{:S(2)}, u32[]{:S(2)}) collective-permute-start(f32[3,2,4,128,128]{4,3,2,1,0:T(8,128)} %dynamic-slice_bitcast_fusion), channel_id=1, source_target_pairs={{0,8},{8,0},{16,24},{24,16},{1,9},{9,1},{17,25},{25,17},{2,10},{10... | collective-permute-start | bytes 4718600 | tf_op jit(solution)/shard_map/ppermute | solution.py:298
  178.8 1.2 copy-start
  180.0 2.2 %copy-start.3 = (f32[16,128,128]{2,1,0:T(8,128)S(1)}, f32[16,128,128]{2,1,0:T(8,128)}, u32[]{:S(2)}) copy-start(f32[16,128,128]{2,1,0:T(8,128)} %get-tuple-element.21) | copy-start | bytes 3145732
  180.9 19.9 %collective-permute-start.7 = (f32[3,4,128,128]{3,2,1,0:T(8,128)}, f32[3,4,128,128]{3,2,1,0:T(8,128)}, u32[]{:S(2)}, u32[]{:S(2)}) collective-permute-start(f32[3,4,128,128]{3,2,1,0:T(8,128)} %dynamic-slice_bitcast_fusion.1), channel_id=1, source_target_pairs={{0,16},{8,24},{16,0},{24,8},{1,17},{9,25},{17,1},{25,9},{2,18},{10... | collective-permute-start | bytes 2359304 | tf_op jit(solution)/shard_map/ppermute | solution.py:303
  182.3 18.6 %copy-start.1 = (f32[3,2,4,128,128]{4,3,2,1,0:T(8,128)S(1)}, f32[3,2,4,128,128]{4,3,2,1,0:T(8,128)}, u32[]{:S(2)}) copy-start(f32[3,2,4,128,128]{4,3,2,1,0:T(8,128)} %copy-done) | copy-start | bytes 4718596
Sparse Core Ops, SparseCore 0:
  9.5 31.2 all-gather.1

commit v3 on v2

--- a/solution.py
+++ b/solution.py
@@ -23,7 +23,16 @@
     dst[..., pl.ds(at + OFF + ax, w), :] = hi
 
 
-def forward_kernel(wave_ref, fs_ref, sl_ref, sr_ref, co_ref, ch_ref, mask_ref, h_ref, z_ref, pl_ref, q_ref, pb, qb, cf_ref):
+def split3(x):
+    hi = x.astype(jnp.bfloat16)
+    rest = x - hi.astype(jnp.float32)
+    mid = rest.astype(jnp.bfloat16)
+    lo = (rest - mid.astype(jnp.float32)).astype(jnp.bfloat16)
+    return hi, mid, lo
+
+
+def forward_kernel(wave_ref, fs_ref, sl_ref, sr_ref, co_ref, ch_ref, mask_ref, rrow_ref, rlane_ref,
+                   h_ref, z_ref, rec_ref, pl_ref, q_ref, pb, qb, cf_ref, racc):
     steps = h_ref.shape[0]
     az, xd, ay = mask_ref.shape
     ax = h_ref.shape[2]
@@ -36,10 +45,12 @@
         place(buf.at[slot, 2:2 + az], fs_ref[k], sl_ref[k], sr_ref[k], PADX)
     place(cf_ref, co_ref[...], ch_ref[:, :, :w], ch_ref[:, :, w:], 0)
     lane = lax.broadcasted_iota(jnp.int32, (xd, ay), 1)
+    n_rec = rrow_ref.shape[0]
     for n in range(steps):
         cur = n % 2
         old = 1 - cur
         wv = wave_ref[n]
+        racc[...] = jnp.zeros(racc.shape, jnp.float32)
 
         def plane(d, carry):
             pc = pb[cur, d + 2, inner, :]
@@ -62,12 +73,22 @@
             qb[old, d + 2, inner, :] = qn
             h_ref[n, d] = h[OFF:OFF + ax]
             z_ref[n, d] = z[OFF:OFF + ax]
-            pl_ref[n, d] = pn[OFF:OFF + ax]
+            po = pn[OFF:OFF + ax]
+            hit = lax.broadcasted_iota(jnp.int32, (n_rec, ax), 1) + d * ax == rrow_ref[...]
+            pick = jnp.where(hit, 1.0, 0.0).astype(jnp.bfloat16)
+            got = None
+            for part in split3(po):
+                term = jnp.dot(pick, part, preferred_element_type=jnp.float32)
+                got = term if got is None else got + term
+            racc[...] = racc[...] + got
             if n == steps - 1:
                 q_ref[d] = qn[OFF:OFF + ax]
+                pl_ref[d] = po
             return carry
 
         lax.fori_loop(0, az, plane, 0)
+        sel = lax.broadcasted_iota(jnp.int32, (n_rec, ay), 1) == rlane_ref[...]
+        rec_ref[n] = jnp.where(sel, racc[...], 0.0)
 
 
 def adjoint_kernel(ad_ref, al_ref, ar_ref, co_ref, ch_ref, h_ref, z_ref, row_ref, m_ref, acc_ref, fin_ref, lb, mb, ob, fb, cf_ref):
@@ -163,21 +184,24 @@
     return hi.astype(jnp.bfloat16), mid.astype(jnp.bfloat16), lo.astype(jnp.bfloat16)
 
 
-def run_forward(wave, fs, sl, sr, co, ch, mask):
+def run_forward(wave, fs, sl, sr, co, ch, mask, rrow, rlane):
     steps = wave.shape[0]
     az, xd, ay = mask.shape
     ax = fs.shape[2]
+    n_rec = rrow.shape[0]
     vm = pl.BlockSpec(memory_space=pltpu.VMEM)
     loc = jax.ShapeDtypeStruct((steps, az, ax, ay), jnp.float32)
+    one = jax.ShapeDtypeStruct((az, ax, ay), jnp.float32)
     return pl.pallas_call(
         forward_kernel,
-        out_shape=(loc, loc, loc, jax.ShapeDtypeStruct((az, ax, ay), jnp.float32)),
-        in_specs=[pl.BlockSpec(memory_space=pltpu.SMEM)] + [vm] * 6,
-        out_specs=(vm, vm, vm, vm),
-        scratch_shapes=[pltpu.VMEM((2, az + 4, xd + 2 * PADX, ay), jnp.float32)] * 2 + [pltpu.VMEM((3, az, xd, ay), jnp.float32)],
+        out_shape=(loc, loc, jax.ShapeDtypeStruct((steps, n_rec, ay), jnp.float32), one, one),
+        in_specs=[pl.BlockSpec(memory_space=pltpu.SMEM)] + [vm] * 8,
+        out_specs=(vm, vm, vm, vm, vm),
+        scratch_shapes=[pltpu.VMEM((2, az + 4, xd + 2 * PADX, ay), jnp.float32)] * 2
+        + [pltpu.VMEM((3, az, xd, ay), jnp.float32), pltpu.VMEM((n_rec, ay), jnp.float32)],
         compiler_params=pltpu.CompilerParams(vmem_limit_bytes=62 * 1024 * 1024),
         interpret=INTERPRET,
-    )(wave, fs, sl, sr, co, ch, mask)
+    )(wave, fs, sl, sr, co, ch, mask, rrow, rlane)
 
 
 def taps(padded, size, axis):
@@ -264,9 +288,10 @@
     ad_head, ad_tail, st_l, st_r = lax.optimization_barrier((rows(ad[:, :, :w]), rows(ad[:, :, ax - w:]), st_l, st_r))
     left2, right2 = to_left_right(ad_head, ad_tail, "tile")
 
-    h_all, z_all, p_all, q_last = run_forward(src_wave[0], fs, st_l, st_r, full, cf_halo, source_mask)
     receivers = rec_cells[0]
-    records = jnp.stack([p_all[n].reshape(-1)[receivers] for n in range(steps)]) - observed[0]
+    h_all, z_all, rec_mat, p_last, q_last = run_forward(
+        src_wave[0], fs, st_l, st_r, full, cf_halo, source_mask, (receivers // ay)[:, None], (receivers % ay)[:, None])
+    records = jnp.sum(rec_mat, axis=2) - observed[0]
 
     msg = jnp.concatenate([records, receivers.astype(jnp.float32)[None]], axis=0)
     left3, right3 = to_left_right(msg, msg, "tile")
@@ -306,7 +331,7 @@
     q_h, q_x, q_z = summed[0], summed[1], summed[2]
     c, a, b = coefs[0], coefs[1], coefs[2]
     gradient = jnp.stack([a * q_h + b * q_x + q_z, c * q_h, c * q_x])
-    fwd_final = jnp.stack([p_all[steps - 1], q_last])[None]
+    fwd_final = jnp.stack([p_last, q_last])[None]
     adj_final = fin[None]
     return (gradient, fwd_final, adj_final)
 

time: 211 us -> 202 us (0.957)
  local copies, waits for them, and re-layouts: 33.2 us -> 14 us
  Pallas kernels: 73.8 us -> 84 us
  other arithmetic: 13.6 us -> 16.7 us
    gather x6 -> x0, local copies, waits for them, and re-layouts: 10.5 us -> none  [per_device(): p_all[n].reshape(-1)[receivers]]
    pallas_call x1, Pallas kernels: 30 us -> 40.3 us  [run_forward(): pl.pallas_call(forward_kernel, out_shape=(loc, loc, jax.ShapeDtypeStruct(...]
    slice x1 -> x0, local copies, waits for them, and re-layouts: 5.27 us -> none  [per_device(): p_all[n].reshape(-1)[receivers]]
where the time goes in v3:
time: 202 us
  Pallas kernels  84 us (42%)
  waiting for transfers between devices  43.3 us (21%)
  starting transfers between devices  19 us (9%)
  other arithmetic  16.7 us (8%)
  between operations  16.6 us (8%)
  local copies, waits for them, and re-layouts  14 us (7%)
  blocking collectives  8.01 us (4%)
    pallas_call x1, Pallas kernels, run_adjoint(): pl.pallas_call(adjoint_kernel, out_shape=(jax.ShapeDtypeStruct((3, az, ax...  43.7 us
    pallas_call x1, Pallas kernels, run_forward(): pl.pallas_call(forward_kernel, out_shape=(loc, loc, jax.ShapeDtypeStruct(...  40.3 us
    ppermute x3, waiting for transfers between devices, to_left_right(): from_left = lax.ppermute(tail, axis, [(i, i + 1) for i in range(count - 1)])  18.8 us
    ppermute x1, waiting for transfers between devices, per_device(): partial = lax.ppermute(partial, 'shot', ring)  15.8 us
    ppermute x3, starting transfers between devices, to_left_right(): from_left = lax.ppermute(tail, axis, [(i, i + 1) for i in range(count - 1)])  13.7 us
    all_gather x1, blocking collectives, per_device(): lax.all_gather(jnp.concatenate([cf_l, cf_r], axis=2), 'shot', axis=1, til...  8.01 us
    ppermute x3, waiting for transfers between devices, to_left_right(): lax.ppermute(head, axis, [(i + 1, i) for i in range(count - 1)])  4.51 us
  transfers between devices with their start and end apart: 9, of which 5 were waited for; matrix products, arithmetic and copies ran while one was open for 8% of the time, Pallas kernels for 0%

profile of v3, /device:TPU:0, one launch (start us, length us, event | category | flops | bytes accessed | tf_op | source)
XLA Modules:
  0.0 201.7 jit_solution(4233391442943714883)
XLA Ops:
  7.2 0.7 all-gather.2.cloned.1.call-update
  8.6 1.4 fusion.46
  10.2 0.2 maximum_maximum_fusion.1
  10.4 4.9 %collective-permute-start = (f32[913,128]{1,0:T(8,128)S(1)}, f32[913,128]{1,0:T(8,128)S(1)}, u32[]{:S(2)}, u32[]{:S(2)}) collective-permute-start(f32[913,128]{1,0:T(8,128)S(1)} %get-tuple-element.73), channel_id=1, source_target_pairs={{0,1},{1,2},{2,3},{3,4},{4,5},{5,6},{6,7},{8,9},{9,10},{10,11},{11... | collective-permute-start | bytes 1402376 | tf_op jit(solution)/shard_map/ppermute | solution.py:227
  15.3 1.3 collective-permute-start.1
  16.6 1.3 fusion.47
  18.0 0.8 reshape.1323
  18.8 0.8 reshape.1324
  19.5 0.1 copy.14
  19.7 0.7 add_select_fusion
  20.4 14.9 %collective-permute-done = f32[913,128]{1,0:T(8,128)S(1)} collective-permute-done((f32[913,128]{1,0:T(8,128)S(1)}, f32[913,128]{1,0:T(8,128)S(1)}, u32[]{:S(2)}, u32[]{:S(2)}) %collective-permute-start) | collective-permute-done | bytes 467488 | tf_op jit(solution)/shard_map/ppermute | solution.py:227
  35.4 0.5 slice.160
  36.6 1.2 slice.161
  38.6 0.8 reshape.1327.sl_ref
  39.4 1.0 slice.157
  40.5 0.8 reshape.1330.sr_ref
  41.3 4.4 %collective-permute-start.2 = (f32[768,128]{1,0:T(8,128)S(1)}, f32[768,128]{1,0:T(8,128)S(1)}, u32[]{:S(2)}, u32[]{:S(2)}) collective-permute-start(f32[768,128]{1,0:T(8,128)S(1)} %copy-done.3), channel_id=1, source_target_pairs={{0,1},{1,2},{2,3},{3,4},{4,5},{5,6},{6,7},{8,9},{9,10},{10,11},{11... | collective-permute-start | bytes 1179656 | tf_op jit(solution)/shard_map/ppermute | solution.py:227
  45.7 1.3 collective-permute-start.3
  47.2 0.9 slice.159
  48.1 1.7 scatter_custom_fusion
  49.8 8.0 %all_gather.7.ch_ref = f32[3,16,24,128]{3,2,1,0:T(8,128)} all-gather(f32[3,4,24,128]{3,2,1,0:T(8,128)S(1)} %pad_maximum_fusion.1), channel_id=1, replica_groups=mesh['shot'=4,'tile'=8] {'shot'}, dimensions={1}, use_global_device_ids=true | all-gather | bytes 737280 | tf_op jit(solution)/shard_map/all_gather | solution.py:269
  57.9 3.9 %collective-permute-done.2 = f32[768,128]{1,0:T(8,128)S(1)} collective-permute-done((f32[768,128]{1,0:T(8,128)S(1)}, f32[768,128]{1,0:T(8,128)S(1)}, u32[]{:S(2)}, u32[]{:S(2)}) %collective-permute-start.2) | collective-permute-done | bytes 393248 | tf_op jit(solution)/shard_map/ppermute | solution.py:227
  61.7 0.8 reshape.1331.al_ref
  62.6 0.8 reshape.1332.ar_ref
  63.4 40.3 %shard_map.94 = (f32[6,16,128,128]{3,2,1,0:T(8,128)}, f32[6,16,128,128]{3,2,1,0:T(8,128)}, f32[6,128,128]{2,1,0:T(8,128)}, f32[16,128,128]{2,1,0:T(8,128)}, f32[16,128,128]{2,1,0:T(8,128)}) custom-call(f32[6]{0:T(128)} %bitcast.159, f32[4,16,128,128]{3,2,1,0:T(8,128)} %bitcast.152, f32[4,16,12,128]{3,2,1,0:T(8,128)} %reshape.1327.sl_ref, ...), custom_call_target="tpu_custom_call" | custom-call | tf_op jit(solution)/shard_map/pallas_call | solution.py:195
  103.7 1.2 reduce_sum.9
  105.0 4.4 %collective-permute-start.4 = (f32[7,128]{1,0:T(8,128)S(1)}, f32[7,128]{1,0:T(8,128)S(1)}, u32[]{:S(2)}, u32[]{:S(2)}) collective-permute-start(f32[7,128]{1,0:T(8,128)S(1)} %pad_maximum_fusion.2), channel_id=1, source_target_pairs={{0,1},{1,2},{2,3},{3,4},{4,5},{5,6},{6,7},{8,9},{9,10},{10,11},{11... | collective-permute-start | bytes 10760 | tf_op jit(solution)/shard_map/ppermute | solution.py:227
  109.4 1.3 collective-permute-start.5
  110.7 4.5 %collective-permute-done.5 = f32[7,128]{1,0:T(8,128)S(1)} collective-permute-done((f32[7,128]{1,0:T(8,128)S(1)}, f32[7,128]{1,0:T(8,128)S(1)}, u32[]{:S(2)}, u32[]{:S(2)}) %collective-permute-start.5) | collective-permute-done | bytes 3616 | tf_op jit(solution)/shard_map/ppermute | solution.py:228
  115.3 0.5 reduce-precision_convert_fusion.1
  115.9 0.7 fusion.2
  116.7 0.6 and_select_fusion.row_ref
  117.3 0.7 fusion.3
  118.0 0.7 fusion.4
  118.7 0.7 fusion.5
  119.5 0.7 fusion.6
  120.2 0.7 fusion.7.m_ref
  120.9 43.7 %shard_map.95 = (f32[3,16,128,128]{3,2,1,0:T(8,128)}, f32[2,16,128,128]{3,2,1,0:T(8,128)}) custom-call(f32[4,16,128,128]{3,2,1,0:T(8,128)} %bitcast.150, f32[4,16,12,128]{3,2,1,0:T(8,128)} %reshape.1331.al_ref, f32[4,16,12,128]{3,2,1,0:T(8,128)} %reshape.1332.ar_ref, f32[3,16,128,128]{3,2,1,0:T(8,128)} %all-gather.2.cloned.1.call-done.co_ref, ...), custom_call_target="tpu_custom_call" | custom-call | tf_op jit(solution)/shard_map/pallas_call | solution.py:162
  164.6 1.5 dynamic-slice_bitcast_fusion
  166.3 3.5 %collective-permute-done.6 = f32[3,2,4,128,128]{4,3,2,1,0:T(8,128)} collective-permute-done((f32[3,2,4,128,128]{4,3,2,1,0:T(8,128)S(1)}, f32[3,2,4,128,128]{4,3,2,1,0:T(8,128)}, u32[]{:S(2)}, u32[]{:S(2)}) %collective-permute-start.6) | collective-permute-done | bytes 1572896 | tf_op jit(solution)/shard_map/ppermute | solution.py:323
  169.7 2.1 %bitcast_add_fusion = f32[3,2,4,128,128]{4,3,2,1,0:T(8,128)S(1)} fusion(f32[3,2,4,128,128]{4,3,2,1,0:T(8,128)} %collective-permute-done.6, f32[3,2,2,4,128,128]{5,4,3,2,1,0:T(8,128)} %bitcast.155, s32[]{:T(128)S(6)} %select_n.489), kind=kLoop, calls=%fused_computation.2 | loop fusion | flops 393216 | bytes 4718596 | tf_op jit(solution)/shard_map/add | solution.py:324
  171.8 0.9 dynamic-slice_bitcast_fusion.1
  172.7 1.3 collective-permute-start.7
  174.1 2.7 %maximum_bitcast_fusion = f32[1,2,16,128,128]{4,3,2,1,0:T(8,128)} fusion(f32[1,16,128,128]{3,2,1,0:T(8,128)} %bitcast.157, f32[1,16,128,128]{3,2,1,0:T(8,128)S(1)} %bitcast.156), kind=kLoop, calls=%fused_computation.1 | loop fusion | flops 524288 | bytes 4194304 | tf_op jit(solution)/shard_map/broadcast_in_dim | solution.py:334
  176.8 15.8 %collective-permute-done.7 = f32[3,4,128,128]{3,2,1,0:T(8,128)} collective-permute-done((f32[3,4,128,128]{3,2,1,0:T(8,128)}, f32[3,4,128,128]{3,2,1,0:T(8,128)}, u32[]{:S(2)}, u32[]{:S(2)}) %collective-permute-start.7) | collective-permute-done | bytes 786464 | tf_op jit(solution)/shard_map/ppermute | solution.py:328
  192.6 1.2 bitcast_add_fusion.1
  193.9 0.1 slice_add_fusion
  194.0 0.9 pad_maximum_fusion
  (46 shorter events, 0.8 us)
Async XLA Ops:
  7.2 56.2 %all-gather.2.cloned.1.call-start = ((), (), s32[]{:S(2)}) async-start(), calls=%async_computation | async-start | bytes 3932160 | tf_op jit(solution)/shard_map/all_gather | solution.py:242
  8.5 1.5 copy-start
  10.2 7.7 %copy-start.5 = (s32[1,128]{1,0:T(1,128)S(1)}, s32[1,128]{1,0:T(1,128)}, u32[]{:S(2)}) copy-start(s32[1,128]{1,0:T(1,128)} %param.12) | copy-start | bytes 1540
  10.4 25.0 %collective-permute-start = (f32[913,128]{1,0:T(8,128)S(1)}, f32[913,128]{1,0:T(8,128)S(1)}, u32[]{:S(2)}, u32[]{:S(2)}) collective-permute-start(f32[913,128]{1,0:T(8,128)S(1)} %get-tuple-element.73), channel_id=1, source_target_pairs={{0,1},{1,2},{2,3},{3,4},{4,5},{5,6},{6,7},{8,9},{9,10},{10,11},{11... | collective-permute-start | bytes 1402376 | tf_op jit(solution)/shard_map/ppermute | solution.py:227
  15.3 21.3 %collective-permute-start.1 = (f32[913,128]{1,0:T(8,128)S(1)}, f32[913,128]{1,0:T(8,128)}, u32[]{:S(2)}, u32[]{:S(2)}) collective-permute-start(f32[913,128]{1,0:T(8,128)S(1)} %get-tuple-element.72), channel_id=1, source_target_pairs={{1,0},{2,1},{3,2},{4,3},{5,4},{6,5},{7,6},{9,8},{10,9},{11,10},{12... | collective-permute-start | bytes 1402376 | tf_op jit(solution)/shard_map/ppermute | solution.py:228
  38.4 2.9 %copy-start.3 = (f32[768,128]{1,0:T(8,128)S(1)}, f32[768,128]{1,0:T(8,128)}, u32[]{:S(2)}) copy-start(f32[768,128]{1,0:T(8,128)} %reshape.1324) | copy-start | bytes 1179652
  38.4 7.3 %copy-start.2 = (f32[768,128]{1,0:T(8,128)S(1)}, f32[768,128]{1,0:T(8,128)}, u32[]{:S(2)}) copy-start(f32[768,128]{1,0:T(8,128)} %reshape.1323) | copy-start | bytes 1179652
  41.3 20.4 %collective-permute-start.2 = (f32[768,128]{1,0:T(8,128)S(1)}, f32[768,128]{1,0:T(8,128)S(1)}, u32[]{:S(2)}, u32[]{:S(2)}) collective-permute-start(f32[768,128]{1,0:T(8,128)S(1)} %copy-done.3), channel_id=1, source_target_pairs={{0,1},{1,2},{2,3},{3,4},{4,5},{5,6},{6,7},{8,9},{9,10},{10,11},{11... | collective-permute-start | bytes 1179656 | tf_op jit(solution)/shard_map/ppermute | solution.py:227
  45.7 16.8 %collective-permute-start.3 = (f32[768,128]{1,0:T(8,128)S(1)}, f32[768,128]{1,0:T(8,128)S(1)}, u32[]{:S(2)}, u32[]{:S(2)}) collective-permute-start(f32[768,128]{1,0:T(8,128)S(1)} %copy-done.2), channel_id=1, source_target_pairs={{1,0},{2,1},{3,2},{4,3},{5,4},{6,5},{7,6},{9,8},{10,9},{11,10},{12... | collective-permute-start | bytes 1179656 | tf_op jit(solution)/shard_map/ppermute | solution.py:228
  63.4 41.5 %copy-start.4 = (f32[1,6,128]{2,0,1:T(1,128)S(1)}, f32[1,6,128]{2,0,1:T(1,128)}, u32[]{:S(2)}) copy-start(f32[1,6,128]{2,0,1:T(1,128)} %param.13) | copy-start | bytes 9220
  105.0 10.2 %collective-permute-start.4 = (f32[7,128]{1,0:T(8,128)S(1)}, f32[7,128]{1,0:T(8,128)S(1)}, u32[]{:S(2)}, u32[]{:S(2)}) collective-permute-start(f32[7,128]{1,0:T(8,128)S(1)} %pad_maximum_fusion.2), channel_id=1, source_target_pairs={{0,1},{1,2},{2,3},{3,4},{4,5},{5,6},{6,7},{8,9},{9,10},{10,11},{11... | collective-permute-start | bytes 10760 | tf_op jit(solution)/shard_map/ppermute | solution.py:227
  109.4 5.8 %collective-permute-start.5 = (f32[7,128]{1,0:T(8,128)S(1)}, f32[7,128]{1,0:T(8,128)S(1)}, u32[]{:S(2)}, u32[]{:S(2)}) collective-permute-start(f32[7,128]{1,0:T(8,128)S(1)} %pad_maximum_fusion.2), channel_id=1, source_target_pairs={{1,0},{2,1},{3,2},{4,3},{5,4},{6,5},{7,6},{9,8},{10,9},{11,10},{12... | collective-permute-start | bytes 10760 | tf_op jit(solution)/shard_map/ppermute | solution.py:228
  166.1 3.6 %collective-permute-start.6 = (f32[3,2,4,128,128]{4,3,2,1,0:T(8,128)S(1)}, f32[3,2,4,128,128]{4,3,2,1,0:T(8,128)}, u32[]{:S(2)}, u32[]{:S(2)}) collective-permute-start(f32[3,2,4,128,128]{4,3,2,1,0:T(8,128)S(1)} %dynamic-slice_bitcast_fusion), channel_id=1, source_target_pairs={{0,8},{8,0},{16,24},{24,16},{1,9},{9,1},{17,25},{25,17},{2,10},{10... | collective-permute-start | bytes 4718600 | tf_op jit(solution)/shard_map/ppermute | solution.py:323
  171.8 2.3 %copy-start.1 = (f32[16,128,128]{2,1,0:T(8,128)S(1)}, f32[16,128,128]{2,1,0:T(8,128)}, u32[]{:S(2)}) copy-start(f32[16,128,128]{2,1,0:T(8,128)} %get-tuple-element.22) | copy-start | bytes 3145732
  172.7 19.9 %collective-permute-start.7 = (f32[3,4,128,128]{3,2,1,0:T(8,128)}, f32[3,4,128,128]{3,2,1,0:T(8,128)}, u32[]{:S(2)}, u32[]{:S(2)}) collective-permute-start(f32[3,4,128,128]{3,2,1,0:T(8,128)} %dynamic-slice_bitcast_fusion.1), channel_id=1, source_target_pairs={{0,16},{8,24},{16,0},{24,8},{1,17},{9,25},{17,1},{25,9},{2,18},{10... | collective-permute-start | bytes 2359304 | tf_op jit(solution)/shard_map/ppermute | solution.py:328
Sparse Core Ops, SparseCore 0:
  9.5 31.2 all-gather.1

commit v4 on v3

--- a/solution.py
+++ b/solution.py
@@ -25,10 +25,8 @@
 
 def split3(x):
     hi = x.astype(jnp.bfloat16)
-    rest = x - hi.astype(jnp.float32)
-    mid = rest.astype(jnp.bfloat16)
-    lo = (rest - mid.astype(jnp.float32)).astype(jnp.bfloat16)
-    return hi, mid, lo
+    lo = (x - hi.astype(jnp.float32)).astype(jnp.bfloat16)
+    return hi, lo
 
 
 def forward_kernel(wave_ref, fs_ref, sl_ref, sr_ref, co_ref, ch_ref, mask_ref, rrow_ref, rlane_ref,
@@ -135,7 +133,6 @@
             pick = jnp.where(hit, 1.0, 0.0).astype(jnp.bfloat16)
             e = jnp.dot(pick, m_ref[s, 0], preferred_element_type=jnp.float32)
             e = e + jnp.dot(pick, m_ref[s, 1], preferred_element_type=jnp.float32)
-            e = e + jnp.dot(pick, m_ref[s, 2], preferred_element_type=jnp.float32)
             ln = e + 2.0 * lc + hf - lb[old, d]
             mn = 2.0 * mc + d2(ob[d], ob[d + 1], ob[d + 2], ob[d + 3], ob[d + 4]) - mb[old, d]
             lb[old, d] = ln
@@ -179,9 +176,8 @@
 def exact_parts(x):
     hi = lax.reduce_precision(x, exponent_bits=8, mantissa_bits=7)
     rest = x - hi
-    mid = lax.reduce_precision(rest, exponent_bits=8, mantissa_bits=7)
-    lo = lax.reduce_precision(rest - mid, exponent_bits=8, mantissa_bits=7)
-    return hi.astype(jnp.bfloat16), mid.astype(jnp.bfloat16), lo.astype(jnp.bfloat16)
+    lo = lax.reduce_precision(rest, exponent_bits=8, mantissa_bits=7)
+    return hi.astype(jnp.bfloat16), lo.astype(jnp.bfloat16)
 
 
 def run_forward(wave, fs, sl, sr, co, ch, mask, rrow, rlane):

time: 202 us -> 194 us (0.960)
  Pallas kernels: 84 us -> 79.3 us
  other arithmetic: 16.7 us -> 12.5 us
    pallas_call x1, Pallas kernels: 43.7 us -> 39.9 us  [run_adjoint(): pl.pallas_call(adjoint_kernel, out_shape=(jax.ShapeDtypeStruct((3, az, ax...]
    unnamed x5, other arithmetic: 3.67 us -> 0.13 us
  transfers between devices with their start and end apart: 9 -> 9, of which waited for: 5 -> 5; matrix products, arithmetic and copies ran while one was open for 8% -> 9% of each run, Pallas kernels for 0% -> 0%
where the time goes in v4:
time: 194 us; the launch traced here: 193 us
  Pallas kernels  79.3 us (41%)
  waiting for transfers between devices  43.1 us (22%)
  starting transfers between devices  19.2 us (10%)
  between operations  16.7 us (9%)
  local copies, waits for them, and re-layouts  14.3 us (7%)
  other arithmetic  12.5 us (6%)
  blocking collectives  8.01 us (4%)
    pallas_call x1, Pallas kernels, run_adjoint(): pl.pallas_call(adjoint_kernel, out_shape=(jax.ShapeDtypeStruct((3, az, ax...  39.9 us
    pallas_call x1, Pallas kernels, run_forward(): pl.pallas_call(forward_kernel, out_shape=(loc, loc, jax.ShapeDtypeStruct(...  39.5 us
    ppermute x3, waiting for transfers between devices, to_left_right(): from_left = lax.ppermute(tail, axis, [(i, i + 1) for i in range(count - 1)])  18.8 us
    ppermute x1, waiting for transfers between devices, per_device(): partial = lax.ppermute(partial, 'shot', ring)  15.7 us
    ppermute x3, starting transfers between devices, to_left_right(): from_left = lax.ppermute(tail, axis, [(i, i + 1) for i in range(count - 1)])  13.7 us
    all_gather x1, blocking collectives, per_device(): lax.all_gather(jnp.concatenate([cf_l, cf_r], axis=2), 'shot', axis=1, til...  8.01 us
    ppermute x3, waiting for transfers between devices, to_left_right(): lax.ppermute(head, axis, [(i + 1, i) for i in range(count - 1)])  4.52 us
  transfers between devices with their start and end apart: 9, of which 5 were waited for; matrix products, arithmetic and copies ran while one was open for 9% of the time, Pallas kernels for 0%

profile of v4, /device:TPU:0, one launch (start us, length us, event | category | flops | bytes accessed | tf_op | source)
XLA Modules:
  0.0 193.1 jit_solution(7040415941223857745)
XLA Ops:
  7.2 0.0 all-gather.2.cloned.1.call-start
  7.2 0.7 all-gather.2.cloned.1.call-update
  8.6 1.4 fusion.46
  10.1 0.1 pad.56.clone
  10.2 0.2 maximum_maximum_fusion.1
  10.4 4.9 %collective-permute-start = (f32[913,128]{1,0:T(8,128)S(1)}, f32[913,128]{1,0:T(8,128)S(1)}, u32[]{:S(2)}, u32[]{:S(2)}) collective-permute-start(f32[913,128]{1,0:T(8,128)S(1)} %get-tuple-element.67), channel_id=1, source_target_pairs={{0,1},{1,2},{2,3},{3,4},{4,5},{5,6},{6,7},{8,9},{9,10},{10,11},{11... | collective-permute-start | bytes 1402376 | tf_op jit(solution)/shard_map/ppermute | solution.py:223
  15.3 1.3 collective-permute-start.1
  16.6 1.3 fusion.47
  18.0 0.8 reshape.1053
  18.8 0.8 reshape.1054
  19.5 0.1 copy.14
  19.7 0.7 add_select_fusion
  20.4 14.9 %collective-permute-done = f32[913,128]{1,0:T(8,128)S(1)} collective-permute-done((f32[913,128]{1,0:T(8,128)S(1)}, f32[913,128]{1,0:T(8,128)S(1)}, u32[]{:S(2)}, u32[]{:S(2)}) %collective-permute-start) | collective-permute-done | bytes 467488 | tf_op jit(solution)/shard_map/ppermute | solution.py:223
  35.4 0.5 slice.160
  36.6 1.2 slice.161
  38.6 0.8 reshape.1057.sl_ref
  39.4 1.0 slice.157
  40.5 0.9 reshape.1060.sr_ref
  41.3 4.4 %collective-permute-start.2 = (f32[768,128]{1,0:T(8,128)S(1)}, f32[768,128]{1,0:T(8,128)S(1)}, u32[]{:S(2)}, u32[]{:S(2)}) collective-permute-start(f32[768,128]{1,0:T(8,128)S(1)} %copy-done.4), channel_id=1, source_target_pairs={{0,1},{1,2},{2,3},{3,4},{4,5},{5,6},{6,7},{8,9},{9,10},{10,11},{11... | collective-permute-start | bytes 1179656 | tf_op jit(solution)/shard_map/ppermute | solution.py:223
  45.7 1.3 collective-permute-start.3
  47.0 0.1 add_convert_fusion
  47.1 0.1 fusion.45
  47.2 0.9 slice.159
  48.1 1.7 scatter_custom_fusion
  49.9 8.0 %all_gather.7.ch_ref = f32[3,16,24,128]{3,2,1,0:T(8,128)} all-gather(f32[3,4,24,128]{3,2,1,0:T(8,128)S(1)} %pad_maximum_fusion.1), channel_id=1, replica_groups=mesh['shot'=4,'tile'=8] {'shot'}, dimensions={1}, use_global_device_ids=true | all-gather | bytes 737280 | tf_op jit(solution)/shard_map/all_gather | solution.py:265
  57.9 3.9 %collective-permute-done.2 = f32[768,128]{1,0:T(8,128)S(1)} collective-permute-done((f32[768,128]{1,0:T(8,128)S(1)}, f32[768,128]{1,0:T(8,128)S(1)}, u32[]{:S(2)}, u32[]{:S(2)}) %collective-permute-start.2) | collective-permute-done | bytes 393248 | tf_op jit(solution)/shard_map/ppermute | solution.py:223
  61.7 0.8 reshape.1061.al_ref
  62.6 0.8 reshape.1062.ar_ref
  63.4 39.5 %shard_map.94 = (f32[6,16,128,128]{3,2,1,0:T(8,128)}, f32[6,16,128,128]{3,2,1,0:T(8,128)}, f32[6,128,128]{2,1,0:T(8,128)}, f32[16,128,128]{2,1,0:T(8,128)}, f32[16,128,128]{2,1,0:T(8,128)}) custom-call(f32[6]{0:T(128)} %bitcast.159, f32[4,16,128,128]{3,2,1,0:T(8,128)} %bitcast.152, f32[4,16,12,128]{3,2,1,0:T(8,128)} %reshape.1057.sl_ref, ...), custom_call_target="tpu_custom_call" | custom-call | tf_op jit(solution)/shard_map/pallas_call | solution.py:191
  102.9 1.2 reduce_sum.9
  104.1 4.4 %collective-permute-start.4 = (f32[7,128]{1,0:T(8,128)S(1)}, f32[7,128]{1,0:T(8,128)S(1)}, u32[]{:S(2)}, u32[]{:S(2)}) collective-permute-start(f32[7,128]{1,0:T(8,128)S(1)} %pad_maximum_fusion.2), channel_id=1, source_target_pairs={{0,1},{1,2},{2,3},{3,4},{4,5},{5,6},{6,7},{8,9},{9,10},{10,11},{11... | collective-permute-start | bytes 10760 | tf_op jit(solution)/shard_map/ppermute | solution.py:223
  108.5 1.3 collective-permute-start.5
  109.8 4.5 %collective-permute-done.5 = f32[7,128]{1,0:T(8,128)S(1)} collective-permute-done((f32[7,128]{1,0:T(8,128)S(1)}, f32[7,128]{1,0:T(8,128)S(1)}, u32[]{:S(2)}, u32[]{:S(2)}) %collective-permute-start.5) | collective-permute-done | bytes 3616 | tf_op jit(solution)/shard_map/ppermute | solution.py:224
  114.5 0.4 reduce-precision_convert_fusion
  115.2 0.7 and_select_fusion.row_ref
  115.9 0.3 copy-done.1
  116.1 39.9 %shard_map.95 = (f32[3,16,128,128]{3,2,1,0:T(8,128)}, f32[2,16,128,128]{3,2,1,0:T(8,128)}) custom-call(f32[4,16,128,128]{3,2,1,0:T(8,128)} %bitcast.150, f32[4,16,12,128]{3,2,1,0:T(8,128)} %reshape.1061.al_ref, f32[4,16,12,128]{3,2,1,0:T(8,128)} %reshape.1062.ar_ref, f32[3,16,128,128]{3,2,1,0:T(8,128)} %all-gather.2.cloned.1.call-done.co_ref, ...), custom_call_target="tpu_custom_call" | custom-call | tf_op jit(solution)/shard_map/pallas_call | solution.py:159
  156.0 1.5 dynamic-slice_bitcast_fusion
  157.5 0.1 collective-permute-start.6
  157.6 3.5 %collective-permute-done.6 = f32[3,2,4,128,128]{4,3,2,1,0:T(8,128)} collective-permute-done((f32[3,2,4,128,128]{4,3,2,1,0:T(8,128)S(1)}, f32[3,2,4,128,128]{4,3,2,1,0:T(8,128)}, u32[]{:S(2)}, u32[]{:S(2)}) %collective-permute-start.6) | collective-permute-done | bytes 1572896 | tf_op jit(solution)/shard_map/ppermute | solution.py:319
  161.1 2.1 %bitcast_add_fusion = f32[3,2,4,128,128]{4,3,2,1,0:T(8,128)S(1)} fusion(f32[3,2,4,128,128]{4,3,2,1,0:T(8,128)} %collective-permute-done.6, f32[3,2,2,4,128,128]{5,4,3,2,1,0:T(8,128)} %bitcast.155, s32[]{:T(128)S(6)} %select_n.465), kind=kLoop, calls=%fused_computation.2 | loop fusion | flops 393216 | bytes 4718596 | tf_op jit(solution)/shard_map/add | solution.py:320
  163.2 0.9 dynamic-slice_bitcast_fusion.1
  164.1 1.5 collective-permute-start.7
  165.7 2.7 %maximum_bitcast_fusion = f32[1,2,16,128,128]{4,3,2,1,0:T(8,128)} fusion(f32[1,16,128,128]{3,2,1,0:T(8,128)} %bitcast.157, f32[1,16,128,128]{3,2,1,0:T(8,128)S(1)} %bitcast.156), kind=kLoop, calls=%fused_computation.1 | loop fusion | flops 524288 | bytes 4194304 | tf_op jit(solution)/shard_map/broadcast_in_dim | solution.py:330
  168.4 15.7 %collective-permute-done.7 = f32[3,4,128,128]{3,2,1,0:T(8,128)} collective-permute-done((f32[3,4,128,128]{3,2,1,0:T(8,128)}, f32[3,4,128,128]{3,2,1,0:T(8,128)}, u32[]{:S(2)}, u32[]{:S(2)}) %collective-permute-start.7) | collective-permute-done | bytes 786464 | tf_op jit(solution)/shard_map/ppermute | solution.py:324
  184.0 1.2 bitcast_add_fusion.1
  185.3 0.1 slice_add_fusion
  185.4 0.9 pad_maximum_fusion
  (48 shorter events, 0.6 us)
Async XLA Ops:
  7.2 56.2 %all-gather.2.cloned.1.call-start = ((), (), s32[]{:S(2)}) async-start(), calls=%async_computation | async-start | bytes 3932160 | tf_op jit(solution)/shard_map/all_gather | solution.py:238
  8.5 1.5 copy-start
  10.2 7.7 %copy-start.6 = (s32[1,128]{1,0:T(1,128)S(1)}, s32[1,128]{1,0:T(1,128)}, u32[]{:S(2)}) copy-start(s32[1,128]{1,0:T(1,128)} %param.12) | copy-start | bytes 1540
  10.4 25.0 %collective-permute-start = (f32[913,128]{1,0:T(8,128)S(1)}, f32[913,128]{1,0:T(8,128)S(1)}, u32[]{:S(2)}, u32[]{:S(2)}) collective-permute-start(f32[913,128]{1,0:T(8,128)S(1)} %get-tuple-element.67), channel_id=1, source_target_pairs={{0,1},{1,2},{2,3},{3,4},{4,5},{5,6},{6,7},{8,9},{9,10},{10,11},{11... | collective-permute-start | bytes 1402376 | tf_op jit(solution)/shard_map/ppermute | solution.py:223
  15.3 21.3 %collective-permute-start.1 = (f32[913,128]{1,0:T(8,128)S(1)}, f32[913,128]{1,0:T(8,128)}, u32[]{:S(2)}, u32[]{:S(2)}) collective-permute-start(f32[913,128]{1,0:T(8,128)S(1)} %get-tuple-element.66), channel_id=1, source_target_pairs={{1,0},{2,1},{3,2},{4,3},{5,4},{6,5},{7,6},{9,8},{10,9},{11,10},{12... | collective-permute-start | bytes 1402376 | tf_op jit(solution)/shard_map/ppermute | solution.py:224
  38.5 2.8 %copy-start.4 = (f32[768,128]{1,0:T(8,128)S(1)}, f32[768,128]{1,0:T(8,128)}, u32[]{:S(2)}) copy-start(f32[768,128]{1,0:T(8,128)} %reshape.1054) | copy-start | bytes 1179652
  38.6 7.2 %copy-start.3 = (f32[768,128]{1,0:T(8,128)S(1)}, f32[768,128]{1,0:T(8,128)}, u32[]{:S(2)}) copy-start(f32[768,128]{1,0:T(8,128)} %reshape.1053) | copy-start | bytes 1179652
  41.3 20.4 %collective-permute-start.2 = (f32[768,128]{1,0:T(8,128)S(1)}, f32[768,128]{1,0:T(8,128)S(1)}, u32[]{:S(2)}, u32[]{:S(2)}) collective-permute-start(f32[768,128]{1,0:T(8,128)S(1)} %copy-done.4), channel_id=1, source_target_pairs={{0,1},{1,2},{2,3},{3,4},{4,5},{5,6},{6,7},{8,9},{9,10},{10,11},{11... | collective-permute-start | bytes 1179656 | tf_op jit(solution)/shard_map/ppermute | solution.py:223
  45.7 16.8 %collective-permute-start.3 = (f32[768,128]{1,0:T(8,128)S(1)}, f32[768,128]{1,0:T(8,128)S(1)}, u32[]{:S(2)}, u32[]{:S(2)}) collective-permute-start(f32[768,128]{1,0:T(8,128)S(1)} %copy-done.3), channel_id=1, source_target_pairs={{1,0},{2,1},{3,2},{4,3},{5,4},{6,5},{7,6},{9,8},{10,9},{11,10},{12... | collective-permute-start | bytes 1179656 | tf_op jit(solution)/shard_map/ppermute | solution.py:224
  63.4 40.6 %copy-start.5 = (f32[1,6,128]{2,0,1:T(1,128)S(1)}, f32[1,6,128]{2,0,1:T(1,128)}, u32[]{:S(2)}) copy-start(f32[1,6,128]{2,0,1:T(1,128)} %param.13) | copy-start | bytes 9220
  104.1 10.2 %collective-permute-start.4 = (f32[7,128]{1,0:T(8,128)S(1)}, f32[7,128]{1,0:T(8,128)S(1)}, u32[]{:S(2)}, u32[]{:S(2)}) collective-permute-start(f32[7,128]{1,0:T(8,128)S(1)} %pad_maximum_fusion.2), channel_id=1, source_target_pairs={{0,1},{1,2},{2,3},{3,4},{4,5},{5,6},{6,7},{8,9},{9,10},{10,11},{11... | collective-permute-start | bytes 10760 | tf_op jit(solution)/shard_map/ppermute | solution.py:223
  108.5 5.8 %collective-permute-start.5 = (f32[7,128]{1,0:T(8,128)S(1)}, f32[7,128]{1,0:T(8,128)S(1)}, u32[]{:S(2)}, u32[]{:S(2)}) collective-permute-start(f32[7,128]{1,0:T(8,128)S(1)} %pad_maximum_fusion.2), channel_id=1, source_target_pairs={{1,0},{2,1},{3,2},{4,3},{5,4},{6,5},{7,6},{9,8},{10,9},{11,10},{12... | collective-permute-start | bytes 10760 | tf_op jit(solution)/shard_map/ppermute | solution.py:224
  115.1 1.0 copy-start.1
  157.5 3.6 %collective-permute-start.6 = (f32[3,2,4,128,128]{4,3,2,1,0:T(8,128)S(1)}, f32[3,2,4,128,128]{4,3,2,1,0:T(8,128)}, u32[]{:S(2)}, u32[]{:S(2)}) collective-permute-start(f32[3,2,4,128,128]{4,3,2,1,0:T(8,128)S(1)} %dynamic-slice_bitcast_fusion), channel_id=1, source_target_pairs={{0,8},{8,0},{16,24},{24,16},{1,9},{9,1},{17,25},{25,17},{2,10},{10... | collective-permute-start | bytes 4718600 | tf_op jit(solution)/shard_map/ppermute | solution.py:319
  163.2 2.5 %copy-start.2 = (f32[16,128,128]{2,1,0:T(8,128)S(1)}, f32[16,128,128]{2,1,0:T(8,128)}, u32[]{:S(2)}) copy-start(f32[16,128,128]{2,1,0:T(8,128)} %get-tuple-element.22) | copy-start | bytes 3145732
  164.1 19.9 %collective-permute-start.7 = (f32[3,4,128,128]{3,2,1,0:T(8,128)}, f32[3,4,128,128]{3,2,1,0:T(8,128)}, u32[]{:S(2)}, u32[]{:S(2)}) collective-permute-start(f32[3,4,128,128]{3,2,1,0:T(8,128)} %dynamic-slice_bitcast_fusion.1), channel_id=1, source_target_pairs={{0,16},{8,24},{16,0},{24,8},{1,17},{9,25},{17,1},{25,9},{2,18},{10... | collective-permute-start | bytes 2359304 | tf_op jit(solution)/shard_map/ppermute | solution.py:324
Sparse Core Ops, SparseCore 0:
  9.5 31.2 all-gather.1

commit v5 on v4

--- a/solution.py
+++ b/solution.py
@@ -30,7 +30,7 @@
 
 
 def forward_kernel(wave_ref, fs_ref, sl_ref, sr_ref, co_ref, ch_ref, mask_ref, rrow_ref, rlane_ref,
-                   h_ref, z_ref, rec_ref, pl_ref, q_ref, pb, qb, cf_ref, racc):
+                   h_ref, z_ref, rec_ref, pl_ref, q_ref, pb, qb, cf_ref, plocal, pickf):
     steps = h_ref.shape[0]
     az, xd, ay = mask_ref.shape
     ax = h_ref.shape[2]
@@ -44,11 +44,11 @@
     place(cf_ref, co_ref[...], ch_ref[:, :, :w], ch_ref[:, :, w:], 0)
     lane = lax.broadcasted_iota(jnp.int32, (xd, ay), 1)
     n_rec = rrow_ref.shape[0]
+    pickf[...] = jnp.where(lax.broadcasted_iota(jnp.int32, pickf.shape, 1) == rrow_ref[...], 1.0, 0.0).astype(jnp.bfloat16)
     for n in range(steps):
         cur = n % 2
         old = 1 - cur
         wv = wave_ref[n]
-        racc[...] = jnp.zeros(racc.shape, jnp.float32)
 
         def plane(d, carry):
             pc = pb[cur, d + 2, inner, :]
@@ -72,24 +72,23 @@
             h_ref[n, d] = h[OFF:OFF + ax]
             z_ref[n, d] = z[OFF:OFF + ax]
             po = pn[OFF:OFF + ax]
-            hit = lax.broadcasted_iota(jnp.int32, (n_rec, ax), 1) + d * ax == rrow_ref[...]
-            pick = jnp.where(hit, 1.0, 0.0).astype(jnp.bfloat16)
-            got = None
-            for part in split3(po):
-                term = jnp.dot(pick, part, preferred_element_type=jnp.float32)
-                got = term if got is None else got + term
-            racc[...] = racc[...] + got
+            plocal[pl.ds(pl.multiple_of(d * ax, ax), ax), :] = po
             if n == steps - 1:
                 q_ref[d] = qn[OFF:OFF + ax]
                 pl_ref[d] = po
             return carry
 
         lax.fori_loop(0, az, plane, 0)
+        got = None
+        for part in split3(plocal[...]):
+            term = jnp.dot(pickf[...], part, preferred_element_type=jnp.float32)
+            got = term if got is None else got + term
         sel = lax.broadcasted_iota(jnp.int32, (n_rec, ay), 1) == rlane_ref[...]
-        rec_ref[n] = jnp.where(sel, racc[...], 0.0)
-
-
-def adjoint_kernel(ad_ref, al_ref, ar_ref, co_ref, ch_ref, h_ref, z_ref, row_ref, m_ref, acc_ref, fin_ref, lb, mb, ob, fb, cf_ref):
+        rec_ref[n] = jnp.where(sel, got, 0.0)
+
+
+def adjoint_kernel(ad_ref, al_ref, ar_ref, co_ref, ch_ref, h_ref, z_ref, row_ref, m_ref, acc_ref, fin_ref, lb, mb, ob, fb, cf_ref,
+                   picka, eb):
     steps = h_ref.shape[0]
     az, xd, ay = ob.shape[0] - 4, ob.shape[1], ob.shape[2]
     ax = h_ref.shape[2]
@@ -100,6 +99,7 @@
     for k, (buf, slot) in enumerate(((lb, 0), (mb, 0), (lb, 1), (mb, 1))):
         place(buf.at[slot], ad_ref[k], al_ref[k], ar_ref[k], 0)
     place(cf_ref, co_ref[...], ch_ref[:, :, :w], ch_ref[:, :, w:], 0)
+    picka[...] = jnp.where(lax.broadcasted_iota(jnp.int32, picka.shape, 0) == row_ref[...], 1.0, 0.0).astype(jnp.bfloat16)
     ob[...] = jnp.zeros(ob.shape, jnp.float32)
     fb[...] = jnp.zeros(fb.shape, jnp.float32)
     acc_ref[...] = jnp.zeros(acc_ref.shape, jnp.float32)
@@ -114,6 +114,8 @@
             return carry
 
         lax.fori_loop(0, az, other_plane, 0)
+        eb[...] = (jnp.dot(picka[...], m_ref[s, 0], preferred_element_type=jnp.float32)
+                   + jnp.dot(picka[...], m_ref[s, 1], preferred_element_type=jnp.float32))
 
         def plane(d, carry):
             lc = lb[cur, d]
@@ -129,10 +131,7 @@
             yp1 = jnp.where(lane < ay - 1, pltpu.roll(f, ay - 1, 1), 0.0)
             yp2 = jnp.where(lane < ay - 2, pltpu.roll(f, ay - 2, 1), 0.0)
             hf = d2x + d2(ym2, ym1, f, yp1, yp2)
-            hit = lax.broadcasted_iota(jnp.int32, (xd, row_ref.shape[1]), 0) + d * xd == row_ref[...]
-            pick = jnp.where(hit, 1.0, 0.0).astype(jnp.bfloat16)
-            e = jnp.dot(pick, m_ref[s, 0], preferred_element_type=jnp.float32)
-            e = e + jnp.dot(pick, m_ref[s, 1], preferred_element_type=jnp.float32)
+            e = eb[pl.ds(pl.multiple_of(d * xd, 8), xd), :]
             ln = e + 2.0 * lc + hf - lb[old, d]
             mn = 2.0 * mc + d2(ob[d], ob[d + 1], ob[d + 2], ob[d + 3], ob[d + 4]) - mb[old, d]
             lb[old, d] = ln
@@ -167,6 +166,8 @@
             pltpu.VMEM((az + 4, xd, ay), jnp.float32),
             pltpu.VMEM((xd + 2 * PADX, ay), jnp.float32),
             pltpu.VMEM((3, az, xd, ay), jnp.float32),
+            pltpu.VMEM((az * xd, row.shape[1]), jnp.bfloat16),
+            pltpu.VMEM((az * xd, ay), jnp.float32),
         ],
         compiler_params=pltpu.CompilerParams(vmem_limit_bytes=62 * 1024 * 1024),
         interpret=INTERPRET,
@@ -194,7 +195,8 @@
         in_specs=[pl.BlockSpec(memory_space=pltpu.SMEM)] + [vm] * 8,
         out_specs=(vm, vm, vm, vm, vm),
         scratch_shapes=[pltpu.VMEM((2, az + 4, xd + 2 * PADX, ay), jnp.float32)] * 2
-        + [pltpu.VMEM((3, az, xd, ay), jnp.float32), pltpu.VMEM((n_rec, ay), jnp.float32)],
+        + [pltpu.VMEM((3, az, xd, ay), jnp.float32), pltpu.VMEM((az * ax, ay), jnp.float32),
+           pltpu.VMEM((n_rec, az * ax), jnp.bfloat16)],
         compiler_params=pltpu.CompilerParams(vmem_limit_bytes=62 * 1024 * 1024),
         interpret=INTERPRET,
     )(wave, fs, sl, sr, co, ch, mask, rrow, rlane)

time: 194 us -> 186 us (0.959)
  Pallas kernels: 79.3 us -> 72 us
    pallas_call x1, Pallas kernels: 39.5 us -> 30.9 us  [run_forward(): pl.pallas_call(forward_kernel, out_shape=(loc, loc, jax.ShapeDtypeStruct(...]
where the time goes in v5:
time: 186 us
  Pallas kernels  72 us (39%)
  waiting for transfers between devices  42.9 us (23%)
  starting transfers between devices  19.4 us (10%)
  between operations  16.7 us (9%)
  local copies, waits for them, and re-layouts  14.3 us (8%)
  other arithmetic  12.5 us (7%)
  blocking collectives  8.01 us (4%)
    pallas_call x1, Pallas kernels, run_adjoint(): pl.pallas_call(adjoint_kernel, out_shape=(jax.ShapeDtypeStruct((3, az, ax...  41.1 us
    pallas_call x1, Pallas kernels, run_forward(): pl.pallas_call(forward_kernel, out_shape=(loc, loc, jax.ShapeDtypeStruct(...  30.9 us
    ppermute x3, waiting for transfers between devices, to_left_right(): from_left = lax.ppermute(tail, axis, [(i, i + 1) for i in range(count - 1)])  18.8 us
    ppermute x1, waiting for transfers between devices, per_device(): partial = lax.ppermute(partial, 'shot', ring)  15.6 us
    ppermute x3, starting transfers between devices, to_left_right(): from_left = lax.ppermute(tail, axis, [(i, i + 1) for i in range(count - 1)])  13.7 us
    all_gather x1, blocking collectives, per_device(): lax.all_gather(jnp.concatenate([cf_l, cf_r], axis=2), 'shot', axis=1, til...  8.01 us
    ppermute x3, waiting for transfers between devices, to_left_right(): lax.ppermute(head, axis, [(i + 1, i) for i in range(count - 1)])  4.33 us
    ppermute x3, starting transfers between devices, to_left_right(): lax.ppermute(head, axis, [(i + 1, i) for i in range(count - 1)])  4.06 us
  transfers between devices with their start and end apart: 9, of which 5 were waited for; matrix products, arithmetic and copies ran while one was open for 9% of the time, Pallas kernels for 0%

profile of v5, /device:TPU:0, one launch (start us, length us, event | category | flops | bytes accessed | tf_op | source)
XLA Modules:
  0.0 185.8 jit_solution(382952138633277848)
XLA Ops:
  7.2 0.0 all-gather.2.cloned.1.call-start
  7.2 0.7 all-gather.2.cloned.1.call-update
  8.6 1.4 fusion.46
  10.1 0.1 pad.56.clone
  10.2 0.2 maximum_maximum_fusion.1
  10.4 4.9 %collective-permute-start = (f32[913,128]{1,0:T(8,128)S(1)}, f32[913,128]{1,0:T(8,128)S(1)}, u32[]{:S(2)}, u32[]{:S(2)}) collective-permute-start(f32[913,128]{1,0:T(8,128)S(1)} %get-tuple-element.67), channel_id=1, source_target_pairs={{0,1},{1,2},{2,3},{3,4},{4,5},{5,6},{6,7},{8,9},{9,10},{10,11},{11... | collective-permute-start | bytes 1402376 | tf_op jit(solution)/shard_map/ppermute | solution.py:225
  15.3 1.3 collective-permute-start.1
  16.6 1.3 fusion.47
  18.0 0.8 reshape.1053
  18.8 0.8 reshape.1054
  19.5 0.1 copy.14
  19.7 0.7 add_select_fusion
  20.4 14.9 %collective-permute-done = f32[913,128]{1,0:T(8,128)S(1)} collective-permute-done((f32[913,128]{1,0:T(8,128)S(1)}, f32[913,128]{1,0:T(8,128)S(1)}, u32[]{:S(2)}, u32[]{:S(2)}) %collective-permute-start) | collective-permute-done | bytes 467488 | tf_op jit(solution)/shard_map/ppermute | solution.py:225
  35.4 0.5 slice.160
  36.6 1.2 slice.161
  38.6 0.8 reshape.1057.sl_ref
  39.4 1.0 slice.157
  40.5 0.9 reshape.1060.sr_ref
  41.3 4.4 %collective-permute-start.2 = (f32[768,128]{1,0:T(8,128)S(1)}, f32[768,128]{1,0:T(8,128)S(1)}, u32[]{:S(2)}, u32[]{:S(2)}) collective-permute-start(f32[768,128]{1,0:T(8,128)S(1)} %copy-done.4), channel_id=1, source_target_pairs={{0,1},{1,2},{2,3},{3,4},{4,5},{5,6},{6,7},{8,9},{9,10},{10,11},{11... | collective-permute-start | bytes 1179656 | tf_op jit(solution)/shard_map/ppermute | solution.py:225
  45.7 1.3 collective-permute-start.3
  47.0 0.1 add_convert_fusion
  47.1 0.1 fusion.45
  47.2 0.9 slice.159
  48.1 1.7 scatter_custom_fusion
  49.9 8.0 %all_gather.7.ch_ref = f32[3,16,24,128]{3,2,1,0:T(8,128)} all-gather(f32[3,4,24,128]{3,2,1,0:T(8,128)S(1)} %pad_maximum_fusion.1), channel_id=1, replica_groups=mesh['shot'=4,'tile'=8] {'shot'}, dimensions={1}, use_global_device_ids=true | all-gather | bytes 737280 | tf_op jit(solution)/shard_map/all_gather | solution.py:267
  57.9 3.9 %collective-permute-done.2 = f32[768,128]{1,0:T(8,128)S(1)} collective-permute-done((f32[768,128]{1,0:T(8,128)S(1)}, f32[768,128]{1,0:T(8,128)S(1)}, u32[]{:S(2)}, u32[]{:S(2)}) %collective-permute-start.2) | collective-permute-done | bytes 393248 | tf_op jit(solution)/shard_map/ppermute | solution.py:225
  61.7 0.8 reshape.1061.al_ref
  62.6 0.8 reshape.1062.ar_ref
  63.4 30.9 %shard_map.94 = (f32[6,16,128,128]{3,2,1,0:T(8,128)}, f32[6,16,128,128]{3,2,1,0:T(8,128)}, f32[6,128,128]{2,1,0:T(8,128)}, f32[16,128,128]{2,1,0:T(8,128)}, f32[16,128,128]{2,1,0:T(8,128)}) custom-call(f32[6]{0:T(128)} %bitcast.159, f32[4,16,128,128]{3,2,1,0:T(8,128)} %bitcast.152, f32[4,16,12,128]{3,2,1,0:T(8,128)} %reshape.1057.sl_ref, ...), custom_call_target="tpu_custom_call" | custom-call | tf_op jit(solution)/shard_map/pallas_call | solution.py:192
  94.3 1.2 reduce_sum.9
  95.5 4.4 %collective-permute-start.4 = (f32[7,128]{1,0:T(8,128)S(1)}, f32[7,128]{1,0:T(8,128)S(1)}, u32[]{:S(2)}, u32[]{:S(2)}) collective-permute-start(f32[7,128]{1,0:T(8,128)S(1)} %pad_maximum_fusion.2), channel_id=1, source_target_pairs={{0,1},{1,2},{2,3},{3,4},{4,5},{5,6},{6,7},{8,9},{9,10},{10,11},{11... | collective-permute-start | bytes 10760 | tf_op jit(solution)/shard_map/ppermute | solution.py:225
  99.9 1.5 collective-permute-start.5
  101.4 4.3 %collective-permute-done.5 = f32[7,128]{1,0:T(8,128)S(1)} collective-permute-done((f32[7,128]{1,0:T(8,128)S(1)}, f32[7,128]{1,0:T(8,128)S(1)}, u32[]{:S(2)}, u32[]{:S(2)}) %collective-permute-start.5) | collective-permute-done | bytes 3616 | tf_op jit(solution)/shard_map/ppermute | solution.py:226
  105.9 0.4 reduce-precision_convert_fusion
  106.6 0.7 and_select_fusion.row_ref
  107.3 0.3 copy-done.1
  107.5 41.1 %shard_map.95 = (f32[3,16,128,128]{3,2,1,0:T(8,128)}, f32[2,16,128,128]{3,2,1,0:T(8,128)}) custom-call(f32[4,16,128,128]{3,2,1,0:T(8,128)} %bitcast.150, f32[4,16,12,128]{3,2,1,0:T(8,128)} %reshape.1061.al_ref, f32[4,16,12,128]{3,2,1,0:T(8,128)} %reshape.1062.ar_ref, f32[3,16,128,128]{3,2,1,0:T(8,128)} %all-gather.2.cloned.1.call-done.co_ref, ...), custom_call_target="tpu_custom_call" | custom-call | tf_op jit(solution)/shard_map/pallas_call | solution.py:158
  148.7 1.5 dynamic-slice_bitcast_fusion
  150.2 0.1 collective-permute-start.6
  150.3 3.5 %collective-permute-done.6 = f32[3,2,4,128,128]{4,3,2,1,0:T(8,128)} collective-permute-done((f32[3,2,4,128,128]{4,3,2,1,0:T(8,128)S(1)}, f32[3,2,4,128,128]{4,3,2,1,0:T(8,128)}, u32[]{:S(2)}, u32[]{:S(2)}) %collective-permute-start.6) | collective-permute-done | bytes 1572896 | tf_op jit(solution)/shard_map/ppermute | solution.py:321
  153.8 2.1 %bitcast_add_fusion = f32[3,2,4,128,128]{4,3,2,1,0:T(8,128)S(1)} fusion(f32[3,2,4,128,128]{4,3,2,1,0:T(8,128)} %collective-permute-done.6, f32[3,2,2,4,128,128]{5,4,3,2,1,0:T(8,128)} %bitcast.155, s32[]{:T(128)S(6)} %select_n.465), kind=kLoop, calls=%fused_computation.2 | loop fusion | flops 393216 | bytes 4718596 | tf_op jit(solution)/shard_map/add | solution.py:322
  155.8 0.9 dynamic-slice_bitcast_fusion.1
  156.8 1.5 collective-permute-start.7
  158.3 2.7 %maximum_bitcast_fusion = f32[1,2,16,128,128]{4,3,2,1,0:T(8,128)} fusion(f32[1,16,128,128]{3,2,1,0:T(8,128)} %bitcast.157, f32[1,16,128,128]{3,2,1,0:T(8,128)S(1)} %bitcast.156), kind=kLoop, calls=%fused_computation.1 | loop fusion | flops 524288 | bytes 4194304 | tf_op jit(solution)/shard_map/broadcast_in_dim | solution.py:332
  161.0 15.6 %collective-permute-done.7 = f32[3,4,128,128]{3,2,1,0:T(8,128)} collective-permute-done((f32[3,4,128,128]{3,2,1,0:T(8,128)}, f32[3,4,128,128]{3,2,1,0:T(8,128)}, u32[]{:S(2)}, u32[]{:S(2)}) %collective-permute-start.7) | collective-permute-done | bytes 786464 | tf_op jit(solution)/shard_map/ppermute | solution.py:326
  176.7 1.2 bitcast_add_fusion.1
  177.9 0.1 slice_add_fusion
  178.0 0.9 pad_maximum_fusion
  (48 shorter events, 0.6 us)
Async XLA Ops:
  7.2 56.2 %all-gather.2.cloned.1.call-start = ((), (), s32[]{:S(2)}) async-start(), calls=%async_computation | async-start | bytes 3932160 | tf_op jit(solution)/shard_map/all_gather | solution.py:240
  8.5 1.5 copy-start
  10.2 7.7 %copy-start.6 = (s32[1,128]{1,0:T(1,128)S(1)}, s32[1,128]{1,0:T(1,128)}, u32[]{:S(2)}) copy-start(s32[1,128]{1,0:T(1,128)} %param.12) | copy-start | bytes 1540
  10.4 25.0 %collective-permute-start = (f32[913,128]{1,0:T(8,128)S(1)}, f32[913,128]{1,0:T(8,128)S(1)}, u32[]{:S(2)}, u32[]{:S(2)}) collective-permute-start(f32[913,128]{1,0:T(8,128)S(1)} %get-tuple-element.67), channel_id=1, source_target_pairs={{0,1},{1,2},{2,3},{3,4},{4,5},{5,6},{6,7},{8,9},{9,10},{10,11},{11... | collective-permute-start | bytes 1402376 | tf_op jit(solution)/shard_map/ppermute | solution.py:225
  15.3 21.3 %collective-permute-start.1 = (f32[913,128]{1,0:T(8,128)S(1)}, f32[913,128]{1,0:T(8,128)}, u32[]{:S(2)}, u32[]{:S(2)}) collective-permute-start(f32[913,128]{1,0:T(8,128)S(1)} %get-tuple-element.66), channel_id=1, source_target_pairs={{1,0},{2,1},{3,2},{4,3},{5,4},{6,5},{7,6},{9,8},{10,9},{11,10},{12... | collective-permute-start | bytes 1402376 | tf_op jit(solution)/shard_map/ppermute | solution.py:226
  38.5 2.8 %copy-start.4 = (f32[768,128]{1,0:T(8,128)S(1)}, f32[768,128]{1,0:T(8,128)}, u32[]{:S(2)}) copy-start(f32[768,128]{1,0:T(8,128)} %reshape.1054) | copy-start | bytes 1179652
  38.6 7.2 %copy-start.3 = (f32[768,128]{1,0:T(8,128)S(1)}, f32[768,128]{1,0:T(8,128)}, u32[]{:S(2)}) copy-start(f32[768,128]{1,0:T(8,128)} %reshape.1053) | copy-start | bytes 1179652
  41.3 20.4 %collective-permute-start.2 = (f32[768,128]{1,0:T(8,128)S(1)}, f32[768,128]{1,0:T(8,128)S(1)}, u32[]{:S(2)}, u32[]{:S(2)}) collective-permute-start(f32[768,128]{1,0:T(8,128)S(1)} %copy-done.4), channel_id=1, source_target_pairs={{0,1},{1,2},{2,3},{3,4},{4,5},{5,6},{6,7},{8,9},{9,10},{10,11},{11... | collective-permute-start | bytes 1179656 | tf_op jit(solution)/shard_map/ppermute | solution.py:225
  45.7 16.8 %collective-permute-start.3 = (f32[768,128]{1,0:T(8,128)S(1)}, f32[768,128]{1,0:T(8,128)S(1)}, u32[]{:S(2)}, u32[]{:S(2)}) collective-permute-start(f32[768,128]{1,0:T(8,128)S(1)} %copy-done.3), channel_id=1, source_target_pairs={{1,0},{2,1},{3,2},{4,3},{5,4},{6,5},{7,6},{9,8},{10,9},{11,10},{12... | collective-permute-start | bytes 1179656 | tf_op jit(solution)/shard_map/ppermute | solution.py:226
  63.4 32.1 %copy-start.5 = (f32[1,6,128]{2,0,1:T(1,128)S(1)}, f32[1,6,128]{2,0,1:T(1,128)}, u32[]{:S(2)}) copy-start(f32[1,6,128]{2,0,1:T(1,128)} %param.13) | copy-start | bytes 9220
  95.5 10.2 %collective-permute-start.4 = (f32[7,128]{1,0:T(8,128)S(1)}, f32[7,128]{1,0:T(8,128)S(1)}, u32[]{:S(2)}, u32[]{:S(2)}) collective-permute-start(f32[7,128]{1,0:T(8,128)S(1)} %pad_maximum_fusion.2), channel_id=1, source_target_pairs={{0,1},{1,2},{2,3},{3,4},{4,5},{5,6},{6,7},{8,9},{9,10},{10,11},{11... | collective-permute-start | bytes 10760 | tf_op jit(solution)/shard_map/ppermute | solution.py:225
  99.9 5.8 %collective-permute-start.5 = (f32[7,128]{1,0:T(8,128)S(1)}, f32[7,128]{1,0:T(8,128)S(1)}, u32[]{:S(2)}, u32[]{:S(2)}) collective-permute-start(f32[7,128]{1,0:T(8,128)S(1)} %pad_maximum_fusion.2), channel_id=1, source_target_pairs={{1,0},{2,1},{3,2},{4,3},{5,4},{6,5},{7,6},{9,8},{10,9},{11,10},{12... | collective-permute-start | bytes 10760 | tf_op jit(solution)/shard_map/ppermute | solution.py:226
  106.5 1.0 copy-start.1
  150.2 3.6 %collective-permute-start.6 = (f32[3,2,4,128,128]{4,3,2,1,0:T(8,128)S(1)}, f32[3,2,4,128,128]{4,3,2,1,0:T(8,128)}, u32[]{:S(2)}, u32[]{:S(2)}) collective-permute-start(f32[3,2,4,128,128]{4,3,2,1,0:T(8,128)S(1)} %dynamic-slice_bitcast_fusion), channel_id=1, source_target_pairs={{0,8},{8,0},{16,24},{24,16},{1,9},{9,1},{17,25},{25,17},{2,10},{10... | collective-permute-start | bytes 4718600 | tf_op jit(solution)/shard_map/ppermute | solution.py:321
  155.8 2.5 %copy-start.2 = (f32[16,128,128]{2,1,0:T(8,128)S(1)}, f32[16,128,128]{2,1,0:T(8,128)}, u32[]{:S(2)}) copy-start(f32[16,128,128]{2,1,0:T(8,128)} %get-tuple-element.22) | copy-start | bytes 3145732
  156.8 19.9 %collective-permute-start.7 = (f32[3,4,128,128]{3,2,1,0:T(8,128)}, f32[3,4,128,128]{3,2,1,0:T(8,128)}, u32[]{:S(2)}, u32[]{:S(2)}) collective-permute-start(f32[3,4,128,128]{3,2,1,0:T(8,128)} %dynamic-slice_bitcast_fusion.1), channel_id=1, source_target_pairs={{0,16},{8,24},{16,0},{24,8},{1,17},{9,25},{17,1},{25,9},{2,18},{10... | collective-permute-start | bytes 2359304 | tf_op jit(solution)/shard_map/ppermute | solution.py:326
Sparse Core Ops, SparseCore 0:
  9.5 31.2 all-gather.1

commit v6 on v5

--- a/solution.py
+++ b/solution.py
@@ -87,8 +87,7 @@
         rec_ref[n] = jnp.where(sel, got, 0.0)
 
 
-def adjoint_kernel(ad_ref, al_ref, ar_ref, co_ref, ch_ref, h_ref, z_ref, row_ref, m_ref, acc_ref, fin_ref, lb, mb, ob, fb, cf_ref,
-                   picka, eb):
+def adjoint_kernel(ad_ref, al_ref, ar_ref, co_ref, ch_ref, h_ref, z_ref, row_ref, m_ref, acc_ref, fin_ref, lb, mb, ob, fb, cf_ref):
     steps = h_ref.shape[0]
     az, xd, ay = ob.shape[0] - 4, ob.shape[1], ob.shape[2]
     ax = h_ref.shape[2]
@@ -99,7 +98,6 @@
     for k, (buf, slot) in enumerate(((lb, 0), (mb, 0), (lb, 1), (mb, 1))):
         place(buf.at[slot], ad_ref[k], al_ref[k], ar_ref[k], 0)
     place(cf_ref, co_ref[...], ch_ref[:, :, :w], ch_ref[:, :, w:], 0)
-    picka[...] = jnp.where(lax.broadcasted_iota(jnp.int32, picka.shape, 0) == row_ref[...], 1.0, 0.0).astype(jnp.bfloat16)
     ob[...] = jnp.zeros(ob.shape, jnp.float32)
     fb[...] = jnp.zeros(fb.shape, jnp.float32)
     acc_ref[...] = jnp.zeros(acc_ref.shape, jnp.float32)
@@ -114,8 +112,6 @@
             return carry
 
         lax.fori_loop(0, az, other_plane, 0)
-        eb[...] = (jnp.dot(picka[...], m_ref[s, 0], preferred_element_type=jnp.float32)
-                   + jnp.dot(picka[...], m_ref[s, 1], preferred_element_type=jnp.float32))
 
         def plane(d, carry):
             lc = lb[cur, d]
@@ -131,7 +127,10 @@
             yp1 = jnp.where(lane < ay - 1, pltpu.roll(f, ay - 1, 1), 0.0)
             yp2 = jnp.where(lane < ay - 2, pltpu.roll(f, ay - 2, 1), 0.0)
             hf = d2x + d2(ym2, ym1, f, yp1, yp2)
-            e = eb[pl.ds(pl.multiple_of(d * xd, 8), xd), :]
+            hit = lax.broadcasted_iota(jnp.int32, (xd, row_ref.shape[1]), 0) + d * xd == row_ref[...]
+            pick = jnp.where(hit, 1.0, 0.0).astype(jnp.bfloat16)
+            e = jnp.dot(pick, m_ref[s, 0], preferred_element_type=jnp.float32)
+            e = e + jnp.dot(pick, m_ref[s, 1], preferred_element_type=jnp.float32)
             ln = e + 2.0 * lc + hf - lb[old, d]
             mn = 2.0 * mc + d2(ob[d], ob[d + 1], ob[d + 2], ob[d + 3], ob[d + 4]) - mb[old, d]
             lb[old, d] = ln
@@ -166,8 +165,6 @@
             pltpu.VMEM((az + 4, xd, ay), jnp.float32),
             pltpu.VMEM((xd + 2 * PADX, ay), jnp.float32),
             pltpu.VMEM((3, az, xd, ay), jnp.float32),
-            pltpu.VMEM((az * xd, row.shape[1]), jnp.bfloat16),
-            pltpu.VMEM((az * xd, ay), jnp.float32),
         ],
         compiler_params=pltpu.CompilerParams(vmem_limit_bytes=62 * 1024 * 1024),
         interpret=INTERPRET,

time: 186 us -> 185 us (level)
  no operation moved by 1% of the time
where the time goes in v6:
time: 185 us
  Pallas kernels  70.7 us (38%)
  waiting for transfers between devices  43.1 us (23%)
  starting transfers between devices  19.2 us (10%)
  between operations  16.7 us (9%)
  local copies, waits for them, and re-layouts  14.3 us (8%)
  other arithmetic  12.5 us (7%)
  blocking collectives  8.01 us (4%)
    pallas_call x1, Pallas kernels, run_adjoint(): pl.pallas_call(adjoint_kernel, out_shape=(jax.ShapeDtypeStruct((3, az, ax...  39.9 us
    pallas_call x1, Pallas kernels, run_forward(): pl.pallas_call(forward_kernel, out_shape=(loc, loc, jax.ShapeDtypeStruct(...  30.9 us
    ppermute x3, waiting for transfers between devices, to_left_right(): from_left = lax.ppermute(tail, axis, [(i, i + 1) for i in range(count - 1)])  18.8 us
    ppermute x1, waiting for transfers between devices, per_device(): partial = lax.ppermute(partial, 'shot', ring)  15.6 us
    ppermute x3, starting transfers between devices, to_left_right(): from_left = lax.ppermute(tail, axis, [(i, i + 1) for i in range(count - 1)])  13.7 us
    all_gather x1, blocking collectives, per_device(): lax.all_gather(jnp.concatenate([cf_l, cf_r], axis=2), 'shot', axis=1, til...  8.01 us
    ppermute x3, waiting for transfers between devices, to_left_right(): lax.ppermute(head, axis, [(i + 1, i) for i in range(count - 1)])  4.51 us
    ppermute x3, starting transfers between devices, to_left_right(): lax.ppermute(head, axis, [(i + 1, i) for i in range(count - 1)])  3.88 us
  transfers between devices with their start and end apart: 9, of which 5 were waited for; matrix products, arithmetic and copies ran while one was open for 9% of the time, Pallas kernels for 0%

profile of v6, /device:TPU:0, one launch (start us, length us, event | category | flops | bytes accessed | tf_op | source)
XLA Modules:
  0.0 184.5 jit_solution(12138978394716165525)
XLA Ops:
  7.2 0.0 all-gather.2.cloned.1.call-start
  7.2 0.7 all-gather.2.cloned.1.call-update
  8.6 1.4 fusion.46
  10.1 0.1 pad.56.clone
  10.2 0.2 maximum_maximum_fusion.1
  10.4 4.9 %collective-permute-start = (f32[913,128]{1,0:T(8,128)S(1)}, f32[913,128]{1,0:T(8,128)S(1)}, u32[]{:S(2)}, u32[]{:S(2)}) collective-permute-start(f32[913,128]{1,0:T(8,128)S(1)} %get-tuple-element.67), channel_id=1, source_target_pairs={{0,1},{1,2},{2,3},{3,4},{4,5},{5,6},{6,7},{8,9},{9,10},{10,11},{11... | collective-permute-start | bytes 1402376 | tf_op jit(solution)/shard_map/ppermute | solution.py:222
  15.3 1.3 collective-permute-start.1
  16.6 1.3 fusion.47
  18.0 0.8 reshape.1053
  18.8 0.8 reshape.1054
  19.5 0.1 copy.14
  19.7 0.7 add_select_fusion
  20.4 14.9 %collective-permute-done = f32[913,128]{1,0:T(8,128)S(1)} collective-permute-done((f32[913,128]{1,0:T(8,128)S(1)}, f32[913,128]{1,0:T(8,128)S(1)}, u32[]{:S(2)}, u32[]{:S(2)}) %collective-permute-start) | collective-permute-done | bytes 467488 | tf_op jit(solution)/shard_map/ppermute | solution.py:222
  35.4 0.5 slice.160
  36.6 1.2 slice.161
  38.6 0.8 reshape.1057.sl_ref
  39.4 1.0 slice.157
  40.5 0.9 reshape.1060.sr_ref
  41.3 4.4 %collective-permute-start.2 = (f32[768,128]{1,0:T(8,128)S(1)}, f32[768,128]{1,0:T(8,128)S(1)}, u32[]{:S(2)}, u32[]{:S(2)}) collective-permute-start(f32[768,128]{1,0:T(8,128)S(1)} %copy-done.4), channel_id=1, source_target_pairs={{0,1},{1,2},{2,3},{3,4},{4,5},{5,6},{6,7},{8,9},{9,10},{10,11},{11... | collective-permute-start | bytes 1179656 | tf_op jit(solution)/shard_map/ppermute | solution.py:222
  45.7 1.3 collective-permute-start.3
  47.0 0.1 add_convert_fusion
  47.1 0.1 fusion.45
  47.2 0.9 slice.159
  48.1 1.7 scatter_custom_fusion
  49.9 8.0 %all_gather.7.ch_ref = f32[3,16,24,128]{3,2,1,0:T(8,128)} all-gather(f32[3,4,24,128]{3,2,1,0:T(8,128)S(1)} %pad_maximum_fusion.1), channel_id=1, replica_groups=mesh['shot'=4,'tile'=8] {'shot'}, dimensions={1}, use_global_device_ids=true | all-gather | bytes 737280 | tf_op jit(solution)/shard_map/all_gather | solution.py:264
  57.9 3.9 %collective-permute-done.2 = f32[768,128]{1,0:T(8,128)S(1)} collective-permute-done((f32[768,128]{1,0:T(8,128)S(1)}, f32[768,128]{1,0:T(8,128)S(1)}, u32[]{:S(2)}, u32[]{:S(2)}) %collective-permute-start.2) | collective-permute-done | bytes 393248 | tf_op jit(solution)/shard_map/ppermute | solution.py:222
  61.7 0.8 reshape.1061.al_ref
  62.6 0.8 reshape.1062.ar_ref
  63.4 30.9 %shard_map.94 = (f32[6,16,128,128]{3,2,1,0:T(8,128)}, f32[6,16,128,128]{3,2,1,0:T(8,128)}, f32[6,128,128]{2,1,0:T(8,128)}, f32[16,128,128]{2,1,0:T(8,128)}, f32[16,128,128]{2,1,0:T(8,128)}) custom-call(f32[6]{0:T(128)} %bitcast.159, f32[4,16,128,128]{3,2,1,0:T(8,128)} %bitcast.152, f32[4,16,12,128]{3,2,1,0:T(8,128)} %reshape.1057.sl_ref, ...), custom_call_target="tpu_custom_call" | custom-call | tf_op jit(solution)/shard_map/pallas_call | solution.py:189
  94.3 1.2 reduce_sum.9
  95.5 4.4 %collective-permute-start.4 = (f32[7,128]{1,0:T(8,128)S(1)}, f32[7,128]{1,0:T(8,128)S(1)}, u32[]{:S(2)}, u32[]{:S(2)}) collective-permute-start(f32[7,128]{1,0:T(8,128)S(1)} %pad_maximum_fusion.2), channel_id=1, source_target_pairs={{0,1},{1,2},{2,3},{3,4},{4,5},{5,6},{6,7},{8,9},{9,10},{10,11},{11... | collective-permute-start | bytes 10760 | tf_op jit(solution)/shard_map/ppermute | solution.py:222
  99.9 1.3 collective-permute-start.5
  101.2 4.5 %collective-permute-done.5 = f32[7,128]{1,0:T(8,128)S(1)} collective-permute-done((f32[7,128]{1,0:T(8,128)S(1)}, f32[7,128]{1,0:T(8,128)S(1)}, u32[]{:S(2)}, u32[]{:S(2)}) %collective-permute-start.5) | collective-permute-done | bytes 3616 | tf_op jit(solution)/shard_map/ppermute | solution.py:223
  105.9 0.4 reduce-precision_convert_fusion
  106.6 0.7 and_select_fusion.row_ref
  107.3 0.3 copy-done.1
  107.5 39.9 %shard_map.95 = (f32[3,16,128,128]{3,2,1,0:T(8,128)}, f32[2,16,128,128]{3,2,1,0:T(8,128)}) custom-call(f32[4,16,128,128]{3,2,1,0:T(8,128)} %bitcast.150, f32[4,16,12,128]{3,2,1,0:T(8,128)} %reshape.1061.al_ref, f32[4,16,12,128]{3,2,1,0:T(8,128)} %reshape.1062.ar_ref, f32[3,16,128,128]{3,2,1,0:T(8,128)} %all-gather.2.cloned.1.call-done.co_ref, ...), custom_call_target="tpu_custom_call" | custom-call | tf_op jit(solution)/shard_map/pallas_call | solution.py:157
  147.4 1.5 dynamic-slice_bitcast_fusion
  148.9 0.1 collective-permute-start.6
  149.0 3.5 %collective-permute-done.6 = f32[3,2,4,128,128]{4,3,2,1,0:T(8,128)} collective-permute-done((f32[3,2,4,128,128]{4,3,2,1,0:T(8,128)S(1)}, f32[3,2,4,128,128]{4,3,2,1,0:T(8,128)}, u32[]{:S(2)}, u32[]{:S(2)}) %collective-permute-start.6) | collective-permute-done | bytes 1572896 | tf_op jit(solution)/shard_map/ppermute | solution.py:318
  152.5 2.1 %bitcast_add_fusion = f32[3,2,4,128,128]{4,3,2,1,0:T(8,128)S(1)} fusion(f32[3,2,4,128,128]{4,3,2,1,0:T(8,128)} %collective-permute-done.6, f32[3,2,2,4,128,128]{5,4,3,2,1,0:T(8,128)} %bitcast.155, s32[]{:T(128)S(6)} %select_n.465), kind=kLoop, calls=%fused_computation.2 | loop fusion | flops 393216 | bytes 4718596 | tf_op jit(solution)/shard_map/add | solution.py:319
  154.6 0.9 dynamic-slice_bitcast_fusion.1
  155.5 1.5 collective-permute-start.7
  157.0 2.7 %maximum_bitcast_fusion = f32[1,2,16,128,128]{4,3,2,1,0:T(8,128)} fusion(f32[1,16,128,128]{3,2,1,0:T(8,128)} %bitcast.157, f32[1,16,128,128]{3,2,1,0:T(8,128)S(1)} %bitcast.156), kind=kLoop, calls=%fused_computation.1 | loop fusion | flops 524288 | bytes 4194304 | tf_op jit(solution)/shard_map/broadcast_in_dim | solution.py:329
  159.8 15.6 %collective-permute-done.7 = f32[3,4,128,128]{3,2,1,0:T(8,128)} collective-permute-done((f32[3,4,128,128]{3,2,1,0:T(8,128)}, f32[3,4,128,128]{3,2,1,0:T(8,128)}, u32[]{:S(2)}, u32[]{:S(2)}) %collective-permute-start.7) | collective-permute-done | bytes 786464 | tf_op jit(solution)/shard_map/ppermute | solution.py:323
  175.4 1.2 bitcast_add_fusion.1
  176.6 0.1 slice_add_fusion
  176.7 0.9 pad_maximum_fusion
  (48 shorter events, 0.6 us)
Async XLA Ops:
  7.2 56.2 %all-gather.2.cloned.1.call-start = ((), (), s32[]{:S(2)}) async-start(), calls=%async_computation | async-start | bytes 3932160 | tf_op jit(solution)/shard_map/all_gather | solution.py:237
  8.5 1.5 copy-start
  10.2 7.7 %copy-start.6 = (s32[1,128]{1,0:T(1,128)S(1)}, s32[1,128]{1,0:T(1,128)}, u32[]{:S(2)}) copy-start(s32[1,128]{1,0:T(1,128)} %param.12) | copy-start | bytes 1540
  10.4 25.0 %collective-permute-start = (f32[913,128]{1,0:T(8,128)S(1)}, f32[913,128]{1,0:T(8,128)S(1)}, u32[]{:S(2)}, u32[]{:S(2)}) collective-permute-start(f32[913,128]{1,0:T(8,128)S(1)} %get-tuple-element.67), channel_id=1, source_target_pairs={{0,1},{1,2},{2,3},{3,4},{4,5},{5,6},{6,7},{8,9},{9,10},{10,11},{11... | collective-permute-start | bytes 1402376 | tf_op jit(solution)/shard_map/ppermute | solution.py:222
  15.3 21.3 %collective-permute-start.1 = (f32[913,128]{1,0:T(8,128)S(1)}, f32[913,128]{1,0:T(8,128)}, u32[]{:S(2)}, u32[]{:S(2)}) collective-permute-start(f32[913,128]{1,0:T(8,128)S(1)} %get-tuple-element.66), channel_id=1, source_target_pairs={{1,0},{2,1},{3,2},{4,3},{5,4},{6,5},{7,6},{9,8},{10,9},{11,10},{12... | collective-permute-start | bytes 1402376 | tf_op jit(solution)/shard_map/ppermute | solution.py:223
  38.5 2.8 %copy-start.4 = (f32[768,128]{1,0:T(8,128)S(1)}, f32[768,128]{1,0:T(8,128)}, u32[]{:S(2)}) copy-start(f32[768,128]{1,0:T(8,128)} %reshape.1054) | copy-start | bytes 1179652
  38.6 7.2 %copy-start.3 = (f32[768,128]{1,0:T(8,128)S(1)}, f32[768,128]{1,0:T(8,128)}, u32[]{:S(2)}) copy-start(f32[768,128]{1,0:T(8,128)} %reshape.1053) | copy-start | bytes 1179652
  41.3 20.4 %collective-permute-start.2 = (f32[768,128]{1,0:T(8,128)S(1)}, f32[768,128]{1,0:T(8,128)S(1)}, u32[]{:S(2)}, u32[]{:S(2)}) collective-permute-start(f32[768,128]{1,0:T(8,128)S(1)} %copy-done.4), channel_id=1, source_target_pairs={{0,1},{1,2},{2,3},{3,4},{4,5},{5,6},{6,7},{8,9},{9,10},{10,11},{11... | collective-permute-start | bytes 1179656 | tf_op jit(solution)/shard_map/ppermute | solution.py:222
  45.7 16.8 %collective-permute-start.3 = (f32[768,128]{1,0:T(8,128)S(1)}, f32[768,128]{1,0:T(8,128)S(1)}, u32[]{:S(2)}, u32[]{:S(2)}) collective-permute-start(f32[768,128]{1,0:T(8,128)S(1)} %copy-done.3), channel_id=1, source_target_pairs={{1,0},{2,1},{3,2},{4,3},{5,4},{6,5},{7,6},{9,8},{10,9},{11,10},{12... | collective-permute-start | bytes 1179656 | tf_op jit(solution)/shard_map/ppermute | solution.py:223
  63.4 32.0 %copy-start.5 = (f32[1,6,128]{2,0,1:T(1,128)S(1)}, f32[1,6,128]{2,0,1:T(1,128)}, u32[]{:S(2)}) copy-start(f32[1,6,128]{2,0,1:T(1,128)} %param.13) | copy-start | bytes 9220
  95.5 10.2 %collective-permute-start.4 = (f32[7,128]{1,0:T(8,128)S(1)}, f32[7,128]{1,0:T(8,128)S(1)}, u32[]{:S(2)}, u32[]{:S(2)}) collective-permute-start(f32[7,128]{1,0:T(8,128)S(1)} %pad_maximum_fusion.2), channel_id=1, source_target_pairs={{0,1},{1,2},{2,3},{3,4},{4,5},{5,6},{6,7},{8,9},{9,10},{10,11},{11... | collective-permute-start | bytes 10760 | tf_op jit(solution)/shard_map/ppermute | solution.py:222
  99.9 5.8 %collective-permute-start.5 = (f32[7,128]{1,0:T(8,128)S(1)}, f32[7,128]{1,0:T(8,128)S(1)}, u32[]{:S(2)}, u32[]{:S(2)}) collective-permute-start(f32[7,128]{1,0:T(8,128)S(1)} %pad_maximum_fusion.2), channel_id=1, source_target_pairs={{1,0},{2,1},{3,2},{4,3},{5,4},{6,5},{7,6},{9,8},{10,9},{11,10},{12... | collective-permute-start | bytes 10760 | tf_op jit(solution)/shard_map/ppermute | solution.py:223
  106.5 1.0 copy-start.1
  148.9 3.6 %collective-permute-start.6 = (f32[3,2,4,128,128]{4,3,2,1,0:T(8,128)S(1)}, f32[3,2,4,128,128]{4,3,2,1,0:T(8,128)}, u32[]{:S(2)}, u32[]{:S(2)}) collective-permute-start(f32[3,2,4,128,128]{4,3,2,1,0:T(8,128)S(1)} %dynamic-slice_bitcast_fusion), channel_id=1, source_target_pairs={{0,8},{8,0},{16,24},{24,16},{1,9},{9,1},{17,25},{25,17},{2,10},{10... | collective-permute-start | bytes 4718600 | tf_op jit(solution)/shard_map/ppermute | solution.py:318
  154.6 2.5 %copy-start.2 = (f32[16,128,128]{2,1,0:T(8,128)S(1)}, f32[16,128,128]{2,1,0:T(8,128)}, u32[]{:S(2)}) copy-start(f32[16,128,128]{2,1,0:T(8,128)} %get-tuple-element.22) | copy-start | bytes 3145732
  155.5 19.9 %collective-permute-start.7 = (f32[3,4,128,128]{3,2,1,0:T(8,128)}, f32[3,4,128,128]{3,2,1,0:T(8,128)}, u32[]{:S(2)}, u32[]{:S(2)}) collective-permute-start(f32[3,4,128,128]{3,2,1,0:T(8,128)} %dynamic-slice_bitcast_fusion.1), channel_id=1, source_target_pairs={{0,16},{8,24},{16,0},{24,8},{1,17},{9,25},{17,1},{25,9},{2,18},{10... | collective-permute-start | bytes 2359304 | tf_op jit(solution)/shard_map/ppermute | solution.py:323
Sparse Core Ops, SparseCore 0:
  9.5 31.2 all-gather.1

commit v7 on v6

--- a/solution.py
+++ b/solution.py
@@ -29,18 +29,19 @@
     return hi, lo
 
 
-def forward_kernel(wave_ref, fs_ref, sl_ref, sr_ref, co_ref, ch_ref, mask_ref, rrow_ref, rlane_ref,
+def forward_kernel(wave_ref, fs_ref, sl_ref, sr_ref, tl_ref, tr_ref, co_ref, ch_ref, mask_ref, rrow_ref, rlane_ref,
                    h_ref, z_ref, rec_ref, pl_ref, q_ref, pb, qb, cf_ref, plocal, pickf):
     steps = h_ref.shape[0]
     az, xd, ay = mask_ref.shape
     ax = h_ref.shape[2]
-    w = sl_ref.shape[2]
+    w = ch_ref.shape[2] // 2
     pb[...] = jnp.zeros(pb.shape, jnp.float32)
     qb[...] = jnp.zeros(qb.shape, jnp.float32)
     cf_ref[...] = jnp.zeros(cf_ref.shape, jnp.float32)
     inner = pl.ds(PADX, xd)
-    for k, (buf, slot) in enumerate(((pb, 0), (qb, 0), (pb, 1), (qb, 1))):
-        place(buf.at[slot, 2:2 + az], fs_ref[k], sl_ref[k], sr_ref[k], PADX)
+    place(pb.at[0, 2:2 + az], fs_ref[0], sl_ref[...], sr_ref[...], PADX)
+    for k, (buf, slot) in enumerate(((qb, 0), (pb, 1), (qb, 1))):
+        place(buf.at[slot, 2:2 + az], fs_ref[k + 1], tl_ref[k], tr_ref[k], PADX)
     place(cf_ref, co_ref[...], ch_ref[:, :, :w], ch_ref[:, :, w:], 0)
     lane = lax.broadcasted_iota(jnp.int32, (xd, ay), 1)
     n_rec = rrow_ref.shape[0]
@@ -87,16 +88,18 @@
         rec_ref[n] = jnp.where(sel, got, 0.0)
 
 
-def adjoint_kernel(ad_ref, al_ref, ar_ref, co_ref, ch_ref, h_ref, z_ref, row_ref, m_ref, acc_ref, fin_ref, lb, mb, ob, fb, cf_ref):
+def adjoint_kernel(ad_ref, al_ref, ar_ref, bl_ref, br_ref, co_ref, ch_ref, h_ref, z_ref, row_ref, m_ref, acc_ref, fin_ref, lb, mb, ob, fb, cf_ref):
     steps = h_ref.shape[0]
     az, xd, ay = ob.shape[0] - 4, ob.shape[1], ob.shape[2]
     ax = h_ref.shape[2]
-    w = al_ref.shape[2]
+    w = ch_ref.shape[2] // 2
     lb[...] = jnp.zeros(lb.shape, jnp.float32)
     mb[...] = jnp.zeros(mb.shape, jnp.float32)
     cf_ref[...] = jnp.zeros(cf_ref.shape, jnp.float32)
-    for k, (buf, slot) in enumerate(((lb, 0), (mb, 0), (lb, 1), (mb, 1))):
+    for k, (buf, slot) in enumerate(((lb, 0), (mb, 0))):
         place(buf.at[slot], ad_ref[k], al_ref[k], ar_ref[k], 0)
+    for k, (buf, slot) in enumerate(((lb, 1), (mb, 1))):
+        place(buf.at[slot], ad_ref[k + 2], bl_ref[k], br_ref[k], 0)
     place(cf_ref, co_ref[...], ch_ref[:, :, :w], ch_ref[:, :, w:], 0)
     ob[...] = jnp.zeros(ob.shape, jnp.float32)
     fb[...] = jnp.zeros(fb.shape, jnp.float32)
@@ -150,14 +153,14 @@
         lax.fori_loop(0, az, plane, 0)
 
 
-def run_adjoint(ad, al, ar, co, ch, h_all, z_all, row, parts):
+def run_adjoint(ad, al, ar, bl, br, co, ch, h_all, z_all, row, parts):
     _, az, ax, ay = ad.shape
     xd = ax + 2 * OFF
     vm = pl.BlockSpec(memory_space=pltpu.VMEM)
     return pl.pallas_call(
         adjoint_kernel,
         out_shape=(jax.ShapeDtypeStruct((3, az, ax, ay), jnp.float32), jax.ShapeDtypeStruct((2, az, ax, ay), jnp.float32)),
-        in_specs=[vm] * 9,
+        in_specs=[vm] * 11,
         out_specs=(vm, vm),
         scratch_shapes=[
             pltpu.VMEM((2, az, xd, ay), jnp.float32),
@@ -168,7 +171,7 @@
         ],
         compiler_params=pltpu.CompilerParams(vmem_limit_bytes=62 * 1024 * 1024),
         interpret=INTERPRET,
-    )(ad, al, ar, co, ch, h_all, z_all, row, parts)
+    )(ad, al, ar, bl, br, co, ch, h_all, z_all, row, parts)
 
 
 def exact_parts(x):
@@ -178,7 +181,7 @@
     return hi.astype(jnp.bfloat16), lo.astype(jnp.bfloat16)
 
 
-def run_forward(wave, fs, sl, sr, co, ch, mask, rrow, rlane):
+def run_forward(wave, fs, sl, sr, tl, tr, co, ch, mask, rrow, rlane):
     steps = wave.shape[0]
     az, xd, ay = mask.shape
     ax = fs.shape[2]
@@ -189,14 +192,14 @@
     return pl.pallas_call(
         forward_kernel,
         out_shape=(loc, loc, jax.ShapeDtypeStruct((steps, n_rec, ay), jnp.float32), one, one),
-        in_specs=[pl.BlockSpec(memory_space=pltpu.SMEM)] + [vm] * 8,
+        in_specs=[pl.BlockSpec(memory_space=pltpu.SMEM)] + [vm] * 10,
         out_specs=(vm, vm, vm, vm, vm),
         scratch_shapes=[pltpu.VMEM((2, az + 4, xd + 2 * PADX, ay), jnp.float32)] * 2
         + [pltpu.VMEM((3, az, xd, ay), jnp.float32), pltpu.VMEM((az * ax, ay), jnp.float32),
            pltpu.VMEM((n_rec, az * ax), jnp.bfloat16)],
         compiler_params=pltpu.CompilerParams(vmem_limit_bytes=62 * 1024 * 1024),
         interpret=INTERPRET,
-    )(wave, fs, sl, sr, co, ch, mask, rrow, rlane)
+    )(wave, fs, sl, sr, tl, tr, co, ch, mask, rrow, rlane)
 
 
 def taps(padded, size, axis):
@@ -247,20 +250,23 @@
 
     fs = fwd_state[0]
     src_row = jnp.broadcast_to(src_cell[0, 0].astype(jnp.float32), (1, ay))
-    head1 = jnp.concatenate([rows(fs[:, :, :w]), rows(coefs[:, :, :w]), src_row], axis=0)
-    tail1 = jnp.concatenate([rows(fs[:, :, ax - w:]), rows(coefs[:, :, ax - w:]), src_row], axis=0)
+    v = w - 2
+    head1 = jnp.concatenate([rows(fs[0, :, :w]), rows(fs[1:, :, :v]), rows(coefs[:, :, :w]), src_row], axis=0)
+    tail1 = jnp.concatenate([rows(fs[0, :, ax - w:]), rows(fs[1:, :, ax - v:]), rows(coefs[:, :, ax - w:]), src_row], axis=0)
     left1, right1 = to_left_right(head1, tail1, "tile")
-    n_fs = 4 * az * w
+    n_p = az * w
+    n_o = 3 * az * v
     n_cf = 3 * zl * w
 
     def unpack1(m):
-        st = m[:n_fs].reshape(4, az, w, ay)
-        cf = m[n_fs:n_fs + n_cf].reshape(3, zl, w, ay)
-        sc = m[n_fs + n_cf, 0]
-        return st, cf, sc
-
-    st_l, cf_l, sc_l = unpack1(left1)
-    st_r, cf_r, sc_r = unpack1(right1)
+        sp = m[:n_p].reshape(az, w, ay)
+        so = m[n_p:n_p + n_o].reshape(3, az, v, ay)
+        cf = m[n_p + n_o:n_p + n_o + n_cf].reshape(3, zl, w, ay)
+        sc = m[n_p + n_o + n_cf, 0]
+        return sp, so, cf, sc
+
+    sp_l, so_l, cf_l, sc_l = unpack1(left1)
+    sp_r, so_r, cf_r, sc_r = unpack1(right1)
     cf_halo = lax.all_gather(jnp.concatenate([cf_l, cf_r], axis=2), "shot", axis=1, tiled=True)
 
     def ext_index(cell, shift):
@@ -280,12 +286,21 @@
     source_mask = jnp.zeros((cells_ext,), jnp.float32).at[src_idx].add(src_on, mode="drop").reshape(ext_shape)
 
     ad = adj_state[0]
-    ad_head, ad_tail, st_l, st_r = lax.optimization_barrier((rows(ad[:, :, :w]), rows(ad[:, :, ax - w:]), st_l, st_r))
+    ad_head = jnp.concatenate([rows(ad[:2, :, :w]), rows(ad[2:, :, :v])], axis=0)
+    ad_tail = jnp.concatenate([rows(ad[:2, :, ax - w:]), rows(ad[2:, :, ax - v:])], axis=0)
+    ad_head, ad_tail, sp_l, sp_r = lax.optimization_barrier((ad_head, ad_tail, sp_l, sp_r))
     left2, right2 = to_left_right(ad_head, ad_tail, "tile")
+    n_a = 2 * az * w
+
+    def unpack2(m):
+        return m[:n_a].reshape(2, az, w, ay), m[n_a:].reshape(2, az, v, ay)
+
+    al, bl = unpack2(left2)
+    ar, br = unpack2(right2)
 
     receivers = rec_cells[0]
     h_all, z_all, rec_mat, p_last, q_last = run_forward(
-        src_wave[0], fs, st_l, st_r, full, cf_halo, source_mask, (receivers // ay)[:, None], (receivers % ay)[:, None])
+        src_wave[0], fs, sp_l, sp_r, so_l, so_r, full, cf_halo, source_mask, (receivers // ay)[:, None], (receivers % ay)[:, None])
     records = jnp.sum(rec_mat, axis=2) - observed[0]
 
     msg = jnp.concatenate([records, receivers.astype(jnp.float32)[None]], axis=0)
@@ -305,7 +320,7 @@
         vals = jnp.concatenate([records[step], left3[step], right3[step]])
         parts.append(jnp.stack(exact_parts(jnp.where(pick_lane, vals[:, None], 0.0))))
     rec_rows = (rec_all // ay)[None, :]
-    acc, fin = run_adjoint(ad, left2.reshape(4, az, w, ay), right2.reshape(4, az, w, ay), full, cf_halo, h_all, z_all, rec_rows, jnp.stack(parts))
+    acc, fin = run_adjoint(ad, al, ar, bl, br, full, cf_halo, h_all, z_all, rec_rows, jnp.stack(parts))
 
     n_shot = lax.axis_size("shot")
     n_y = n_shot // 2

time: 185 us -> 182 us (0.984)
  waiting for transfers between devices: 43.1 us -> 37 us
  other arithmetic: 12.5 us -> 14.5 us
    ppermute x3, waiting for transfers between devices: 18.8 us -> 12.6 us  [to_left_right(): from_left = lax.ppermute(tail, axis, [(i, i + 1) for i in range(count - 1)])]
    reshape x6 -> x10, local copies, waits for them, and re-layouts: 3.37 us -> 5.81 us  [the longest x4 2.93 us: unpack2(): return (m[:n_a].reshape(2, az, w, ay), m[n_a:].reshape(2, az, v, ay))]
    slice x8 -> x16, local copies, waits for them, and re-layouts: 6.31 us -> 5.65 us  [the longest x1 1.26 us: per_device(): fs[1:, :, :v]]
  transfers between devices with their start and end apart: 9 -> 9, of which waited for: 5 -> 5; matrix products, arithmetic and copies ran while one was open for 9% -> 11% of each run, Pallas kernels for 0% -> 0%
where the time goes in v7:
time: 182 us
  Pallas kernels  70.8 us (39%)
  waiting for transfers between devices  37 us (20%)
  starting transfers between devices  19.1 us (10%)
  between operations  16.8 us (9%)
  local copies, waits for them, and re-layouts  15.3 us (8%)
  other arithmetic  14.5 us (8%)
  blocking collectives  8.01 us (4%)
    pallas_call x1, Pallas kernels, run_adjoint(): pl.pallas_call(adjoint_kernel, out_shape=(jax.ShapeDtypeStruct((3, az, ax...  39.9 us
    pallas_call x1, Pallas kernels, run_forward(): pl.pallas_call(forward_kernel, out_shape=(loc, loc, jax.ShapeDtypeStruct(...  30.9 us
    ppermute x1, waiting for transfers between devices, per_device(): partial = lax.ppermute(partial, 'shot', ring)  15.7 us
    ppermute x3, starting transfers between devices, to_left_right(): from_left = lax.ppermute(tail, axis, [(i, i + 1) for i in range(count - 1)])  13.6 us
    ppermute x3, waiting for transfers between devices, to_left_right(): from_left = lax.ppermute(tail, axis, [(i, i + 1) for i in range(count - 1)])  12.6 us
    all_gather x1, blocking collectives, per_device(): lax.all_gather(jnp.concatenate([cf_l, cf_r], axis=2), 'shot', axis=1, til...  8.01 us
    ppermute x3, waiting for transfers between devices, to_left_right(): lax.ppermute(head, axis, [(i + 1, i) for i in range(count - 1)])  4.57 us
    ppermute x3, starting transfers between devices, to_left_right(): lax.ppermute(head, axis, [(i + 1, i) for i in range(count - 1)])  3.88 us
  transfers between devices with their start and end apart: 9, of which 5 were waited for; matrix products, arithmetic and copies ran while one was open for 11% of the time, Pallas kernels for 0%

profile of v7, /device:TPU:0, one launch (start us, length us, event | category | flops | bytes accessed | tf_op | source)
XLA Modules:
  0.0 181.5 jit_solution(12100543294805399877)
XLA Ops:
  7.2 0.7 all-gather.2.cloned.1.call-update
  8.6 1.3 fusion.47
  9.9 1.0 fusion.46
  11.1 0.2 maximum_maximum_fusion.1
  11.2 4.9 %collective-permute-start = (f32[817,128]{1,0:T(8,128)S(1)}, f32[817,128]{1,0:T(8,128)S(1)}, u32[]{:S(2)}, u32[]{:S(2)}) collective-permute-start(f32[817,128]{1,0:T(8,128)S(1)} %get-tuple-element.71), channel_id=1, source_target_pairs={{0,1},{1,2},{2,3},{3,4},{4,5},{5,6},{6,7},{8,9},{9,10},{10,11},{11... | collective-permute-start | bytes 1254920 | tf_op jit(solution)/shard_map/ppermute | solution.py:225
  16.2 1.3 collective-permute-start.1
  17.5 1.1 fusion.48
  18.7 1.1 fusion.49
  19.9 0.8 copy.14
  20.7 0.9 pad_maximum_fusion.1
  21.7 0.6 and_select_fusion.28
  22.3 0.6 and_select_fusion.13
  22.9 0.7 add_select_fusion
  23.6 10.6 %collective-permute-done = f32[817,128]{1,0:T(8,128)S(1)} collective-permute-done((f32[817,128]{1,0:T(8,128)S(1)}, f32[817,128]{1,0:T(8,128)S(1)}, u32[]{:S(2)}, u32[]{:S(2)}) %collective-permute-start) | collective-permute-done | bytes 418336 | tf_op jit(solution)/shard_map/ppermute | solution.py:225
  34.1 0.5 slice.210
  35.4 0.5 slice.211
  36.7 0.7 reshape.1077.sl_ref
  37.3 0.7 reshape.1080.sr_ref
  38.0 4.4 %collective-permute-start.2 = (f32[704,128]{1,0:T(8,128)}, f32[704,128]{1,0:T(8,128)S(1)}, u32[]{:S(2)}, u32[]{:S(2)}) collective-permute-start(f32[704,128]{1,0:T(8,128)} %get-tuple-element.14), channel_id=1, source_target_pairs={{0,1},{1,2},{2,3},{3,4},{4,5},{5,6},{6,7},{8,9},{9,10},{10,11},{11... | collective-permute-start | bytes 1081352 | tf_op jit(solution)/shard_map/ppermute | solution.py:225
  42.4 1.3 collective-permute-start.3
  43.9 0.8 reshape.1087.tl_ref
  44.7 0.8 reshape.1088.tr_ref
  45.5 1.7 scatter_custom_fusion
  47.2 8.0 %all_gather.7.ch_ref = f32[3,16,24,128]{3,2,1,0:T(8,128)} all-gather(f32[3,4,24,128]{3,2,1,0:T(8,128)S(1)} %pad_maximum_fusion.3), channel_id=1, replica_groups=mesh['shot'=4,'tile'=8] {'shot'}, dimensions={1}, use_global_device_ids=true | all-gather | bytes 737280 | tf_op jit(solution)/shard_map/all_gather | solution.py:270
  55.2 2.1 %collective-permute-done.2 = f32[704,128]{1,0:T(8,128)S(1)} collective-permute-done((f32[704,128]{1,0:T(8,128)}, f32[704,128]{1,0:T(8,128)S(1)}, u32[]{:S(2)}, u32[]{:S(2)}) %collective-permute-start.2) | collective-permute-done | bytes 360480 | tf_op jit(solution)/shard_map/ppermute | solution.py:225
  57.3 0.7 reshape.1081.al_ref
  58.1 0.7 reshape.1082.ar_ref
  58.8 0.7 reshape.1083.bl_ref
  59.6 0.7 reshape.1084.br_ref
  60.3 30.9 %shard_map.94 = (f32[6,16,128,128]{3,2,1,0:T(8,128)}, f32[6,16,128,128]{3,2,1,0:T(8,128)}, f32[6,128,128]{2,1,0:T(8,128)}, f32[16,128,128]{2,1,0:T(8,128)}, f32[16,128,128]{2,1,0:T(8,128)}) custom-call(f32[6]{0:T(128)} %bitcast.161, f32[4,16,128,128]{3,2,1,0:T(8,128)} %bitcast.154, f32[16,12,128]{2,1,0:T(8,128)} %reshape.1077.sl_ref, ...), custom_call_target="tpu_custom_call" | custom-call | tf_op jit(solution)/shard_map/pallas_call | solution.py:192
  91.3 1.2 reduce_sum.9
  92.5 4.3 %collective-permute-start.4 = (f32[7,128]{1,0:T(8,128)S(1)}, f32[7,128]{1,0:T(8,128)S(1)}, u32[]{:S(2)}, u32[]{:S(2)}) collective-permute-start(f32[7,128]{1,0:T(8,128)S(1)} %pad_maximum_fusion.4), channel_id=1, source_target_pairs={{0,1},{1,2},{2,3},{3,4},{4,5},{5,6},{6,7},{8,9},{9,10},{10,11},{11... | collective-permute-start | bytes 10760 | tf_op jit(solution)/shard_map/ppermute | solution.py:225
  96.8 1.3 collective-permute-start.5
  98.1 4.6 %collective-permute-done.5 = f32[7,128]{1,0:T(8,128)S(1)} collective-permute-done((f32[7,128]{1,0:T(8,128)S(1)}, f32[7,128]{1,0:T(8,128)S(1)}, u32[]{:S(2)}, u32[]{:S(2)}) %collective-permute-start.5) | collective-permute-done | bytes 3616 | tf_op jit(solution)/shard_map/ppermute | solution.py:226
  102.9 0.4 reduce-precision_convert_fusion
  103.6 0.7 and_select_fusion.row_ref
  104.3 0.3 copy-done.1
  104.5 39.9 %shard_map.95 = (f32[3,16,128,128]{3,2,1,0:T(8,128)}, f32[2,16,128,128]{3,2,1,0:T(8,128)}) custom-call(f32[4,16,128,128]{3,2,1,0:T(8,128)} %bitcast.151, f32[2,16,12,128]{3,2,1,0:T(8,128)} %reshape.1081.al_ref, f32[2,16,12,128]{3,2,1,0:T(8,128)} %reshape.1082.ar_ref, f32[2,16,10,128]{3,2,1,0:T(8,128)} %reshape.1083.bl_ref, ...), custom_call_target="tpu_custom_call" | custom-call | tf_op jit(solution)/shard_map/pallas_call | solution.py:160
  144.4 1.5 dynamic-slice_bitcast_fusion
  146.0 3.5 %collective-permute-done.6 = f32[3,2,4,128,128]{4,3,2,1,0:T(8,128)} collective-permute-done((f32[3,2,4,128,128]{4,3,2,1,0:T(8,128)S(1)}, f32[3,2,4,128,128]{4,3,2,1,0:T(8,128)}, u32[]{:S(2)}, u32[]{:S(2)}) %collective-permute-start.6) | collective-permute-done | bytes 1572896 | tf_op jit(solution)/shard_map/ppermute | solution.py:333
  149.5 2.1 %bitcast_add_fusion = f32[3,2,4,128,128]{4,3,2,1,0:T(8,128)S(1)} fusion(f32[3,2,4,128,128]{4,3,2,1,0:T(8,128)} %collective-permute-done.6, f32[3,2,2,4,128,128]{5,4,3,2,1,0:T(8,128)} %bitcast.157, s32[]{:T(128)S(6)} %select_n.465), kind=kLoop, calls=%fused_computation.2 | loop fusion | flops 393216 | bytes 4718596 | tf_op jit(solution)/shard_map/add | solution.py:334
  151.6 0.9 dynamic-slice_bitcast_fusion.1
  152.5 1.5 collective-permute-start.7
  154.1 2.7 %maximum_bitcast_fusion = f32[1,2,16,128,128]{4,3,2,1,0:T(8,128)} fusion(f32[1,16,128,128]{3,2,1,0:T(8,128)} %bitcast.159, f32[1,16,128,128]{3,2,1,0:T(8,128)S(1)} %bitcast.158), kind=kLoop, calls=%fused_computation.1 | loop fusion | flops 524288 | bytes 4194304 | tf_op jit(solution)/shard_map/broadcast_in_dim | solution.py:344
  156.8 15.7 %collective-permute-done.7 = f32[3,4,128,128]{3,2,1,0:T(8,128)} collective-permute-done((f32[3,4,128,128]{3,2,1,0:T(8,128)}, f32[3,4,128,128]{3,2,1,0:T(8,128)}, u32[]{:S(2)}, u32[]{:S(2)}) %collective-permute-start.7) | collective-permute-done | bytes 786464 | tf_op jit(solution)/shard_map/ppermute | solution.py:338
  172.4 1.2 bitcast_add_fusion.1
  173.7 0.1 slice_add_fusion
  173.8 0.9 pad_maximum_fusion
  (70 shorter events, 1.1 us)
Async XLA Ops:
  7.2 53.2 %all-gather.2.cloned.1.call-start = ((), (), s32[]{:S(2)}) async-start(), calls=%async_computation | async-start | bytes 3932160 | tf_op jit(solution)/shard_map/all_gather | solution.py:240
  8.5 2.4 %copy-start = (f32[3,4,128,128]{3,2,1,0:T(8,128)S(1)}, f32[3,4,128,128]{3,2,1,0:T(8,128)}, u32[]{:S(2)}) copy-start(f32[3,4,128,128]{3,2,1,0:T(8,128)} %param.7) | copy-start | bytes 2359300
  11.2 22.9 %collective-permute-start = (f32[817,128]{1,0:T(8,128)S(1)}, f32[817,128]{1,0:T(8,128)S(1)}, u32[]{:S(2)}, u32[]{:S(2)}) collective-permute-start(f32[817,128]{1,0:T(8,128)S(1)} %get-tuple-element.71), channel_id=1, source_target_pairs={{0,1},{1,2},{2,3},{3,4},{4,5},{5,6},{6,7},{8,9},{9,10},{10,11},{11... | collective-permute-start | bytes 1254920 | tf_op jit(solution)/shard_map/ppermute | solution.py:225
  16.2 19.2 %collective-permute-start.1 = (f32[817,128]{1,0:T(8,128)S(1)}, f32[817,128]{1,0:T(8,128)S(1)}, u32[]{:S(2)}, u32[]{:S(2)}) collective-permute-start(f32[817,128]{1,0:T(8,128)S(1)} %get-tuple-element.70), channel_id=1, source_target_pairs={{1,0},{2,1},{3,2},{4,3},{5,4},{6,5},{7,6},{9,8},{10,9},{11,10},{12... | collective-permute-start | bytes 1254920 | tf_op jit(solution)/shard_map/ppermute | solution.py:226
  19.9 1.8 copy-start.4
  38.0 19.3 %collective-permute-start.2 = (f32[704,128]{1,0:T(8,128)}, f32[704,128]{1,0:T(8,128)S(1)}, u32[]{:S(2)}, u32[]{:S(2)}) collective-permute-start(f32[704,128]{1,0:T(8,128)} %get-tuple-element.14), channel_id=1, source_target_pairs={{0,1},{1,2},{2,3},{3,4},{4,5},{5,6},{6,7},{8,9},{9,10},{10,11},{11... | collective-permute-start | bytes 1081352 | tf_op jit(solution)/shard_map/ppermute | solution.py:225
  42.4 15.7 %collective-permute-start.3 = (f32[704,128]{1,0:T(8,128)}, f32[704,128]{1,0:T(8,128)S(1)}, u32[]{:S(2)}, u32[]{:S(2)}) collective-permute-start(f32[704,128]{1,0:T(8,128)} %get-tuple-element.15), channel_id=1, source_target_pairs={{1,0},{2,1},{3,2},{4,3},{5,4},{6,5},{7,6},{9,8},{10,9},{11,10},{12... | collective-permute-start | bytes 1081352 | tf_op jit(solution)/shard_map/ppermute | solution.py:226
  60.3 32.1 %copy-start.3 = (f32[1,6,128]{2,0,1:T(1,128)S(1)}, f32[1,6,128]{2,0,1:T(1,128)}, u32[]{:S(2)}) copy-start(f32[1,6,128]{2,0,1:T(1,128)} %param.13) | copy-start | bytes 9220
  60.3 32.1 %copy-start.6 = (f32[1,128]{1,0:T(1,128)S(1)}, f32[1,128]{1,0:T(1,128)}, u32[]{:S(2)}) copy-start(f32[1,128]{1,0:T(1,128)} %get-tuple-element.83) | copy-start | bytes 1540
  60.3 42.5 %copy-start.5 = (s32[128]{0:T(128)S(1)}, s32[128]{0:T(128)}, u32[]{:S(2)}) copy-start(s32[128]{0:T(128)} %and_select_fusion.13) | copy-start | bytes 1540
  92.5 5.6 %collective-permute-start.4 = (f32[7,128]{1,0:T(8,128)S(1)}, f32[7,128]{1,0:T(8,128)S(1)}, u32[]{:S(2)}, u32[]{:S(2)}) collective-permute-start(f32[7,128]{1,0:T(8,128)S(1)} %pad_maximum_fusion.4), channel_id=1, source_target_pairs={{0,1},{1,2},{2,3},{3,4},{4,5},{5,6},{6,7},{8,9},{9,10},{10,11},{11... | collective-permute-start | bytes 10760 | tf_op jit(solution)/shard_map/ppermute | solution.py:225
  96.8 5.9 %collective-permute-start.5 = (f32[7,128]{1,0:T(8,128)S(1)}, f32[7,128]{1,0:T(8,128)S(1)}, u32[]{:S(2)}, u32[]{:S(2)}) collective-permute-start(f32[7,128]{1,0:T(8,128)S(1)} %pad_maximum_fusion.4), channel_id=1, source_target_pairs={{1,0},{2,1},{3,2},{4,3},{5,4},{6,5},{7,6},{9,8},{10,9},{11,10},{12... | collective-permute-start | bytes 10760 | tf_op jit(solution)/shard_map/ppermute | solution.py:226
  102.9 0.7 copy-start.7
  103.5 1.0 copy-start.1
  145.9 3.6 %collective-permute-start.6 = (f32[3,2,4,128,128]{4,3,2,1,0:T(8,128)S(1)}, f32[3,2,4,128,128]{4,3,2,1,0:T(8,128)}, u32[]{:S(2)}, u32[]{:S(2)}) collective-permute-start(f32[3,2,4,128,128]{4,3,2,1,0:T(8,128)S(1)} %dynamic-slice_bitcast_fusion), channel_id=1, source_target_pairs={{0,8},{8,0},{16,24},{24,16},{1,9},{9,1},{17,25},{25,17},{2,10},{10... | collective-permute-start | bytes 4718600 | tf_op jit(solution)/shard_map/ppermute | solution.py:333
  151.6 2.5 %copy-start.2 = (f32[16,128,128]{2,1,0:T(8,128)S(1)}, f32[16,128,128]{2,1,0:T(8,128)}, u32[]{:S(2)}) copy-start(f32[16,128,128]{2,1,0:T(8,128)} %get-tuple-element.22) | copy-start | bytes 3145732
  152.5 19.9 %collective-permute-start.7 = (f32[3,4,128,128]{3,2,1,0:T(8,128)}, f32[3,4,128,128]{3,2,1,0:T(8,128)}, u32[]{:S(2)}, u32[]{:S(2)}) collective-permute-start(f32[3,4,128,128]{3,2,1,0:T(8,128)} %dynamic-slice_bitcast_fusion.1), channel_id=1, source_target_pairs={{0,16},{8,24},{16,0},{24,8},{1,17},{9,25},{17,1},{25,9},{2,18},{10... | collective-permute-start | bytes 2359304 | tf_op jit(solution)/shard_map/ppermute | solution.py:338
Sparse Core Ops, SparseCore 0:
  9.5 31.2 all-gather.1
